TPU v7x, 32 devices: a whole 2x2x4 slice. The times are simulated.
32 devices in a mesh: tm: 4 (over y, x), chan: 8 (over z, core).
Axes of the slice: x: 2, y: 2, z: 4, core: 2. Of those that a mesh axis runs over, the one named last changes fastest.
Arguments:
- strain: bfloat16 [256, 16384], P('chan', 'tm'), may hold values from -6 to 6
- fir_taps: bfloat16 [256, 256], P('chan'), may hold values from -0.375 to 0.375
Outputs:
- stacked: float32 [2, 256, 256, 256], P(None, 'tm', 'chan')
All inputs are finite; a program needn't handle non-finite values.
Results may differ from a plain program's by a relative error of at most 0.0062.
Values may be sent and summed in bfloat16 or wider, within the bound.
No kernel may reach another device: no remote copies, remote signals or barrier semaphores. Data moves between devices by JAX's collectives and lax.ppermute only.
A program may use at most 128 MiB of HBM per device.

v0:
```python
import math

import jax
import jax.numpy as jnp
from jax import lax
from jax.sharding import PartitionSpec as P

SEG = 512


def shifted(value, axis, by):
    size = lax.axis_size(axis)
    pairs = [(i, i + by) for i in range(size) if 0 <= i + by < size]
    return lax.ppermute(value, axis, pairs)


def make_table():
    sample_idx = jnp.arange(SEG, dtype=jnp.int32)
    bin_idx = jnp.arange(SEG // 2, dtype=jnp.int32)
    phases = sample_idx[:, None] * bin_idx[None, :] % SEG
    angles = phases.astype(jnp.float32) * (2.0 * math.pi / SEG)
    window = 0.5 - 0.5 * jnp.cos(sample_idx.astype(jnp.float32) * (2.0 * math.pi / SEG))
    cosine = window[:, None] * jnp.cos(angles)
    sine_part = -window[:, None] * jnp.sin(angles)
    return jnp.stack([cosine, sine_part], axis=1).astype(jnp.bfloat16)


def toeplitz(fir_taps):
    tap_count = fir_taps.shape[1]
    row_idx = jnp.arange(2 * tap_count, dtype=jnp.int32)[:, None]
    col_idx = jnp.arange(tap_count, dtype=jnp.int32)[None, :]
    lag_idx = col_idx + tap_count - row_idx
    valid = (lag_idx >= 0) & (lag_idx < tap_count)
    picked = jnp.take(fir_taps, jnp.clip(lag_idx, 0, tap_count - 1), axis=1)
    return jnp.where(valid[None, :, :], picked, jnp.zeros_like(picked))


def cross_block(own_bins, other_bins):
    swapped = jnp.stack([-other_bins[:, 1], other_bins[:, 0]], axis=1)
    real_part = jnp.einsum(
        "kpsi,kpsj->kij", own_bins, other_bins, preferred_element_type=jnp.float32
    )
    imag_part = jnp.einsum("kpsi,kpsj->kij", own_bins, swapped, preferred_element_type=jnp.float32)
    return jnp.stack([real_part, imag_part], axis=0)


def shards(strain, fir_taps):
    tap_count = fir_taps.shape[1]
    channels = strain.shape[0]
    previous = shifted(strain[:, -tap_count:], "tm", 1)
    extended = jnp.concatenate([previous, strain], axis=1)
    blocks = extended.reshape(channels, -1, tap_count)
    block_pairs = jnp.concatenate([blocks[:, :-1], blocks[:, 1:]], axis=2)
    filtered = jnp.einsum(
        "cbr,cri->cbi", block_pairs, toeplitz(fir_taps), preferred_element_type=jnp.float32
    )
    whitened = filtered.reshape(channels, -1).astype(jnp.bfloat16)
    segments = whitened.reshape(channels, whitened.shape[1] // SEG, SEG)
    spectra = jnp.einsum(
        "csn,npk->kpsc", segments, make_table(), preferred_element_type=jnp.float32
    ).astype(jnp.bfloat16)
    gathered = lax.all_gather(spectra, "chan", axis=3, tiled=True)
    all_bins = lax.all_to_all(gathered, "tm", split_axis=0, concat_axis=2, tiled=True)
    factor = 1.0 / (all_bins.shape[2] * SEG)
    first_col = lax.axis_index("chan") * channels
    own_bins = lax.dynamic_slice_in_dim(all_bins, first_col, channels, 3)
    result = cross_block(own_bins, all_bins) * factor
    return result


def solution(mesh):
    placed = (P("chan", "tm"), P("chan", None))
    return jax.shard_map(
        shards, mesh=mesh, in_specs=placed, out_specs=P(None, "tm", "chan", None), check_vma=False
    )
```

profile of v0, /device:TPU:0, one launch (start us, length us, event | category | flops | bytes accessed | tf_op | source)
XLA Modules:
  0.0 581.4 jit_solution(17817019750190096485)
XLA Ops:
  6.5 0.7 slice.15
  7.3 4.8 collective-permute-start
  12.2 0.1 fusion.24
  12.4 0.3 copy.28
  12.7 0.1 broadcast_clamp_fusion
  12.7 2.3 multiply_convert_fusion
  15.0 0.4 fusion.37
  15.4 0.1 copy.16
  15.5 454.0 %gather_fusion = bf16[131072,32]{1,0:T(8,128)(2,1)} fusion(bf16[32,256]{0,1:T(8,128)(2,1)S(1)} %copy.16, s32[131072]{0:T(1024)S(1)} %broadcast_clamp_fusion), kind=kCustom, calls=%fused_computation | custom fusion | bytes 17301504 | tf_op jit(solution)/shard_map/jit(_take)/gather | solution.py:34
  469.5 30.7 %copy.17 = bf16[512,256,32]{1,0,2:T(8,128)(2,1)} copy(bf16[512,256,32]{2,1,0:T(8,128)(2,1)} %bitcast.35) | data formatting | bytes 16777216 | tf_op jit(solution)/shard_map/jit(_take)/gather | solution.py:34
  500.3 0.1 reshape.212
  500.4 0.1 fusion.49
  500.6 4.7 fusion.15
  505.3 0.1 convert_element_type.45
  505.4 1.0 fusion.18
  506.4 29.6 %all-gather.2.cloned.1.call-done = bf16[256,2,8,256]{0,3,2,1:T(8,128)(2,1)} async-done(((bf16[256,2,8,32]{0,3,2,1:T(8,128)(2,1)}), bf16[256,2,8,256]{0,3,2,1:T(8,128)(2,1)}) %all-gather.2.cloned.1.call-update) | async-done | bytes 2097168 | tf_op jit(solution)/shard_map/all_gather | solution.py:62
  536.0 4.5 copy.19
  540.5 3.6 all-to-all-start
  544.1 25.5 %all-to-all-done = bf16[256,2,8,256]{3,2,1,0:T(8,128)(2,1)S(1)} async-done(((bf16[256,2,8,256]{3,2,1,0:T(8,128)(2,1)}), bf16[256,2,8,256]{3,2,1,0:T(8,128)(2,1)S(1)}, u32[]{:S(2)}, u32[]{:S(2)}) %all-to-all-start) | async-done | bytes 2097184 | tf_op jit(solution)/shard_map/all_to_all | solution.py:63
  569.6 0.3 copy.34
  569.9 0.1 slice_negate_fusion
  570.0 1.0 convolution_bitcast_fusion
  571.1 1.0 fusion.12
  572.1 2.5 maximum_multiply_fusion
  (11 shorter events, 0.1 us)
Async XLA Ops:
  6.5 8.9 %copy-start.1 = (bf16[32,256]{1,0:T(8,128)(2,1)S(1)}, bf16[32,256]{1,0:T(8,128)(2,1)}, u32[]{:S(2)}) copy-start(bf16[32,256]{1,0:T(8,128)(2,1)} %param.3) | copy-start | bytes 49156
  6.5 529.5 %all-gather.2.cloned.1.call-start = ((), (), s32[]{:S(2)}) async-start(), calls=%async_computation.1 | async-start | bytes 2359296 | tf_op jit(solution)/shard_map/all_gather | solution.py:62
  7.3 493.0 %collective-permute-start = (bf16[32,256]{1,0:T(8,128)(2,1)S(1)}, bf16[32,256]{1,0:T(8,128)(2,1)S(1)}, u32[]{:S(2)}, u32[]{:S(2)}) collective-permute-start(bf16[32,256]{1,0:T(8,128)(2,1)S(1)} %slice.15), channel_id=1, source_target_pairs={{0,8},{8,16},{16,24},{1,9},{9,17},{17,25},{2,10},{10,18},{18,26},{... | collective-permute-start | bytes 49160 | tf_op jit(solution)/shard_map/ppermute | solution.py:14
  469.5 30.7 %copy-start = (bf16[32,4096]{1,0:T(8,128)(2,1)S(1)}, bf16[32,4096]{1,0:T(8,128)(2,1)}, u32[]{:S(2)}) copy-start(bf16[32,4096]{1,0:T(8,128)(2,1)} %param.2) | copy-start | bytes 786436
  540.5 29.1 %all-to-all-start = ((bf16[256,2,8,256]{3,2,1,0:T(8,128)(2,1)}), bf16[256,2,8,256]{3,2,1,0:T(8,128)(2,1)S(1)}, u32[]{:S(2)}, u32[]{:S(2)}) async-start(bf16[256,2,8,256]{3,2,1,0:T(8,128)(2,1)} %copy.19), calls=%async_computation | async-start | bytes 4194304 | tf_op jit(solution)/shard_map/all_to_all | solution.py:63
Sparse Core Ops, SparseCore 0:
  506.5 29.4 all-gather.1
where the time goes:
time: 583 us; the launch traced here: 581 us
  local copies, waits for them, and re-layouts  491 us (84%)
  waiting for transfers between devices  55.1 us (9%)
  between operations  13.5 us (2%)
  starting transfers between devices  8.48 us (1%)
  matrix products  7.77 us (1%)
    gather x2, local copies, waits for them, and re-layouts, toeplitz(): picked = jnp.take(fir_taps, jnp.clip(lag_idx, 0, tap_count - 1), axis=1)  485 us
    all_gather x1, waiting for transfers between devices, shards(): gathered = lax.all_gather(spectra, 'chan', axis=3, tiled=True)  29.6 us
    all_to_all x1, waiting for transfers between devices, shards(): lax.all_to_all(gathered, 'tm', split_axis=0, concat_axis=2, tiled=True)  25.5 us
  transfers between devices with their start and end apart: 3, of which 2 were waited for; matrix products, arithmetic and copies ran while one was open for 84% of the time, Pallas kernels for 0%

commit v1 on v0

--- a/solution.py
+++ b/solution.py
@@ -48,12 +48,16 @@
     tap_count = fir_taps.shape[1]
     channels = strain.shape[0]
     previous = shifted(strain[:, -tap_count:], "tm", 1)
-    extended = jnp.concatenate([previous, strain], axis=1)
-    blocks = extended.reshape(channels, -1, tap_count)
-    block_pairs = jnp.concatenate([blocks[:, :-1], blocks[:, 1:]], axis=2)
-    filtered = jnp.einsum(
-        "cbr,cri->cbi", block_pairs, toeplitz(fir_taps), preferred_element_type=jnp.float32
-    )
+    extended = jnp.concatenate([previous, strain], axis=1)[:, 1:]
+    filtered = lax.conv_general_dilated(
+        extended[None],
+        jnp.flip(fir_taps, axis=1)[:, None, :],
+        window_strides=(1,),
+        padding="VALID",
+        dimension_numbers=("NCH", "OIH", "NCH"),
+        feature_group_count=channels,
+        preferred_element_type=jnp.float32,
+    )[0]
     whitened = filtered.reshape(channels, -1).astype(jnp.bfloat16)
     segments = whitened.reshape(channels, whitened.shape[1] // SEG, SEG)
     spectra = jnp.einsum(

time: 583 us -> 157 us (0.27)
  local copies, waits for them, and re-layouts: 491 us -> 9.31 us
  matrix products: 7.77 us -> 64.1 us
    gather x2 -> x0, local copies, waits for them, and re-layouts: 485 us -> none  [toeplitz(): picked = jnp.take(fir_taps, jnp.clip(lag_idx, 0, tap_count - 1), axis=1)]
    conv_general_dilated x0 -> x1, matrix products: none -> 61 us  [shards(): lax.conv_general_dilated(extended[None], jnp.flip(fir_taps, axis=1)[:, No...]
  transfers between devices with their start and end apart: 3 -> 3, of which waited for: 2 -> 2; matrix products, arithmetic and copies ran while one was open for 84% -> 2% of each run, Pallas kernels for 0% -> 0%
where the time goes in v1:
time: 157 us
  matrix products  64.1 us (41%)
  waiting for transfers between devices  55.1 us (35%)
  between operations  13.6 us (9%)
  local copies, waits for them, and re-layouts  9.31 us (6%)
  starting transfers between devices  8.48 us (5%)
  other arithmetic  6.53 us (4%)
    conv_general_dilated x1, matrix products, shards(): lax.conv_general_dilated(extended[None], jnp.flip(fir_taps, axis=1)[:, No...  61 us
    all_gather x1, waiting for transfers between devices, shards(): gathered = lax.all_gather(spectra, 'chan', axis=3, tiled=True)  29.6 us
    all_to_all x1, waiting for transfers between devices, shards(): lax.all_to_all(gathered, 'tm', split_axis=0, concat_axis=2, tiled=True)  25.5 us
    ppermute x1, starting transfers between devices, shifted(): return lax.ppermute(value, axis, pairs)  4.83 us
    all_gather x1, local copies, waits for them, and re-layouts, shards(): gathered = lax.all_gather(spectra, 'chan', axis=3, tiled=True)  4.49 us
    all_to_all x1, starting transfers between devices, shards(): lax.all_to_all(gathered, 'tm', split_axis=0, concat_axis=2, tiled=True)  3.65 us
  transfers between devices with their start and end apart: 3, of which 2 were waited for; matrix products, arithmetic and copies ran while one was open for 2% of the time, Pallas kernels for 0%

profile of v1, /device:TPU:0, one launch (start us, length us, event | category | flops | bytes accessed | tf_op | source)
XLA Modules:
  0.0 157.0 jit_solution(7761917013179768277)
XLA Ops:
  6.5 0.7 slice.12
  7.3 4.8 %collective-permute-start = (bf16[32,256]{1,0:T(8,128)(2,1)S(1)}, bf16[32,256]{1,0:T(8,128)(2,1)S(1)}, u32[]{:S(2)}, u32[]{:S(2)}) collective-permute-start(bf16[32,256]{1,0:T(8,128)(2,1)S(1)} %slice.12), channel_id=1, source_target_pairs={{0,8},{8,16},{16,24},{1,9},{9,17},{17,25},{2,10},{10,18},{18,26},{... | collective-permute-start | bytes 49160 | tf_op jit(solution)/shard_map/ppermute | solution.py:14
  12.2 2.3 %multiply_convert_fusion = (bf16[512,1,256]{2,0,1:T(8,128)(2,1)S(1)}, bf16[512,1,256]{2,0,1:T(8,128)(2,1)S(1)}) fusion(f32[512]{0:T(512)S(1)} %fusion.30, f32[512]{0:T(512)S(1)} %multiply_subtract_fusion), kind=kLoop, calls=%fused_computation.32 | loop fusion | flops 2359296 | bytes 528384 | tf_op jit(solution)/shard_map/convert.1
  14.5 0.9 rev.4
  15.4 0.1 copy.37
  15.5 1.1 fusion.27
  16.6 0.6 reshape.125
  17.2 0.9 copy.36
  18.1 0.1 slice.18
  18.2 0.4 fusion.43
  18.6 61.0 %fusion.7 = bf16[8,544,32]{2,0,1:T(8,128)(2,1)S(1)} fusion(bf16[32,1,256]{0,1,2:T(2,128)(2,1)S(1)} %copy.37, bf16[32,8,799]{0,1,2:T(8,128)(2,1)S(1)} %fusion.43), kind=kOutput, calls=%fused_computation.10 | convolution fusion | flops 71303168 | bytes 704000 | tf_op jit(solution)/shard_map/conv_general_dilated | solution.py:52
  79.6 0.8 copy.38
  80.5 0.1 copy.39
  80.6 0.3 reshape.129
  81.0 1.0 fusion.15
  82.0 29.6 %all-gather.2.cloned.1.call-done = bf16[256,2,8,256]{0,3,2,1:T(8,128)(2,1)} async-done(((bf16[256,2,8,32]{0,3,2,1:T(8,128)(2,1)}), bf16[256,2,8,256]{0,3,2,1:T(8,128)(2,1)}) %all-gather.2.cloned.1.call-update) | async-done | bytes 2097168 | tf_op jit(solution)/shard_map/all_gather | solution.py:66
  111.6 4.5 %copy.41 = bf16[256,2,8,256]{3,2,1,0:T(8,128)(2,1)} copy(bf16[256,2,8,256]{0,3,2,1:T(8,128)(2,1)} %all-gather.2.cloned.1.call-done) | data formatting | bytes 4194304 | tf_op jit(solution)/shard_map/all_gather | solution.py:66
  116.1 3.6 %all-to-all-start = ((bf16[256,2,8,256]{3,2,1,0:T(8,128)(2,1)}), bf16[256,2,8,256]{3,2,1,0:T(8,128)(2,1)S(1)}, u32[]{:S(2)}, u32[]{:S(2)}) async-start(bf16[256,2,8,256]{3,2,1,0:T(8,128)(2,1)} %copy.41), calls=%async_computation | async-start | bytes 4194304 | tf_op jit(solution)/shard_map/all_to_all | solution.py:67
  119.7 25.5 %all-to-all-done = bf16[256,2,8,256]{3,2,1,0:T(8,128)(2,1)S(1)} async-done(((bf16[256,2,8,256]{3,2,1,0:T(8,128)(2,1)}), bf16[256,2,8,256]{3,2,1,0:T(8,128)(2,1)S(1)}, u32[]{:S(2)}, u32[]{:S(2)}) %all-to-all-start) | async-done | bytes 2097184 | tf_op jit(solution)/shard_map/all_to_all | solution.py:67
  145.2 0.3 copy.56
  145.5 0.1 slice_negate_fusion
  145.7 1.0 convolution_bitcast_fusion
  146.7 1.0 fusion.12
  147.7 2.5 %maximum_multiply_fusion = f32[2,64,32,256]{3,2,1,0:T(8,128)} fusion(f32[1,64,32,256]{3,2,1,0:T(8,128)S(1)} %fusion.12, f32[1,64,32,256]{3,2,1,0:T(8,128)S(1)} %convolution_bitcast_fusion), kind=kLoop, calls=%fused_computation | loop fusion | flops 2097152 | bytes 8388608 | tf_op jit(solution)/shard_map/mul | solution.py:71
  (11 shorter events, 0.3 us)
Async XLA Ops:
  6.5 105.1 %all-gather.2.cloned.1.call-start = ((), (), s32[]{:S(2)}) async-start(), calls=%async_computation.1 | async-start | bytes 2359296 | tf_op jit(solution)/shard_map/all_gather | solution.py:66
  7.3 8.3 %collective-permute-start = (bf16[32,256]{1,0:T(8,128)(2,1)S(1)}, bf16[32,256]{1,0:T(8,128)(2,1)S(1)}, u32[]{:S(2)}, u32[]{:S(2)}) collective-permute-start(bf16[32,256]{1,0:T(8,128)(2,1)S(1)} %slice.12), channel_id=1, source_target_pairs={{0,8},{8,16},{16,24},{1,9},{9,17},{17,25},{2,10},{10,18},{18,26},{... | collective-permute-start | bytes 49160 | tf_op jit(solution)/shard_map/ppermute | solution.py:14
  18.6 61.8 %copy-start = (pred[8,544]{1,0:T(8,128)(4,1)S(1)}, pred[8,544]{1,0:T(8,128)(4,1)}, u32[]{:S(2)}) copy-start(pred[8,544]{1,0:T(8,128)(4,1)} %constant.37) | copy-start | bytes 13060
  116.1 29.1 %all-to-all-start = ((bf16[256,2,8,256]{3,2,1,0:T(8,128)(2,1)}), bf16[256,2,8,256]{3,2,1,0:T(8,128)(2,1)S(1)}, u32[]{:S(2)}, u32[]{:S(2)}) async-start(bf16[256,2,8,256]{3,2,1,0:T(8,128)(2,1)} %copy.41), calls=%async_computation | async-start | bytes 4194304 | tf_op jit(solution)/shard_map/all_to_all | solution.py:67
Sparse Core Ops, SparseCore 0:
  82.1 29.4 all-gather.1

commit v2 on v1

--- a/solution.py
+++ b/solution.py
@@ -63,11 +63,9 @@
     spectra = jnp.einsum(
         "csn,npk->kpsc", segments, make_table(), preferred_element_type=jnp.float32
     ).astype(jnp.bfloat16)
-    gathered = lax.all_gather(spectra, "chan", axis=3, tiled=True)
-    all_bins = lax.all_to_all(gathered, "tm", split_axis=0, concat_axis=2, tiled=True)
+    own_bins = lax.all_to_all(spectra, "tm", split_axis=0, concat_axis=2, tiled=True)
+    all_bins = lax.all_gather(own_bins, "chan", axis=3, tiled=True)
     factor = 1.0 / (all_bins.shape[2] * SEG)
-    first_col = lax.axis_index("chan") * channels
-    own_bins = lax.dynamic_slice_in_dim(all_bins, first_col, channels, 3)
     result = cross_block(own_bins, all_bins) * factor
     return result
 

time: 157 us -> 159 us (1.013)
  waiting for transfers between devices: 55.1 us -> 45.3 us
  local copies, waits for them, and re-layouts: 9.31 us -> 18.1 us
  blocking collectives: 0 us -> 8.32 us
  starting transfers between devices: 8.48 us -> 4.83 us
  matrix products: 64.1 us -> 62.3 us
    all_to_all x1 -> x0, waiting for transfers between devices: 25.5 us -> none  [shards(): lax.all_to_all(gathered, 'tm', split_axis=0, concat_axis=2, tiled=True)]
    all_gather x1, waiting for transfers between devices: 29.6 us -> 45.2 us  [shards(): all_bins = lax.all_gather(own_bins, 'chan', axis=3, tiled=True)]
    all_to_all x0 -> x1, blocking collectives: none -> 8.32 us  [shards(): lax.all_to_all(spectra, 'tm', split_axis=0, concat_axis=2, tiled=True)]
    all_to_all x1 -> x4, local copies, waits for them, and re-layouts: 0.27 us -> 4.15 us  [shards(): lax.all_to_all(spectra, 'tm', split_axis=0, concat_axis=2, tiled=True)]
    all_to_all x1 -> x0, starting transfers between devices: 3.65 us -> none  [shards(): lax.all_to_all(gathered, 'tm', split_axis=0, concat_axis=2, tiled=True)]
    all_gather x1, local copies, waits for them, and re-layouts: 4.49 us -> 7.02 us  [shards(): all_bins = lax.all_gather(own_bins, 'chan', axis=3, tiled=True)]
  transfers between devices with their start and end apart: 3 -> 2, of which waited for: 2 -> 1; matrix products, arithmetic and copies ran while one was open for 2% -> 3% of each run, Pallas kernels for 0% -> 0%
where the time goes in v2:
time: 159 us
  matrix products  62.3 us (39%)
  waiting for transfers between devices  45.3 us (28%)
  local copies, waits for them, and re-layouts  18.1 us (11%)
  between operations  13.6 us (9%)
  blocking collectives  8.32 us (5%)
  other arithmetic  6.52 us (4%)
  starting transfers between devices  4.83 us (3%)
    conv_general_dilated x1, matrix products, shards(): lax.conv_general_dilated(extended[None], jnp.flip(fir_taps, axis=1)[:, No...  61 us
    all_gather x1, waiting for transfers between devices, shards(): all_bins = lax.all_gather(own_bins, 'chan', axis=3, tiled=True)  45.2 us
    all_to_all x1, blocking collectives, shards(): lax.all_to_all(spectra, 'tm', split_axis=0, concat_axis=2, tiled=True)  8.32 us
    all_gather x1, local copies, waits for them, and re-layouts, shards(): all_bins = lax.all_gather(own_bins, 'chan', axis=3, tiled=True)  7.02 us
    ppermute x1, starting transfers between devices, shifted(): return lax.ppermute(value, axis, pairs)  4.83 us
    all_to_all x4, local copies, waits for them, and re-layouts, shards(): lax.all_to_all(spectra, 'tm', split_axis=0, concat_axis=2, tiled=True)  4.15 us
  transfers between devices with their start and end apart: 2, of which 1 were waited for; matrix products, arithmetic and copies ran while one was open for 3% of the time, Pallas kernels for 0%

profile of v2, /device:TPU:0, one launch (start us, length us, event | category | flops | bytes accessed | tf_op | source)
XLA Modules:
  0.0 159.0 jit_solution(11957964831942247785)
XLA Ops:
  6.5 0.7 slice.12
  7.3 4.8 %collective-permute-start = (bf16[32,256]{1,0:T(8,128)(2,1)S(1)}, bf16[32,256]{1,0:T(8,128)(2,1)S(1)}, u32[]{:S(2)}, u32[]{:S(2)}) collective-permute-start(bf16[32,256]{1,0:T(8,128)(2,1)S(1)} %slice.12), channel_id=1, source_target_pairs={{0,8},{8,16},{16,24},{1,9},{9,17},{17,25},{2,10},{10,18},{18,26},{... | collective-permute-start | bytes 49160 | tf_op jit(solution)/shard_map/ppermute | solution.py:14
  12.2 2.3 %multiply_convert_fusion = (bf16[512,1,256]{2,0,1:T(8,128)(2,1)S(1)}, bf16[512,1,256]{2,0,1:T(8,128)(2,1)S(1)}) fusion(f32[512]{0:T(512)S(1)} %fusion.28, f32[512]{0:T(512)S(1)} %multiply_subtract_fusion), kind=kLoop, calls=%fused_computation.30 | loop fusion | flops 2359296 | bytes 528384 | tf_op jit(solution)/shard_map/convert.1
  14.5 0.9 rev.4
  15.5 1.1 fusion.25
  16.6 0.6 reshape.125
  17.2 0.9 copy.70
  18.2 0.4 fusion.41
  18.6 61.0 %fusion.7 = bf16[8,544,32]{2,0,1:T(8,128)(2,1)S(1)} fusion(bf16[32,1,256]{0,1,2:T(2,128)(2,1)S(1)} %copy.71, bf16[32,8,799]{0,1,2:T(8,128)(2,1)S(1)} %fusion.41), kind=kOutput, calls=%fused_computation.9 | convolution fusion | flops 71303168 | bytes 704000 | tf_op jit(solution)/shard_map/conv_general_dilated | solution.py:52
  79.6 0.8 copy.72
  80.6 0.3 reshape.129
  81.0 0.3 fusion.15
  81.3 0.9 copy.75
  82.3 1.0 reshape.139
  83.2 8.3 %all_to_all.18 = bf16[4,2,16384]{2,1,0:T(2,128)(2,1)S(1)} all-to-all(bf16[4,2,16384]{2,1,0:T(2,128)(2,1)S(1)} %reshape.139), channel_id=1, replica_groups=mesh['tm'=4,'chan'=8] {'tm'}, dimensions={0} | all-to-all | bytes 524288 | tf_op jit(solution)/shard_map/all_to_all | solution.py:66
  91.5 0.5 reshape.140
  92.0 1.0 copy.87
  93.0 1.4 copy.95
  94.5 1.7 %copy.79 = bf16[64,2,32,32]{2,3,1,0:T(8,128)(2,1)S(1)} copy(bf16[64,2,32,32]{0,3,2,1:T(8,128)(2,1)S(1)} %bitcast.50) | data formatting | bytes 524288 | tf_op jit(solution)/shard_map/all_to_all | solution.py:66
  96.2 45.2 %all-gather.2.cloned.1.call-done = bf16[64,2,32,256]{0,2,1,3:T(8,128)(2,1)} async-done(((bf16[64,2,32,32]{0,2,1,3:T(8,128)(2,1)}), bf16[64,2,32,256]{0,2,1,3:T(8,128)(2,1)}) %all-gather.2.cloned.1.call-update) | async-done | bytes 2097168 | tf_op jit(solution)/shard_map/all_gather | solution.py:67
  141.5 7.0 %copy.80 = bf16[64,2,32,256]{3,2,1,0:T(8,128)(2,1)S(1)} copy(bf16[64,2,32,256]{0,2,1,3:T(8,128)(2,1)} %all-gather.2.cloned.1.call-done) | data formatting | bytes 4194304 | tf_op jit(solution)/shard_map/all_gather | solution.py:67
  148.6 0.5 convolution_bitcast_fusion
  149.1 0.5 fusion.12
  149.7 2.5 %maximum_multiply_fusion = f32[2,64,32,256]{3,2,1,0:T(8,128)} fusion(f32[1,64,32,256]{3,2,1,0:T(8,128)S(1)} %fusion.12, f32[1,64,32,256]{3,2,1,0:T(8,128)S(1)} %convolution_bitcast_fusion), kind=kLoop, calls=%fused_computation | loop fusion | flops 2097152 | bytes 8388608 | tf_op jit(solution)/shard_map/mul | solution.py:69
  (16 shorter events, 0.9 us)
Async XLA Ops:
  6.5 134.9 %all-gather.2.cloned.1.call-start = ((), (), s32[]{:S(2)}) async-start(), calls=%async_computation.1 | async-start | bytes 4718592 | tf_op jit(solution)/shard_map/all_gather | solution.py:67
  7.3 8.3 %collective-permute-start = (bf16[32,256]{1,0:T(8,128)(2,1)S(1)}, bf16[32,256]{1,0:T(8,128)(2,1)S(1)}, u32[]{:S(2)}, u32[]{:S(2)}) collective-permute-start(bf16[32,256]{1,0:T(8,128)(2,1)S(1)} %slice.12), channel_id=1, source_target_pairs={{0,8},{8,16},{16,24},{1,9},{9,17},{17,25},{2,10},{10,18},{18,26},{... | collective-permute-start | bytes 49160 | tf_op jit(solution)/shard_map/ppermute | solution.py:14
  18.6 61.8 %copy-start = (pred[8,544]{1,0:T(8,128)(4,1)S(1)}, pred[8,544]{1,0:T(8,128)(4,1)}, u32[]{:S(2)}) copy-start(pred[8,544]{1,0:T(8,128)(4,1)} %constant.28) | copy-start | bytes 13060
Sparse Core Ops, SparseCore 0:
  94.6 46.8 all-gather.1

commit v3 on v2

--- a/solution.py
+++ b/solution.py
@@ -3,6 +3,8 @@
 import jax
 import jax.numpy as jnp
 from jax import lax
+from jax.experimental import pallas as pl
+from jax.experimental.pallas import tpu as pltpu
 from jax.sharding import PartitionSpec as P
 
 SEG = 512
@@ -44,21 +46,59 @@
     return jnp.stack([real_part, imag_part], axis=0)
 
 
+def fir_kernel(taps_ref, early_ref, late_ref, out_ref):
+    half = taps_ref.shape[1] // 2
+    row = lax.broadcasted_iota(jnp.int32, (half, half), 0)
+    col = lax.broadcasted_iota(jnp.int32, (half, half), 1)
+    upper = col >= row
+    zero = jnp.zeros((half, half), jnp.float32)
+    for ci in range(taps_ref.shape[0]):
+        taps = taps_ref[pl.ds(ci, 1), :].astype(jnp.float32)
+        low = jnp.broadcast_to(taps[:, :half], (half, half))
+        high = jnp.broadcast_to(taps[:, half:], (half, half))
+        low = pltpu.roll(low, 0, 1, stride=1, stride_axis=0)
+        high = pltpu.roll(high, 0, 1, stride=1, stride_axis=0)
+        d0 = jnp.where(upper, zero, high).astype(jnp.bfloat16)
+        d1 = jnp.where(upper, high, low).astype(jnp.bfloat16)
+        d2 = jnp.where(upper, low, zero).astype(jnp.bfloat16)
+        none = jnp.zeros_like(d0)
+        top = jnp.concatenate(
+            [jnp.concatenate([d0, none], axis=1), jnp.concatenate([d1, d0], axis=1)], axis=0
+        )
+        bottom = jnp.concatenate(
+            [jnp.concatenate([d2, d1], axis=1), jnp.concatenate([none, d2], axis=1)], axis=0
+        )
+        acc = jnp.dot(early_ref[ci], top, preferred_element_type=jnp.float32)
+        acc = acc + jnp.dot(late_ref[ci], bottom, preferred_element_type=jnp.float32)
+        out_ref[ci] = acc.astype(out_ref.dtype)
+
+
+def whiten(fir_taps, early, late):
+    channels, nblocks, tap_count = late.shape
+    group = 8
+    block = pl.BlockSpec((group, nblocks, tap_count), lambda g: (g, 0, 0))
+    return pl.pallas_call(
+        fir_kernel,
+        out_shape=jax.ShapeDtypeStruct(late.shape, jnp.bfloat16),
+        grid=(channels // group,),
+        in_specs=[pl.BlockSpec((group, tap_count), lambda g: (g, 0)), block, block],
+        out_specs=block,
+        cost_estimate=pl.CostEstimate(
+            flops=4 * channels * nblocks * tap_count * tap_count,
+            bytes_accessed=3 * late.size * 2 + fir_taps.size * 2,
+            transcendentals=0,
+        ),
+    )(fir_taps, early, late)
+
+
 def shards(strain, fir_taps):
     tap_count = fir_taps.shape[1]
     channels = strain.shape[0]
     previous = shifted(strain[:, -tap_count:], "tm", 1)
-    extended = jnp.concatenate([previous, strain], axis=1)[:, 1:]
-    filtered = lax.conv_general_dilated(
-        extended[None],
-        jnp.flip(fir_taps, axis=1)[:, None, :],
-        window_strides=(1,),
-        padding="VALID",
-        dimension_numbers=("NCH", "OIH", "NCH"),
-        feature_group_count=channels,
-        preferred_element_type=jnp.float32,
-    )[0]
-    whitened = filtered.reshape(channels, -1).astype(jnp.bfloat16)
+    early = jnp.concatenate([previous, strain[:, :-tap_count]], axis=1)
+    early = early.reshape(channels, -1, tap_count)
+    late = strain.reshape(channels, -1, tap_count)
+    whitened = whiten(fir_taps, early, late).reshape(channels, -1)
     segments = whitened.reshape(channels, whitened.shape[1] // SEG, SEG)
     spectra = jnp.einsum(
         "csn,npk->kpsc", segments, make_table(), preferred_element_type=jnp.float32

time: 159 us -> 101 us (0.64)
  matrix products: 62.3 us -> 1.32 us
  Pallas kernels: 0 us -> 4 us
    conv_general_dilated x1 -> x0, matrix products: 61 us -> none  [shards(): lax.conv_general_dilated(extended[None], jnp.flip(fir_taps, axis=1)[:, No...]
    pallas_call x0 -> x1, Pallas kernels: none -> 4 us  [whiten(): pl.pallas_call(fir_kernel, out_shape=jax.ShapeDtypeStruct(late.shape, jnp...]
    unnamed x5 -> x4, local copies, waits for them, and re-layouts: 1.55 us -> 3.9 us
    conv_general_dilated x4 -> x0, local copies, waits for them, and re-layouts: 2.33 us -> none  [shards(): lax.conv_general_dilated(extended[None], jnp.flip(fir_taps, axis=1)[:, No...]
  transfers between devices with their start and end apart: 2 -> 2, of which waited for: 1 -> 1; matrix products, arithmetic and copies ran while one was open for 3% -> 7% of each run, Pallas kernels for 0% -> 0%
where the time goes in v3:
time: 101 us
  waiting for transfers between devices  45.3 us (45%)
  local copies, waits for them, and re-layouts  18.7 us (19%)
  between operations  13.5 us (13%)
  blocking collectives  8.31 us (8%)
  other arithmetic  5.02 us (5%)
  starting transfers between devices  4.83 us (5%)
  Pallas kernels  4 us (4%)
  matrix products  1.32 us (1%)
    all_gather x1, waiting for transfers between devices, shards(): all_bins = lax.all_gather(own_bins, 'chan', axis=3, tiled=True)  45.2 us
    all_to_all x1, blocking collectives, shards(): lax.all_to_all(spectra, 'tm', split_axis=0, concat_axis=2, tiled=True)  8.31 us
    all_gather x1, local copies, waits for them, and re-layouts, shards(): all_bins = lax.all_gather(own_bins, 'chan', axis=3, tiled=True)  7.02 us
    ppermute x1, starting transfers between devices, shifted(): return lax.ppermute(value, axis, pairs)  4.83 us
    all_to_all x4, local copies, waits for them, and re-layouts, shards(): lax.all_to_all(spectra, 'tm', split_axis=0, concat_axis=2, tiled=True)  4.15 us
    pallas_call x1, Pallas kernels, whiten(): pl.pallas_call(fir_kernel, out_shape=jax.ShapeDtypeStruct(late.shape, jnp...  4 us
    unnamed x4, local copies, waits for them, and re-layouts  3.9 us
    mul x1, other arithmetic, shards(): result = cross_block(own_bins, all_bins) * factor  2.46 us
  transfers between devices with their start and end apart: 2, of which 1 were waited for; matrix products, arithmetic and copies ran while one was open for 7% of the time, Pallas kernels for 0%

profile of v3, /device:TPU:0, one launch (start us, length us, event | category | flops | bytes accessed | tf_op | source)
XLA Modules:
  0.0 101.0 jit_solution(18006720905762257617)
XLA Ops:
  6.5 0.7 slice.12
  7.3 4.8 %collective-permute-start = (bf16[32,256]{1,0:T(8,128)(2,1)S(1)}, bf16[32,256]{1,0:T(8,128)(2,1)S(1)}, u32[]{:S(2)}, u32[]{:S(2)}) collective-permute-start(bf16[32,256]{1,0:T(8,128)(2,1)S(1)} %slice.12), channel_id=1, source_target_pairs={{0,8},{8,16},{16,24},{1,9},{9,17},{17,25},{2,10},{10,18},{18,26},{... | collective-permute-start | bytes 49160 | tf_op jit(solution)/shard_map/ppermute | solution.py:16
  12.2 2.3 %multiply_convert_fusion = (bf16[512,1,256]{2,0,1:T(8,128)(2,1)S(1)}, bf16[512,1,256]{2,0,1:T(8,128)(2,1)S(1)}) fusion(f32[512]{0:T(512)S(1)} %fusion.18, f32[512]{0:T(512)S(1)} %multiply_subtract_fusion), kind=kLoop, calls=%fused_computation.20 | loop fusion | flops 2359296 | bytes 528384 | tf_op jit(solution)/shard_map/convert.1
  14.5 1.0 slice.13
  15.5 1.7 %copy.38 = bf16[4,8,16,256]{3,2,1,0:T(8,128)(2,1)} copy(bf16[4,8,16,256]{3,1,2,0:T(8,128)(2,1)} %bitcast.38) | data formatting | bytes 524288
  17.2 0.8 copy.37
  18.0 4.0 %shard_map.28 = bf16[32,16,256]{2,1,0:T(8,128)(2,1)} custom-call(bf16[32,256]{1,0:T(8,128)(2,1)} %taps_ref.1, bf16[32,16,256]{2,1,0:T(8,128)(2,1)} %bitcast.37, bf16[32,16,256]{2,1,0:T(8,128)(2,1)} %bitcast.36), custom_call_target="tpu_custom_call" | custom-call | flops 134217728 | bytes 802816 | tf_op jit(solution)/shard_map/pallas_call | solution.py:80
  22.0 1.0 %reshape_reshape.3 = bf16[32,8,512]{2,1,0:T(8,128)(2,1)S(1)} reshape(bf16[32,16,256]{2,1,0:T(8,128)(2,1)} %shard_map.28) | data formatting | bytes 524288 | tf_op jit(solution)/shard_map/reshape;reshape | solution.py:102
  23.0 0.3 fusion.7
  23.3 0.9 copy.23
  24.3 1.0 reshape.132
  25.2 8.3 %all_to_all.18 = bf16[4,2,16384]{2,1,0:T(2,128)(2,1)S(1)} all-to-all(bf16[4,2,16384]{2,1,0:T(2,128)(2,1)S(1)} %reshape.132), channel_id=1, replica_groups=mesh['tm'=4,'chan'=8] {'tm'}, dimensions={0} | all-to-all | bytes 524288 | tf_op jit(solution)/shard_map/all_to_all | solution.py:106
  33.5 0.5 reshape.133
  34.0 1.0 copy.35
  35.0 1.4 %copy.44 = bf16[64,2,4,8,32]{0,3,2,1,4:T(8,128)(2,1)} copy(bf16[64,2,4,8,32]{0,2,4,3,1:T(4,128)(2,1)S(1)} %bitcast.31) | data formatting | bytes 524288 | tf_op jit(solution)/shard_map/all_to_all | solution.py:106
  36.4 0.0 all-gather.2.cloned.1.call-update
  36.5 0.1 copy.25
  36.6 1.7 %copy.27 = bf16[64,2,32,32]{2,3,1,0:T(8,128)(2,1)S(1)} copy(bf16[64,2,32,32]{0,3,2,1:T(8,128)(2,1)S(1)} %bitcast.34) | data formatting | bytes 524288 | tf_op jit(solution)/shard_map/all_to_all | solution.py:106
  38.2 45.2 %all-gather.2.cloned.1.call-done = bf16[64,2,32,256]{0,2,1,3:T(8,128)(2,1)} async-done(((bf16[64,2,32,32]{0,2,1,3:T(8,128)(2,1)}), bf16[64,2,32,256]{0,2,1,3:T(8,128)(2,1)}) %all-gather.2.cloned.1.call-update) | async-done | bytes 2097168 | tf_op jit(solution)/shard_map/all_gather | solution.py:107
  83.5 7.0 %copy.28 = bf16[64,2,32,256]{3,2,1,0:T(8,128)(2,1)S(1)} copy(bf16[64,2,32,256]{0,2,1,3:T(8,128)(2,1)} %all-gather.2.cloned.1.call-done) | data formatting | bytes 4194304 | tf_op jit(solution)/shard_map/all_gather | solution.py:107
  90.5 0.1 slice_negate_fusion
  90.7 0.5 convolution_bitcast_fusion
  91.2 0.5 fusion.4
  91.7 2.5 %maximum_multiply_fusion = f32[2,64,32,256]{3,2,1,0:T(8,128)} fusion(f32[1,64,32,256]{3,2,1,0:T(8,128)S(1)} %fusion.4, f32[1,64,32,256]{3,2,1,0:T(8,128)S(1)} %convolution_bitcast_fusion), kind=kLoop, calls=%fused_computation | loop fusion | flops 2097152 | bytes 8388608 | tf_op jit(solution)/shard_map/mul | solution.py:109
  (5 shorter events, 0.1 us)
Async XLA Ops:
  6.5 77.0 %all-gather.2.cloned.1.call-start = ((), (), s32[]{:S(2)}) async-start(), calls=%async_computation.1 | async-start | bytes 4718592 | tf_op jit(solution)/shard_map/all_gather | solution.py:107
  7.3 9.9 %collective-permute-start = (bf16[32,256]{1,0:T(8,128)(2,1)S(1)}, bf16[32,256]{1,0:T(8,128)(2,1)S(1)}, u32[]{:S(2)}, u32[]{:S(2)}) collective-permute-start(bf16[32,256]{1,0:T(8,128)(2,1)S(1)} %slice.12), channel_id=1, source_target_pairs={{0,8},{8,16},{16,24},{1,9},{9,17},{17,25},{2,10},{10,18},{18,26},{... | collective-permute-start | bytes 49160 | tf_op jit(solution)/shard_map/ppermute | solution.py:16
Sparse Core Ops, SparseCore 0:
  36.6 46.8 all-gather.1

commit v4 on v3

--- a/solution.py
+++ b/solution.py
@@ -103,11 +103,61 @@
     spectra = jnp.einsum(
         "csn,npk->kpsc", segments, make_table(), preferred_element_type=jnp.float32
     ).astype(jnp.bfloat16)
-    own_bins = lax.all_to_all(spectra, "tm", split_axis=0, concat_axis=2, tiled=True)
-    all_bins = lax.all_gather(own_bins, "chan", axis=3, tiled=True)
-    factor = 1.0 / (all_bins.shape[2] * SEG)
-    result = cross_block(own_bins, all_bins) * factor
-    return result
+    return cross_spectra(spectra)
+
+
+def permuted(value, axis, pairs):
+    return lax.ppermute(value, axis, [(a, b) for a, b in pairs])
+
+
+def exchange_bins(spectra):
+    size = lax.axis_size("tm")
+    me = lax.axis_index("tm")
+    pieces = spectra.reshape((size, spectra.shape[0] // size) + spectra.shape[1:])
+    received = [pieces[me]]
+    for m in range(1, size):
+        piece = lax.dynamic_index_in_dim(pieces, me ^ m, 0, keepdims=False)
+        received.append(permuted(piece, "tm", [(i, i ^ m) for i in range(size)]))
+    return jnp.stack(received, axis=0)
+
+
+def gather_channels(shard):
+    size = lax.axis_size("chan")
+    chips = size // 2
+    me = lax.axis_index("chan")
+    chip, core = me // 2, me % 2
+    right = [(c * 2 + k, (c + 1) * 2 + k) for c in range(chips - 1) for k in range(2)]
+    left = [(b, a) for a, b in right]
+    from_left, from_right = [None], [None]
+    going_right, going_left = shard, shard
+    for _ in range(1, chips):
+        going_right = permuted(going_right, "chan", right)
+        going_left = permuted(going_left, "chan", left)
+        from_left.append(going_right)
+        from_right.append(going_left)
+    rotated = [shard]
+    for u in range(1, chips):
+        rotated.append(jnp.where(chip + u < chips, from_right[u], from_left[chips - u]))
+    rotated = jnp.stack(rotated, axis=0)
+    doubled = jnp.concatenate([rotated, rotated], axis=0)
+    mine = lax.dynamic_slice_in_dim(doubled, chips - chip, chips, axis=0)
+    other = permuted(mine, "chan", [(i, i ^ 1) for i in range(size)])
+    first = jnp.where(core == 0, mine, other)
+    second = jnp.where(core == 0, other, mine)
+    return jnp.stack([first, second], axis=1)
+
+
+def cross_spectra(spectra):
+    own = exchange_bins(spectra)
+    every = gather_channels(own)
+    wide = every.shape[0] * every.shape[1] * every.shape[-1]
+    swapped = jnp.stack([-every[:, :, :, :, 1], every[:, :, :, :, 0]], axis=4)
+    real_part = jnp.einsum("ukpsi,qrukpsj->kiqrj", own, every, preferred_element_type=jnp.float32)
+    imag_part = jnp.einsum("ukpsi,qrukpsj->kiqrj", own, swapped, preferred_element_type=jnp.float32)
+    result = jnp.stack([real_part, imag_part], axis=0)
+    result = result.reshape(result.shape[:3] + (wide,))
+    factor = 1.0 / (own.shape[0] * own.shape[3] * SEG)
+    return result * factor
 
 
 def solution(mesh):

time: 101 us -> 171 us (1.69)
  local copies, waits for them, and re-layouts: 18.7 us -> 68.2 us
  other arithmetic: 5.02 us -> 28.9 us
  starting transfers between devices: 4.83 us -> 26.4 us
  waiting for transfers between devices: 45.3 us -> 30.6 us
  between operations: 13.5 us -> 0.27 us
  matrix products: 1.32 us -> 10.9 us
  blocking collectives: 8.31 us -> 0 us
    all_gather x1 -> x0, waiting for transfers between devices: 45.2 us -> none  [shards(): all_bins = lax.all_gather(own_bins, 'chan', axis=3, tiled=True)]
    ppermute x0 -> x10, waiting for transfers between devices: none -> 30.6 us  [permuted(): return lax.ppermute(value, axis, [(a, b) for a, b in pairs])]
    ppermute x0 -> x7, local copies, waits for them, and re-layouts: none -> 23.8 us  [permuted(): return lax.ppermute(value, axis, [(a, b) for a, b in pairs])]
    ppermute x0 -> x10, starting transfers between devices: none -> 21.6 us  [permuted(): return lax.ppermute(value, axis, [(a, b) for a, b in pairs])]
    dot_general x0 -> x2, local copies, waits for them, and re-layouts: none -> 15.5 us  [the longest x1 7.77 us: cross_spectra(): jnp.einsum('ukpsi,qrukpsj->kiqrj', own, swapped, preferred_element_type=j...]
    dynamic_slice x0 -> x6, local copies, waits for them, and re-layouts: none -> 13.7 us  [the longest x2 11.7 us: gather_channels(): mine = lax.dynamic_slice_in_dim(doubled, chips - chip, chips, axis=0)]
    unnamed x0 -> x7, other arithmetic: none -> 12.4 us
    dot_general x2, matrix products: 1.02 us -> 10.6 us  [the longest x1 6.4 us: cross_spectra(): jnp.einsum('ukpsi,qrukpsj->kiqrj', own, swapped, preferred_element_type=j...]
  transfers between devices with their start and end apart: 2 -> 11, of which waited for: 1 -> 5; matrix products, arithmetic and copies ran while one was open for 7% -> 13% of each run, Pallas kernels for 0% -> 0%
where the time goes in v4:
time: 171 us; the launch traced here: 169 us
  local copies, waits for them, and re-layouts  68.2 us (40%)
  waiting for transfers between devices  30.6 us (18%)
  other arithmetic  28.9 us (17%)
  starting transfers between devices  26.4 us (15%)
  matrix products  10.9 us (6%)
  Pallas kernels  4 us (2%)
    ppermute x10, waiting for transfers between devices, permuted(): return lax.ppermute(value, axis, [(a, b) for a, b in pairs])  30.6 us
    ppermute x7, local copies, waits for them, and re-layouts, permuted(): return lax.ppermute(value, axis, [(a, b) for a, b in pairs])  23.8 us
    ppermute x10, starting transfers between devices, permuted(): return lax.ppermute(value, axis, [(a, b) for a, b in pairs])  21.6 us
    unnamed x7, other arithmetic  12.4 us
    dynamic_slice x2, local copies, waits for them, and re-layouts, gather_channels(): mine = lax.dynamic_slice_in_dim(doubled, chips - chip, chips, axis=0)  11.7 us
    dot_general x1, local copies, waits for them, and re-layouts, cross_spectra(): jnp.einsum('ukpsi,qrukpsj->kiqrj', own, swapped, preferred_element_type=j...  7.77 us
    dot_general x1, local copies, waits for them, and re-layouts, cross_spectra(): jnp.einsum('ukpsi,qrukpsj->kiqrj', own, every, preferred_element_type=jnp...  7.76 us
    another operation x2, local copies, waits for them, and re-layouts, cross_spectra(): result = jnp.stack([real_part, imag_part], axis=0)  7.55 us
  transfers between devices with their start and end apart: 11, of which 5 were waited for; matrix products, arithmetic and copies ran while one was open for 13% of the time, Pallas kernels for 0%

profile of v4, /device:TPU:0, one launch (start us, length us, event | category | flops | bytes accessed | tf_op | source)
XLA Modules:
  0.0 169.3 jit_solution(2108389623654176403)
XLA Ops:
  0.7 4.8 %collective-permute-start = (bf16[32,256]{1,0:T(8,128)(2,1)S(1)}, bf16[32,256]{1,0:T(8,128)(2,1)S(1)}, u32[]{:S(2)}, u32[]{:S(2)}) collective-permute-start(bf16[32,256]{1,0:T(8,128)(2,1)S(1)} %slice.12), channel_id=1, source_target_pairs={{0,8},{8,16},{16,24},{1,9},{9,17},{17,25},{2,10},{10,18},{18,26},{... | collective-permute-start | bytes 49160 | tf_op jit(solution)/shard_map/ppermute | solution.py:16
  11.4 4.0 %shard_map.28 = bf16[32,16,256]{2,1,0:T(8,128)(2,1)} custom-call(bf16[32,256]{1,0:T(8,128)(2,1)} %taps_ref.1, bf16[32,16,256]{2,1,0:T(8,128)(2,1)} %bitcast.77, bf16[32,16,256]{2,1,0:T(8,128)(2,1)} %bitcast.76), custom_call_target="tpu_custom_call" | custom-call | flops 134217728 | bytes 802816 | tf_op jit(solution)/shard_map/pallas_call | solution.py:80
  22.9 5.5 %collective-permute-done.1 = bf16[64,2,8,32]{3,2,1,0:T(8,128)(2,1)S(1)} collective-permute-done((bf16[64,2,8,32]{3,2,1,0:T(8,128)(2,1)S(1)}, bf16[64,2,8,32]{3,2,1,0:T(8,128)(2,1)S(1)}, u32[]{:S(2)}, u32[]{:S(2)}) %collective-permute-start.1) | collective-permute-done | bytes 65568 | tf_op jit(solution)/shard_map/ppermute | solution.py:110
  28.4 5.4 %collective-permute-done.2 = bf16[64,2,8,32]{3,2,1,0:T(8,128)(2,1)S(1)} collective-permute-done((bf16[64,2,8,32]{3,2,1,0:T(8,128)(2,1)S(1)}, bf16[64,2,8,32]{3,2,1,0:T(8,128)(2,1)S(1)}, u32[]{:S(2)}, u32[]{:S(2)}) %collective-permute-start.2) | collective-permute-done | bytes 65568 | tf_op jit(solution)/shard_map/ppermute | solution.py:110
  36.0 3.5 %collective-permute-start.5 = (bf16[4,64,2,8,32]{1,4,3,2,0:T(8,128)(2,1)}, bf16[4,64,2,8,32]{1,4,3,2,0:T(8,128)(2,1)S(1)}, u32[]{:S(2)}, u32[]{:S(2)}) collective-permute-start(bf16[4,64,2,8,32]{1,4,3,2,0:T(8,128)(2,1)} %copy.55), channel_id=1, source_target_pairs={{0,2},{1,3},{2,4},{3,5},{4,6},{5,7},{8,10},{9,11},{10,12},{11,13},... | collective-permute-start | bytes 786440 | tf_op jit(solution)/shard_map/ppermute | solution.py:110
  40.8 8.7 %collective-permute-done.5 = bf16[4,64,2,8,32]{1,4,3,2,0:T(8,128)(2,1)S(1)} collective-permute-done((bf16[4,64,2,8,32]{1,4,3,2,0:T(8,128)(2,1)}, bf16[4,64,2,8,32]{1,4,3,2,0:T(8,128)(2,1)S(1)}, u32[]{:S(2)}, u32[]{:S(2)}) %collective-permute-start.5) | collective-permute-done | bytes 262176 | tf_op jit(solution)/shard_map/ppermute | solution.py:110
  49.6 5.1 %collective-permute-start.6 = (bf16[4,64,2,8,32]{1,4,3,2,0:T(8,128)(2,1)S(1)}, bf16[4,64,2,8,32]{1,4,3,2,0:T(8,128)(2,1)}, u32[]{:S(2)}, u32[]{:S(2)}) collective-permute-start(bf16[4,64,2,8,32]{1,4,3,2,0:T(8,128)(2,1)S(1)} %collective-permute-done.5), channel_id=1, source_target_pairs={{0,2},{1,3},{2,4},{3,5},{4,6},{5,7},{8,10},{9,11},{10,12},{11,13},... | collective-permute-start | bytes 786440 | tf_op jit(solution)/shard_map/ppermute | solution.py:110
  56.0 6.7 %collective-permute-done.6 = bf16[4,64,2,8,32]{1,4,3,2,0:T(8,128)(2,1)} collective-permute-done((bf16[4,64,2,8,32]{1,4,3,2,0:T(8,128)(2,1)S(1)}, bf16[4,64,2,8,32]{1,4,3,2,0:T(8,128)(2,1)}, u32[]{:S(2)}, u32[]{:S(2)}) %collective-permute-start.6) | collective-permute-done | bytes 262176 | tf_op jit(solution)/shard_map/ppermute | solution.py:110
  62.7 5.3 %collective-permute-start.7 = (bf16[4,64,2,8,32]{1,4,3,2,0:T(8,128)(2,1)}, bf16[4,64,2,8,32]{1,4,3,2,0:T(8,128)(2,1)}, u32[]{:S(2)}, u32[]{:S(2)}) collective-permute-start(bf16[4,64,2,8,32]{1,4,3,2,0:T(8,128)(2,1)} %collective-permute-done.6), channel_id=1, source_target_pairs={{0,2},{1,3},{2,4},{3,5},{4,6},{5,7},{8,10},{9,11},{10,12},{11,13},... | collective-permute-start | bytes 786440 | tf_op jit(solution)/shard_map/ppermute | solution.py:110
  76.6 3.5 %copy.60 = bf16[4,64,2,8,32]{4,3,0,2,1:T(8,128)(2,1)} copy(bf16[4,64,2,8,32]{1,4,3,2,0:T(8,128)(2,1)} %collective-permute-done.6) | data formatting | bytes 524288 | tf_op jit(solution)/shard_map/ppermute | solution.py:110
  80.1 3.4 %copy.58 = bf16[4,64,2,8,32]{4,3,0,2,1:T(8,128)(2,1)} copy(bf16[4,64,2,8,32]{1,4,3,2,0:T(8,128)(2,1)} %collective-permute-done.7) | data formatting | bytes 524288 | tf_op jit(solution)/shard_map/ppermute | solution.py:110
  86.4 3.4 %copy.61 = bf16[4,64,2,8,32]{4,3,0,2,1:T(8,128)(2,1)} copy(bf16[4,64,2,8,32]{1,4,3,2,0:T(8,128)(2,1)} %collective-permute-done.9) | data formatting | bytes 524288 | tf_op jit(solution)/shard_map/ppermute | solution.py:110
  99.4 6.0 %constant_dynamic-slice_fusion = bf16[4,4,64,2,8,32]{5,4,1,3,0,2:T(8,128)(2,1)} fusion(bf16[8,4,64,2,8,32]{5,4,1,3,0,2:T(8,128)(2,1)} %bitcast_dynamic-update-slice_fusion.1, s32[]{:T(128)S(6)} %select_n.92), kind=kLoop, calls=%fused_computation.52 | loop fusion | bytes 2097156 | tf_op jit(solution)/shard_map/dynamic_slice | solution.py:143
  105.4 5.7 %copy.63 = bf16[4,4,64,2,8,32]{2,5,4,3,1,0:T(8,128)(2,1)S(1)} copy(bf16[4,4,64,2,8,32]{5,4,1,3,0,2:T(8,128)(2,1)} %constant_dynamic-slice_fusion) | data formatting | bytes 2097152 | tf_op jit(solution)/shard_map/dynamic_slice | solution.py:143
  111.2 4.3 %collective-permute-done.10 = bf16[4,4,64,2,8,32]{2,5,4,3,1,0:T(8,128)(2,1)} collective-permute-done((bf16[4,4,64,2,8,32]{2,5,4,3,1,0:T(8,128)(2,1)S(1)}, bf16[4,4,64,2,8,32]{2,5,4,3,1,0:T(8,128)(2,1)}, u32[]{:S(2)}, u32[]{:S(2)}) %collective-permute-start.10) | collective-permute-done | bytes 1048608 | tf_op jit(solution)/shard_map/ppermute | solution.py:110
  115.5 7.7 %copy.64 = bf16[4,4,64,2,8,32]{5,4,1,3,0,2:T(8,128)(2,1)} copy(bf16[4,4,64,2,8,32]{2,5,4,3,1,0:T(8,128)(2,1)} %collective-permute-done.10) | data formatting | bytes 2097152 | tf_op jit(solution)/shard_map/ppermute | solution.py:110
  123.1 3.8 %select_bitcast_fusion = (bf16[4,1,4,64,2,8,32]{6,5,2,4,1,0,3:T(8,128)(2,1)S(1)}, bf16[4,1,4,64,2,8,32]{6,5,2,4,1,0,3:T(8,128)(2,1)S(1)}) fusion(bf16[4,4,64,2,8,32]{5,4,1,3,0,2:T(8,128)(2,1)} %copy.64, pred[]{:T(512)S(6)} %eq.8, bf16[8,4,64,2,8,32]{5,4,1,3,0,2:T(8,128)(2,1)} %bitcast_dynamic-update-slice_fusion.1, s32[]{:T(128)S(6)} %select_n.92), kind=kLoop, calls=%fused_computation.14 | loop fusion | flops 1048576 | bytes 4194309 | tf_op jit(solution)/shard_map/stack | solution.py:147
  127.0 4.2 %fusion.11 = f32[64,32,4,2,32]{4,1,3,2,0:T(8,128)} fusion(bf16[4,1,4,64,2,8,32]{6,5,2,4,1,0,3:T(8,128)(2,1)S(1)} %get-tuple-element.7, bf16[4,1,4,64,2,8,32]{6,5,2,4,1,0,3:T(8,128)(2,1)S(1)} %get-tuple-element.8, bf16[1,64,2,8,32]{4,3,0,2,1:T(8,128)(2,1)S(1)} %bitcast.74, bf16[1,64,2,8,32]{4,3,0,2,1:T(8,128)(2,1)S(1)} %bitcast.69, ...), kind=kOutput, calls=%fused_computation.17 | convolution fusion | flops 72351744 | bytes 4456448 | tf_op jit(solution)/shard_map/ukpsi,qrukpsj->kiqrj/dot_general | solution.py:155
  131.2 4.3 %fusion.6 = (bf16[4,2,4,64,1,8,32]{6,5,2,4,1,0,3:T(8,128)(2,1)}, bf16[4,2,4,64,1,8,32]{6,5,2,4,1,0,3:T(8,128)(2,1)}) fusion(bf16[4,1,4,64,2,8,32]{6,5,2,4,1,0,3:T(8,128)(2,1)S(1)} %get-tuple-element.8, bf16[4,1,4,64,2,8,32]{6,5,2,4,1,0,3:T(8,128)(2,1)S(1)} %get-tuple-element.7), kind=kLoop, calls=%fused_computation.11 | loop fusion | flops 1572864 | bytes 4194304 | tf_op jit(solution)/shard_map/neg | solution.py:154
  135.6 7.8 %copy.67 = f32[64,32,4,2,32]{0,4,3,2,1:T(8,128)} copy(f32[64,32,4,2,32]{4,1,3,2,0:T(8,128)} %fusion.11) | data formatting | bytes 4194304 | tf_op jit(solution)/shard_map/ukpsi,qrukpsj->kiqrj/dot_general | solution.py:155
  146.7 6.4 %fusion.8 = f32[64,32,4,2,32]{4,1,3,2,0:T(8,128)} fusion(bf16[4,2,4,64,1,8,32]{6,5,2,4,1,0,3:T(8,128)(2,1)} %get-tuple-element.6, bf16[4,2,4,64,1,8,32]{6,5,2,4,1,0,3:T(8,128)(2,1)} %get-tuple-element.5, bf16[1,64,2,8,32]{4,3,0,2,1:T(8,128)(2,1)S(1)} %bitcast.75, bf16[1,64,2,8,32]{4,3,0,2,1:T(8,128)(2,1)S(1)} %bitcast.70, ...), kind=kOutput, calls=%fused_computation.16 | convolution fusion | flops 72351744 | bytes 4456448 | tf_op jit(solution)/shard_map/ukpsi,qrukpsj->kiqrj/dot_general | solution.py:156
  153.1 7.8 %copy.68 = f32[64,32,4,2,32]{0,4,3,2,1:T(8,128)} copy(f32[64,32,4,2,32]{4,1,3,2,0:T(8,128)} %fusion.8) | data formatting | bytes 4194304 | tf_op jit(solution)/shard_map/ukpsi,qrukpsj->kiqrj/dot_general | solution.py:156
  160.9 4.2 %copy.70 = f32[1,64,32,256]{3,2,1,0:T(8,128)} copy(f32[1,64,32,256]{1,3,2,0:T(8,128)} %bitcast.60) | data formatting | bytes 4194304 | tf_op jit(solution)/shard_map/stack | solution.py:157
  165.1 4.2 %maximum_multiply_fusion = f32[2,64,32,256]{3,2,1,0:T(8,128)} fusion(f32[1,64,32,256]{3,2,1,0:T(8,128)} %copy.70, f32[1,64,32,256]{3,2,1,0:T(8,128)S(1)} %copy.69), kind=kLoop, calls=%fused_computation.13 | loop fusion | flops 2097152 | bytes 8388608 | tf_op jit(solution)/shard_map/mul | solution.py:160
  (61 shorter events, 43.3 us)
Async XLA Ops:
  0.7 9.9 %collective-permute-start = (bf16[32,256]{1,0:T(8,128)(2,1)S(1)}, bf16[32,256]{1,0:T(8,128)(2,1)S(1)}, u32[]{:S(2)}, u32[]{:S(2)}) collective-permute-start(bf16[32,256]{1,0:T(8,128)(2,1)S(1)} %slice.12), channel_id=1, source_target_pairs={{0,8},{8,16},{16,24},{1,9},{9,17},{17,25},{2,10},{10,18},{18,26},{... | collective-permute-start | bytes 49160 | tf_op jit(solution)/shard_map/ppermute | solution.py:16
  19.1 9.3 %collective-permute-start.1 = (bf16[64,2,8,32]{3,2,1,0:T(8,128)(2,1)S(1)}, bf16[64,2,8,32]{3,2,1,0:T(8,128)(2,1)S(1)}, u32[]{:S(2)}, u32[]{:S(2)}) collective-permute-start(bf16[64,2,8,32]{3,2,1,0:T(8,128)(2,1)S(1)} %bitcast.82), channel_id=1, source_target_pairs={{0,8},{8,0},{16,24},{24,16},{1,9},{9,1},{17,25},{25,17},{2,10},{10... | collective-permute-start | bytes 196616 | tf_op jit(solution)/shard_map/ppermute | solution.py:110
  20.6 13.1 %collective-permute-start.2 = (bf16[64,2,8,32]{3,2,1,0:T(8,128)(2,1)S(1)}, bf16[64,2,8,32]{3,2,1,0:T(8,128)(2,1)S(1)}, u32[]{:S(2)}, u32[]{:S(2)}) collective-permute-start(bf16[64,2,8,32]{3,2,1,0:T(8,128)(2,1)S(1)} %bitcast.81), channel_id=1, source_target_pairs={{0,16},{8,24},{16,0},{24,8},{1,17},{9,25},{17,1},{25,9},{2,18},{10... | collective-permute-start | bytes 196616 | tf_op jit(solution)/shard_map/ppermute | solution.py:110
  20.8 13.0 %collective-permute-start.3 = (bf16[64,2,8,32]{3,2,1,0:T(8,128)(2,1)S(1)}, bf16[64,2,8,32]{3,2,1,0:T(8,128)(2,1)S(1)}, u32[]{:S(2)}, u32[]{:S(2)}) collective-permute-start(bf16[64,2,8,32]{3,2,1,0:T(8,128)(2,1)S(1)} %bitcast.80), channel_id=1, source_target_pairs={{0,24},{8,16},{16,8},{24,0},{1,25},{9,17},{17,9},{25,1},{2,26},{10... | collective-permute-start | bytes 196616 | tf_op jit(solution)/shard_map/ppermute | solution.py:110
  28.4 40.9 %copy-start.3 = (bf16[64,2,8,32]{3,2,1,0:T(8,128)(2,1)}, bf16[64,2,8,32]{3,2,1,0:T(8,128)(2,1)S(1)}, u32[]{:S(2)}) copy-start(bf16[64,2,8,32]{3,2,1,0:T(8,128)(2,1)S(1)} %collective-permute-done.1) | copy-start | bytes 196612
  33.7 35.6 %copy-start.5 = (bf16[64,2,8,32]{3,2,1,0:T(8,128)(2,1)}, bf16[64,2,8,32]{3,2,1,0:T(8,128)(2,1)S(1)}, u32[]{:S(2)}) copy-start(bf16[64,2,8,32]{3,2,1,0:T(8,128)(2,1)S(1)} %collective-permute-done.2) | copy-start | bytes 196612
  33.8 35.6 %copy-start.7 = (bf16[64,2,8,32]{3,2,1,0:T(8,128)(2,1)}, bf16[64,2,8,32]{3,2,1,0:T(8,128)(2,1)S(1)}, u32[]{:S(2)}) copy-start(bf16[64,2,8,32]{3,2,1,0:T(8,128)(2,1)S(1)} %collective-permute-done.3) | copy-start | bytes 196612
  36.0 13.5 %collective-permute-start.5 = (bf16[4,64,2,8,32]{1,4,3,2,0:T(8,128)(2,1)}, bf16[4,64,2,8,32]{1,4,3,2,0:T(8,128)(2,1)S(1)}, u32[]{:S(2)}, u32[]{:S(2)}) collective-permute-start(bf16[4,64,2,8,32]{1,4,3,2,0:T(8,128)(2,1)} %copy.55), channel_id=1, source_target_pairs={{0,2},{1,3},{2,4},{3,5},{4,6},{5,7},{8,10},{9,11},{10,12},{11,13},... | collective-permute-start | bytes 786440 | tf_op jit(solution)/shard_map/ppermute | solution.py:110
  39.5 15.1 %collective-permute-start.4 = (bf16[4,64,2,8,32]{1,4,3,2,0:T(8,128)(2,1)}, bf16[4,64,2,8,32]{1,4,3,2,0:T(8,128)(2,1)S(1)}, u32[]{:S(2)}, u32[]{:S(2)}) collective-permute-start(bf16[4,64,2,8,32]{1,4,3,2,0:T(8,128)(2,1)} %copy.55), channel_id=1, source_target_pairs={{2,0},{3,1},{4,2},{5,3},{6,4},{7,5},{10,8},{11,9},{12,10},{13,11},... | collective-permute-start | bytes 786440 | tf_op jit(solution)/shard_map/ppermute | solution.py:110
  49.6 13.1 %collective-permute-start.6 = (bf16[4,64,2,8,32]{1,4,3,2,0:T(8,128)(2,1)S(1)}, bf16[4,64,2,8,32]{1,4,3,2,0:T(8,128)(2,1)}, u32[]{:S(2)}, u32[]{:S(2)}) collective-permute-start(bf16[4,64,2,8,32]{1,4,3,2,0:T(8,128)(2,1)S(1)} %collective-permute-done.5), channel_id=1, source_target_pairs={{0,2},{1,3},{2,4},{3,5},{4,6},{5,7},{8,10},{9,11},{10,12},{11,13},... | collective-permute-start | bytes 786440 | tf_op jit(solution)/shard_map/ppermute | solution.py:110
  54.7 17.9 %collective-permute-start.8 = (bf16[4,64,2,8,32]{1,4,3,2,0:T(8,128)(2,1)S(1)}, bf16[4,64,2,8,32]{1,4,3,2,0:T(8,128)(2,1)}, u32[]{:S(2)}, u32[]{:S(2)}) collective-permute-start(bf16[4,64,2,8,32]{1,4,3,2,0:T(8,128)(2,1)S(1)} %collective-permute-done.4), channel_id=1, source_target_pairs={{2,0},{3,1},{4,2},{5,3},{6,4},{7,5},{10,8},{11,9},{12,10},{13,11},... | collective-permute-start | bytes 786440 | tf_op jit(solution)/shard_map/ppermute | solution.py:110
  62.7 17.5 %collective-permute-start.7 = (bf16[4,64,2,8,32]{1,4,3,2,0:T(8,128)(2,1)}, bf16[4,64,2,8,32]{1,4,3,2,0:T(8,128)(2,1)}, u32[]{:S(2)}, u32[]{:S(2)}) collective-permute-start(bf16[4,64,2,8,32]{1,4,3,2,0:T(8,128)(2,1)} %collective-permute-done.6), channel_id=1, source_target_pairs={{0,2},{1,3},{2,4},{3,5},{4,6},{5,7},{8,10},{9,11},{10,12},{11,13},... | collective-permute-start | bytes 786440 | tf_op jit(solution)/shard_map/ppermute | solution.py:110
  72.5 13.9 %collective-permute-start.9 = (bf16[4,64,2,8,32]{1,4,3,2,0:T(8,128)(2,1)}, bf16[4,64,2,8,32]{1,4,3,2,0:T(8,128)(2,1)}, u32[]{:S(2)}, u32[]{:S(2)}) collective-permute-start(bf16[4,64,2,8,32]{1,4,3,2,0:T(8,128)(2,1)} %collective-permute-done.8), channel_id=1, source_target_pairs={{2,0},{3,1},{4,2},{5,3},{6,4},{7,5},{10,8},{11,9},{12,10},{13,11},... | collective-permute-start | bytes 786440 | tf_op jit(solution)/shard_map/ppermute | solution.py:110
  89.9 5.3 %copy-start.1 = (bf16[4,64,2,8,32]{4,3,0,2,1:T(8,128)(2,1)S(1)}, bf16[4,64,2,8,32]{4,3,0,2,1:T(8,128)(2,1)}, u32[]{:S(2)}) copy-start(bf16[4,64,2,8,32]{4,3,0,2,1:T(8,128)(2,1)} %copy.58) | copy-start | bytes 786436
  89.9 6.7 %copy-start = (bf16[4,64,2,8,32]{4,3,0,2,1:T(8,128)(2,1)S(1)}, bf16[4,64,2,8,32]{4,3,0,2,1:T(8,128)(2,1)}, u32[]{:S(2)}) copy-start(bf16[4,64,2,8,32]{4,3,0,2,1:T(8,128)(2,1)} %copy.60) | copy-start | bytes 786436
  92.6 5.4 %copy-start.2 = (bf16[4,64,2,8,32]{4,3,0,2,1:T(8,128)(2,1)S(1)}, bf16[4,64,2,8,32]{4,3,0,2,1:T(8,128)(2,1)}, u32[]{:S(2)}) copy-start(bf16[4,64,2,8,32]{4,3,0,2,1:T(8,128)(2,1)} %copy.61) | copy-start | bytes 786436
  111.1 4.4 %collective-permute-start.10 = (bf16[4,4,64,2,8,32]{2,5,4,3,1,0:T(8,128)(2,1)S(1)}, bf16[4,4,64,2,8,32]{2,5,4,3,1,0:T(8,128)(2,1)}, u32[]{:S(2)}, u32[]{:S(2)}) collective-permute-start(bf16[4,4,64,2,8,32]{2,5,4,3,1,0:T(8,128)(2,1)S(1)} %copy.63), channel_id=1, source_target_pairs={{0,1},{1,0},{2,3},{3,2},{4,5},{5,4},{6,7},{7,6},{8,9},{9,8},{10,11... | collective-permute-start | bytes 3145736 | tf_op jit(solution)/shard_map/ppermute | solution.py:110
  123.1 3.9 %copy-start.4 = (bf16[64,2,8,32]{3,2,1,0:T(8,128)(2,1)S(1)}, bf16[64,2,8,32]{3,2,1,0:T(8,128)(2,1)}, u32[]{:S(2)}) copy-start(bf16[64,2,8,32]{3,2,1,0:T(8,128)(2,1)} %copy-done.3) | copy-start | bytes 196612
  123.1 3.9 %copy-start.6 = (bf16[64,2,8,32]{3,2,1,0:T(8,128)(2,1)S(1)}, bf16[64,2,8,32]{3,2,1,0:T(8,128)(2,1)}, u32[]{:S(2)}) copy-start(bf16[64,2,8,32]{3,2,1,0:T(8,128)(2,1)} %copy-done.5) | copy-start | bytes 196612
  123.1 3.9 %copy-start.8 = (bf16[64,2,8,32]{3,2,1,0:T(8,128)(2,1)S(1)}, bf16[64,2,8,32]{3,2,1,0:T(8,128)(2,1)}, u32[]{:S(2)}) copy-start(bf16[64,2,8,32]{3,2,1,0:T(8,128)(2,1)} %copy-done.7) | copy-start | bytes 196612

commit v5 on v3

--- a/solution.py
+++ b/solution.py
@@ -99,15 +99,26 @@
     early = early.reshape(channels, -1, tap_count)
     late = strain.reshape(channels, -1, tap_count)
     whitened = whiten(fir_taps, early, late).reshape(channels, -1)
-    segments = whitened.reshape(channels, whitened.shape[1] // SEG, SEG)
+    segments = whitened.reshape(channels * (whitened.shape[1] // SEG), SEG)
+    parts = lax.axis_size("tm")
+    table = make_table()
+    bins = table.shape[2]
+    table = table.reshape(SEG, 2, parts, bins // parts).transpose(0, 2, 1, 3).reshape(SEG, 2 * bins)
     spectra = jnp.einsum(
-        "csn,npk->kpsc", segments, make_table(), preferred_element_type=jnp.float32
+        "xn,nq->qx", segments, table, preferred_element_type=jnp.float32
     ).astype(jnp.bfloat16)
-    own_bins = lax.all_to_all(spectra, "tm", split_axis=0, concat_axis=2, tiled=True)
-    all_bins = lax.all_gather(own_bins, "chan", axis=3, tiled=True)
-    factor = 1.0 / (all_bins.shape[2] * SEG)
-    result = cross_block(own_bins, all_bins) * factor
-    return result
+    spectra = spectra.reshape(parts, spectra.shape[0] // parts, spectra.shape[1])
+    own = lax.all_to_all(spectra, "tm", split_axis=0, concat_axis=0, tiled=True)
+    every = lax.all_gather(own, "chan", axis=0)
+    own = own.reshape(parts, 2, bins // parts, channels, -1)
+    every = every.reshape(every.shape[:2] + (2, bins // parts, channels, -1))
+    swapped = jnp.stack([-every[:, :, 1], every[:, :, 0]], axis=2)
+    real_part = jnp.einsum("upkis,Jupkjs->kiJj", own, every, preferred_element_type=jnp.float32)
+    imag_part = jnp.einsum("upkis,Jupkjs->kiJj", own, swapped, preferred_element_type=jnp.float32)
+    result = jnp.stack([real_part, imag_part], axis=0)
+    result = result.reshape(result.shape[:3] + (-1,))
+    factor = 1.0 / (parts * own.shape[-1] * SEG)
+    return result * factor
 
 
 def solution(mesh):

time: 101 us -> 143 us (1.42); the launches traced: 101 us -> 141 us
  local copies, waits for them, and re-layouts: 18.7 us -> 57.4 us
  waiting for transfers between devices: 45.3 us -> 25.9 us
  matrix products: 1.32 us -> 13.3 us
  other arithmetic: 5.02 us -> 13.8 us
    reshape x0 -> x4, local copies, waits for them, and re-layouts: none -> 22.9 us  [the longest x2 20.9 us: shards(): every = every.reshape(every.shape[:2] + (2, bins // parts, channels, -1))]
    all_gather x1, waiting for transfers between devices: 45.2 us -> 25.9 us  [shards(): every = lax.all_gather(own, 'chan', axis=0)]
    dot_general x0 -> x2, local copies, waits for them, and re-layouts: none -> 15.5 us  [the longest x1 7.78 us: shards(): jnp.einsum('upkis,Jupkjs->kiJj', own, every, preferred_element_type=jnp.f...]
    dot_general x3, matrix products: 1.32 us -> 13.3 us  [the longest x1 8.3 us: shards(): jnp.einsum('upkis,Jupkjs->kiJj', own, swapped, preferred_element_type=jnp...]
    another operation x1 -> x3, local copies, waits for them, and re-layouts: 1.04 us -> 8.6 us  [the longest x2 7.56 us: shards(): result = jnp.stack([real_part, imag_part], axis=0)]
    neg x2 -> x1, other arithmetic: 0.18 us -> 6.96 us  [shards(): swapped = jnp.stack([-every[:, :, 1], every[:, :, 0]], axis=2)]
    all_gather x1, local copies, waits for them, and re-layouts: 7.02 us -> 3.21 us  [shards(): every = lax.all_gather(own, 'chan', axis=0)]
    all_to_all x4 -> x1, local copies, waits for them, and re-layouts: 4.15 us -> 1.12 us  [shards(): own = lax.all_to_all(spectra, 'tm', split_axis=0, concat_axis=0, tiled=True)]
  transfers between devices with their start and end apart: 2 -> 2, of which waited for: 1 -> 1; matrix products, arithmetic and copies ran while one was open for 7% -> 6% of each run, Pallas kernels for 0% -> 0%
where the time goes in v5:
time: 143 us; the launch traced here: 141 us
  local copies, waits for them, and re-layouts  57.4 us (40%)
  waiting for transfers between devices  25.9 us (18%)
  other arithmetic  13.8 us (10%)
  between operations  13.5 us (9%)
  matrix products  13.3 us (9%)
  blocking collectives  8.78 us (6%)
  starting transfers between devices  4.83 us (3%)
  Pallas kernels  4 us (3%)
    all_gather x1, waiting for transfers between devices, shards(): every = lax.all_gather(own, 'chan', axis=0)  25.9 us
    reshape x2, local copies, waits for them, and re-layouts, shards(): every = every.reshape(every.shape[:2] + (2, bins // parts, channels, -1))  20.9 us
    all_to_all x1, blocking collectives, shards(): own = lax.all_to_all(spectra, 'tm', split_axis=0, concat_axis=0, tiled=True)  8.78 us
    dot_general x1, matrix products, shards(): jnp.einsum('upkis,Jupkjs->kiJj', own, swapped, preferred_element_type=jnp...  8.3 us
    dot_general x1, local copies, waits for them, and re-layouts, shards(): jnp.einsum('upkis,Jupkjs->kiJj', own, every, preferred_element_type=jnp.f...  7.78 us
    dot_general x1, local copies, waits for them, and re-layouts, shards(): jnp.einsum('upkis,Jupkjs->kiJj', own, swapped, preferred_element_type=jnp...  7.77 us
    another operation x2, local copies, waits for them, and re-layouts, shards(): result = jnp.stack([real_part, imag_part], axis=0)  7.56 us
    neg x1, other arithmetic, shards(): swapped = jnp.stack([-every[:, :, 1], every[:, :, 0]], axis=2)  6.96 us
  transfers between devices with their start and end apart: 2, of which 1 were waited for; matrix products, arithmetic and copies ran while one was open for 6% of the time, Pallas kernels for 0%

profile of v5, /device:TPU:0, one launch (start us, length us, event | category | flops | bytes accessed | tf_op | source)
XLA Modules:
  0.0 141.5 jit_solution(3814722075751402275)
XLA Ops:
  6.5 0.7 slice.12
  7.3 4.8 %collective-permute-start = (bf16[32,256]{1,0:T(8,128)(2,1)S(1)}, bf16[32,256]{1,0:T(8,128)(2,1)S(1)}, u32[]{:S(2)}, u32[]{:S(2)}) collective-permute-start(bf16[32,256]{1,0:T(8,128)(2,1)S(1)} %slice.12), channel_id=1, source_target_pairs={{0,8},{8,16},{16,24},{1,9},{9,17},{17,25},{2,10},{10,18},{18,26},{... | collective-permute-start | bytes 49160 | tf_op jit(solution)/shard_map/ppermute | solution.py:16
  12.2 2.5 %multiply_convert_fusion.1 = (bf16[512,1,4,64]{0,3,1,2:T(8,128)(2,1)S(1)}, bf16[512,1,4,64]{0,3,1,2:T(8,128)(2,1)S(1)}) fusion(s32[4,64]{1,0:T(4,128)S(1)} %multiply_add_fusion, f32[512]{0:T(512)S(1)} %get-tuple-element.9, f32[512]{0:T(512)S(1)} %get-tuple-element.10), kind=kLoop, calls=%fused_computation.17 | loop fusion | flops 2359296 | bytes 529408 | tf_op jit(solution)/shard_map/convert
  14.7 1.0 slice.13
  15.7 1.7 %copy.42 = bf16[4,8,16,256]{3,2,1,0:T(8,128)(2,1)} copy(bf16[4,8,16,256]{3,1,2,0:T(8,128)(2,1)} %bitcast.35) | data formatting | bytes 524288
  17.4 0.8 copy.41
  18.1 4.0 %shard_map.28 = bf16[32,16,256]{2,1,0:T(8,128)(2,1)} custom-call(bf16[32,256]{1,0:T(8,128)(2,1)} %taps_ref.1, bf16[32,16,256]{2,1,0:T(8,128)(2,1)} %bitcast.34, bf16[32,16,256]{2,1,0:T(8,128)(2,1)} %bitcast.33), custom_call_target="tpu_custom_call" | custom-call | flops 134217728 | bytes 802816 | tf_op jit(solution)/shard_map/pallas_call | solution.py:80
  22.1 1.0 reshape_reshape.3
  23.5 8.8 %all_to_all.5 = bf16[4,128,256]{2,1,0:T(8,128)(2,1)} all-to-all(bf16[4,128,256]{2,1,0:T(8,128)(2,1)S(1)} %bitcast.37), channel_id=1, replica_groups=mesh['tm'=4,'chan'=8] {'tm'}, dimensions={0} | all-to-all | bytes 524288 | tf_op jit(solution)/shard_map/all_to_all | solution.py:111
  32.3 1.1 copy.22
  33.7 1.7 %copy.33 = bf16[4,2,64,32,8,1]{3,4,0,1,5,2:T(8,128)(2,1)S(1)} copy(bf16[4,2,64,32,8,1]{2,1,4,3,0,5:T(2,128)(2,1)S(1)} %bitcast.31) | data formatting | bytes 524288 | tf_op jit(solution)/shard_map/reshape | solution.py:113
  35.4 25.9 %all-gather.3.cloned.1.call-done = bf16[32,128,256]{2,1,0:T(8,128)(2,1)} async-done(((bf16[4,128,256]{2,1,0:T(8,128)(2,1)}), bf16[32,128,256]{2,1,0:T(8,128)(2,1)}) %all-gather.3.cloned.1.call-update) | async-done | bytes 2097168 | tf_op jit(solution)/shard_map/all_gather | solution.py:112
  61.3 3.2 %copy.23 = bf16[32,128,256]{1,2,0:T(8,128)(2,1)S(1)} copy(bf16[32,128,256]{2,1,0:T(8,128)(2,1)} %all-gather.3.cloned.1.call-done) | data formatting | bytes 4194304 | tf_op jit(solution)/shard_map/all_gather | solution.py:112
  64.5 3.3 %reshape.139 = bf16[8,4,2,64,32,8]{3,2,5,4,1,0:T(2,128)(2,1)} reshape(bf16[32,128,256]{1,2,0:T(8,128)(2,1)S(1)} %copy.23) | data formatting | bytes 4194304 | tf_op jit(solution)/shard_map/reshape | solution.py:114
  67.8 17.7 %copy.25 = bf16[8,4,2,64,32,8]{4,5,1,2,0,3:T(8,128)(2,1)} copy(bf16[8,4,2,64,32,8]{3,2,5,4,1,0:T(2,128)(2,1)} %reshape.139) | data formatting | bytes 4194304 | tf_op jit(solution)/shard_map/reshape | solution.py:114
  85.5 7.0 %slice_negate_fusion = (bf16[8,4,1,64,32,8]{4,5,1,2,0,3:T(8,128)(2,1)}, bf16[8,4,1,64,32,8]{4,5,1,2,0,3:T(8,128)(2,1)}) fusion(bf16[8,4,2,64,32,8]{4,5,1,2,0,3:T(8,128)(2,1)} %copy.25), kind=kLoop, calls=%fused_computation.4 | loop fusion | flops 524288 | bytes 4194304 | tf_op jit(solution)/shard_map/neg | solution.py:115
  92.4 1.9 %copy-done = bf16[8,4,2,64,32,8]{4,5,1,2,0,3:T(8,128)(2,1)S(1)} copy-done((bf16[8,4,2,64,32,8]{4,5,1,2,0,3:T(8,128)(2,1)S(1)}, bf16[8,4,2,64,32,8]{4,5,1,2,0,3:T(8,128)(2,1)}, u32[]{:S(2)}) %copy-start) | copy-done | bytes 2097176
  94.3 4.7 %convolution_bitcast_fusion = f32[64,32,8,32]{3,1,2,0:T(8,128)} fusion(bf16[4,2,64,32,8,1]{3,4,0,1,5,2:T(8,128)(2,1)S(1)} %copy.33, bf16[8,4,2,64,32,8]{4,5,1,2,0,3:T(8,128)(2,1)S(1)} %copy-done), kind=kOutput, calls=%fused_computation.7 | convolution fusion | flops 67108864 | bytes 4456448 | tf_op jit(solution)/shard_map/upkis,Jupkjs->kiJj/dot_general | solution.py:116
  98.9 7.8 %copy.26 = f32[64,32,8,32]{0,3,2,1:T(8,128)} copy(f32[64,32,8,32]{3,1,2,0:T(8,128)} %convolution_bitcast_fusion) | data formatting | bytes 4194304 | tf_op jit(solution)/shard_map/upkis,Jupkjs->kiJj/dot_general | solution.py:116
  106.7 3.4 %copy.31 = f32[1,64,32,256]{3,2,1,0:T(8,128)S(1)} copy(f32[1,64,32,256]{1,3,2,0:T(8,128)} %bitcast.29) | data formatting | bytes 4194304 | tf_op jit(solution)/shard_map/stack | solution.py:118
  110.1 8.3 %fusion.4 = f32[64,32,8,32]{3,1,2,0:T(8,128)} fusion(bf16[4,2,64,32,8,1]{3,4,0,1,5,2:T(8,128)(2,1)S(1)} %copy.33, bf16[8,4,1,64,32,8]{4,5,1,2,0,3:T(8,128)(2,1)} %get-tuple-element.6, bf16[8,4,1,64,32,8]{4,5,1,2,0,3:T(8,128)(2,1)} %get-tuple-element.5), kind=kOutput, calls=%fused_computation.6 | convolution fusion | flops 71303168 | bytes 4456448 | tf_op jit(solution)/shard_map/upkis,Jupkjs->kiJj/dot_general | solution.py:117
  118.4 7.8 %copy.30 = f32[64,32,8,32]{0,3,2,1:T(8,128)} copy(f32[64,32,8,32]{3,1,2,0:T(8,128)} %fusion.4) | data formatting | bytes 4194304 | tf_op jit(solution)/shard_map/upkis,Jupkjs->kiJj/dot_general | solution.py:117
  126.2 4.2 %copy.32 = f32[1,64,32,256]{3,2,1,0:T(8,128)} copy(f32[1,64,32,256]{1,3,2,0:T(8,128)} %bitcast.30) | data formatting | bytes 4194304 | tf_op jit(solution)/shard_map/stack | solution.py:118
  130.4 4.2 %maximum_multiply_fusion = f32[2,64,32,256]{3,2,1,0:T(8,128)} fusion(f32[1,64,32,256]{3,2,1,0:T(8,128)} %copy.32, f32[1,64,32,256]{3,2,1,0:T(8,128)S(1)} %copy.31), kind=kLoop, calls=%fused_computation.5 | loop fusion | flops 2097152 | bytes 8388608 | tf_op jit(solution)/shard_map/mul | solution.py:121
  (10 shorter events, 0.7 us)
Async XLA Ops:
  6.5 54.7 %all-gather.3.cloned.1.call-start = ((), (), s32[]{:S(2)}) async-start(), calls=%async_computation.1 | async-start | bytes 2359296 | tf_op jit(solution)/shard_map/all_gather | solution.py:112
  7.3 10.1 %collective-permute-start = (bf16[32,256]{1,0:T(8,128)(2,1)S(1)}, bf16[32,256]{1,0:T(8,128)(2,1)S(1)}, u32[]{:S(2)}, u32[]{:S(2)}) collective-permute-start(bf16[32,256]{1,0:T(8,128)(2,1)S(1)} %slice.12), channel_id=1, source_target_pairs={{0,8},{8,16},{16,24},{1,9},{9,17},{17,25},{2,10},{10,18},{18,26},{... | collective-permute-start | bytes 49160 | tf_op jit(solution)/shard_map/ppermute | solution.py:16
  85.5 8.8 %copy-start = (bf16[8,4,2,64,32,8]{4,5,1,2,0,3:T(8,128)(2,1)S(1)}, bf16[8,4,2,64,32,8]{4,5,1,2,0,3:T(8,128)(2,1)}, u32[]{:S(2)}) copy-start(bf16[8,4,2,64,32,8]{4,5,1,2,0,3:T(8,128)(2,1)} %copy.25) | copy-start | bytes 6291460
Sparse Core Ops, SparseCore 0:
  32.4 28.8 all-gather.2

commit v6 on v5

--- a/solution.py
+++ b/solution.py
@@ -109,16 +109,58 @@
     ).astype(jnp.bfloat16)
     spectra = spectra.reshape(parts, spectra.shape[0] // parts, spectra.shape[1])
     own = lax.all_to_all(spectra, "tm", split_axis=0, concat_axis=0, tiled=True)
-    every = lax.all_gather(own, "chan", axis=0)
-    own = own.reshape(parts, 2, bins // parts, channels, -1)
-    every = every.reshape(every.shape[:2] + (2, bins // parts, channels, -1))
-    swapped = jnp.stack([-every[:, :, 1], every[:, :, 0]], axis=2)
-    real_part = jnp.einsum("upkis,Jupkjs->kiJj", own, every, preferred_element_type=jnp.float32)
-    imag_part = jnp.einsum("upkis,Jupkjs->kiJj", own, swapped, preferred_element_type=jnp.float32)
-    result = jnp.stack([real_part, imag_part], axis=0)
-    result = result.reshape(result.shape[:3] + (-1,))
-    factor = 1.0 / (parts * own.shape[-1] * SEG)
-    return result * factor
+    pairs = bins // parts // 2
+    shard = own.reshape(parts, 2, pairs, 2, channels, -1).transpose(2, 4, 3, 1, 0, 5)
+    shard = shard.reshape(pairs, channels, -1)
+    every = lax.all_gather(shard, "chan", axis=0)
+    return cross_spectra(lhs_rows(shard), every)
+
+
+def lhs_rows(shard):
+    pairs, channels, lanes = shard.shape
+    split = shard.reshape(pairs, channels, 2, 2, lanes // 4)
+    parity = lax.broadcasted_iota(jnp.int32, split.shape, 2)
+    zero = jnp.zeros_like(split)
+    swapped = jnp.concatenate([split[:, :, :, 1:], -split[:, :, :, :1]], axis=3)
+    rows = []
+    for part in (split, swapped):
+        for b in range(2):
+            rows.append(jnp.where(parity == b, part, zero).reshape(pairs, channels, lanes))
+    return jnp.stack(rows, axis=1).reshape(pairs, 4 * channels, lanes)
+
+
+def cross_kernel(lhs_ref, every_ref, out_ref):
+    sources, count, channels, lanes = every_ref.shape
+    factor = 1.0 / (lanes // 4 * SEG)
+    for t in range(count):
+        rhs = every_ref[:, t].reshape(sources * channels, lanes)
+        prod = lax.dot_general(
+            lhs_ref[t], rhs, (((1,), (1,)), ((), ())), preferred_element_type=jnp.float32
+        )
+        prod = prod * factor
+        for q in range(4):
+            out_ref[q // 2, 2 * t + q % 2] = prod[q * channels:(q + 1) * channels]
+
+
+def cross_spectra(lhs, every):
+    sources, pairs, channels, lanes = every.shape
+    step = 8 if pairs % 8 == 0 else pairs
+    wide = sources * channels
+    return pl.pallas_call(
+        cross_kernel,
+        out_shape=jax.ShapeDtypeStruct((2, 2 * pairs, channels, wide), jnp.float32),
+        grid=(pairs // step,),
+        in_specs=[
+            pl.BlockSpec((step, 4 * channels, lanes), lambda g: (g, 0, 0)),
+            pl.BlockSpec((sources, step, channels, lanes), lambda g: (0, g, 0, 0)),
+        ],
+        out_specs=pl.BlockSpec((2, 2 * step, channels, wide), lambda g: (0, g, 0, 0)),
+        cost_estimate=pl.CostEstimate(
+            flops=2 * pairs * 4 * channels * lanes * wide,
+            bytes_accessed=lhs.size * 2 + every.size * 2 + 2 * 2 * pairs * channels * wide * 4,
+            transcendentals=0,
+        ),
+    )(lhs, every)
 
 
 def solution(mesh):

time: 143 us -> 83.8 us (0.59)
  local copies, waits for them, and re-layouts: 57.4 us -> 19.9 us
  matrix products: 13.3 us -> 0.33 us
  other arithmetic: 13.8 us -> 5.75 us
  Pallas kernels: 4 us -> 8.89 us
  waiting for transfers between devices: 25.9 us -> 21.6 us
    reshape x4 -> x1, local copies, waits for them, and re-layouts: 22.9 us -> 5.86 us  [shards(): own.reshape(parts, 2, pairs, 2, channels, -1).transpose(2, 4, 3, 1, 0, 5)]
    dot_general x2 -> x0, local copies, waits for them, and re-layouts: 15.5 us -> none  [the longest x1 7.78 us: shards(): jnp.einsum('upkis,Jupkjs->kiJj', own, every, preferred_element_type=jnp.f...]
    dot_general x2 -> x0, matrix products: 13 us -> none  [the longest x1 8.3 us: shards(): jnp.einsum('upkis,Jupkjs->kiJj', own, swapped, preferred_element_type=jnp...]
    neg x1 -> x0, other arithmetic: 6.96 us -> none  [shards(): swapped = jnp.stack([-every[:, :, 1], every[:, :, 0]], axis=2)]
    another operation x2 -> x1, local copies, waits for them, and re-layouts: 7.56 us -> 1.03 us  [shards(): every = lax.all_gather(shard, 'chan', axis=0)]
    pallas_call x0 -> x1, Pallas kernels: none -> 4.9 us  [cross_spectra(): pl.pallas_call(cross_kernel, out_shape=jax.ShapeDtypeStruct((2, 2 * pairs...]
    all_gather x1, waiting for transfers between devices: 25.9 us -> 21.6 us  [shards(): every = lax.all_gather(shard, 'chan', axis=0)]
    mul x1 -> x0, other arithmetic: 4.24 us -> none  [shards(): return result * factor]
  transfers between devices with their start and end apart: 2 -> 2, of which waited for: 1 -> 1; matrix products, arithmetic and copies ran while one was open for 6% -> 15% of each run, Pallas kernels for 0% -> 0%
where the time goes in v6:
time: 83.8 us; the launch traced here: 83.2 us
  waiting for transfers between devices  21.6 us (26%)
  local copies, waits for them, and re-layouts  19.9 us (24%)
  between operations  13.5 us (16%)
  Pallas kernels  8.89 us (11%)
  blocking collectives  8.32 us (10%)
  other arithmetic  5.75 us (7%)
  starting transfers between devices  4.83 us (6%)
    all_gather x1, waiting for transfers between devices, shards(): every = lax.all_gather(shard, 'chan', axis=0)  21.6 us
    all_to_all x1, blocking collectives, shards(): own = lax.all_to_all(spectra, 'tm', split_axis=0, concat_axis=0, tiled=True)  8.32 us
    reshape x1, local copies, waits for them, and re-layouts, shards(): own.reshape(parts, 2, pairs, 2, channels, -1).transpose(2, 4, 3, 1, 0, 5)  5.86 us
    pallas_call x1, Pallas kernels, cross_spectra(): pl.pallas_call(cross_kernel, out_shape=jax.ShapeDtypeStruct((2, 2 * pairs...  4.9 us
    ppermute x1, starting transfers between devices, shifted(): return lax.ppermute(value, axis, pairs)  4.83 us
    pallas_call x1, Pallas kernels, whiten(): pl.pallas_call(fir_kernel, out_shape=jax.ShapeDtypeStruct(late.shape, jnp...  4 us
    select_n x4, local copies, waits for them, and re-layouts, lhs_rows(): jnp.where(parity == b, part, zero).reshape(pairs, channels, lanes)  3.83 us
    transpose x1, local copies, waits for them, and re-layouts, shards(): own.reshape(parts, 2, pairs, 2, channels, -1).transpose(2, 4, 3, 1, 0, 5)  3.69 us
  transfers between devices with their start and end apart: 2, of which 1 were waited for; matrix products, arithmetic and copies ran while one was open for 15% of the time, Pallas kernels for 0%

profile of v6, /device:TPU:0, one launch (start us, length us, event | category | flops | bytes accessed | tf_op | source)
XLA Modules:
  0.0 83.2 jit_solution(5423091737690631329)
XLA Ops:
  6.5 0.7 slice.12
  7.3 4.8 %collective-permute-start = (bf16[32,256]{1,0:T(8,128)(2,1)S(1)}, bf16[32,256]{1,0:T(8,128)(2,1)S(1)}, u32[]{:S(2)}, u32[]{:S(2)}) collective-permute-start(bf16[32,256]{1,0:T(8,128)(2,1)S(1)} %slice.12), channel_id=1, source_target_pairs={{0,8},{8,16},{16,24},{1,9},{9,17},{17,25},{2,10},{10,18},{18,26},{... | collective-permute-start | bytes 49160 | tf_op jit(solution)/shard_map/ppermute | solution.py:16
  12.2 2.5 %multiply_convert_fusion.1 = (bf16[512,1,4,64]{0,3,1,2:T(8,128)(2,1)S(1)}, bf16[512,1,4,64]{0,3,1,2:T(8,128)(2,1)S(1)}) fusion(s32[4,64]{1,0:T(4,128)S(1)} %multiply_add_fusion, f32[512]{0:T(512)S(1)} %get-tuple-element.15, f32[512]{0:T(512)S(1)} %get-tuple-element.16), kind=kLoop, calls=%fused_computation.16 | loop fusion | flops 2359296 | bytes 529408 | tf_op jit(solution)/shard_map/convert
  14.7 1.0 %slice.13 = bf16[32,3840]{1,0:T(8,128)(2,1)S(1)} slice(bf16[32,4096]{1,0:T(8,128)(2,1)} %param.2), slice={[0:32], [0:3840]} | slice | bytes 491520 | tf_op jit(solution)/shard_map/slice | solution.py:98
  15.7 1.7 %copy.19 = bf16[4,8,16,256]{3,2,1,0:T(8,128)(2,1)} copy(bf16[4,8,16,256]{3,1,2,0:T(8,128)(2,1)} %bitcast.25) | data formatting | bytes 524288
  17.4 0.8 copy.18
  18.1 4.0 %shard_map.28 = bf16[32,16,256]{2,1,0:T(8,128)(2,1)} custom-call(bf16[32,256]{1,0:T(8,128)(2,1)} %taps_ref.1, bf16[32,16,256]{2,1,0:T(8,128)(2,1)} %bitcast.24, bf16[32,16,256]{2,1,0:T(8,128)(2,1)} %bitcast.23), custom_call_target="tpu_custom_call" | custom-call | flops 134217728 | bytes 802816 | tf_op jit(solution)/shard_map/pallas_call | solution.py:80
  22.1 1.0 %reshape_reshape.8 = bf16[256,512]{1,0:T(8,128)(2,1)S(1)} reshape(bf16[32,16,256]{2,1,0:T(8,128)(2,1)} %shard_map.28) | data formatting | bytes 524288 | tf_op jit(solution)/shard_map/reshape;reshape | solution.py:102
  23.2 0.3 convolution_convert_fusion
  23.5 8.3 %all_to_all.5 = bf16[4,128,256]{2,1,0:T(8,128)(2,1)S(1)} all-to-all(bf16[4,128,256]{2,1,0:T(8,128)(2,1)S(1)} %bitcast.27), channel_id=1, replica_groups=mesh['tm'=4,'chan'=8] {'tm'}, dimensions={0} | all-to-all | bytes 524288 | tf_op jit(solution)/shard_map/all_to_all | solution.py:111
  31.8 5.9 %reshape.177 = bf16[4,2,32,2,32,8]{5,4,3,2,1,0:T(8,128)(2,1)} reshape(bf16[4,128,256]{2,1,0:T(8,128)(2,1)S(1)} %all_to_all.5) | data formatting | bytes 524288 | tf_op jit(solution)/shard_map/reshape | solution.py:113
  37.7 3.7 %copy.10 = bf16[32,32,2,2,4,8]{1,5,4,3,2,0:T(8,128)(2,1)S(1)} copy(bf16[32,32,2,2,4,8]{5,1,2,0,3,4:T(8,128)(2,1)} %bitcast.16) | data formatting | bytes 524288 | tf_op jit(solution)/shard_map/transpose | solution.py:113
  41.4 1.0 %copy.17 = bf16[1,32,32,128]{3,2,1,0:T(8,128)(2,1)} copy(bf16[1,32,32,128]{2,3,1,0:T(8,128)(2,1)S(1)} %bitcast.17) | data formatting | bytes 524288 | tf_op jit(solution)/shard_map/all_gather;reshape | solution.py:115
  42.5 0.1 iota.70
  42.8 0.1 fusion.7
  42.9 0.2 pad_maximum_fusion
  43.1 1.7 %broadcast_select_fusion.2 = (bf16[32,1,32,128]{2,3,0,1:T(8,128)(2,1)S(1)}, bf16[32,1,32,128]{2,3,0,1:T(8,128)(2,1)S(1)}, bf16[32,1,32,128]{2,3,0,1:T(8,128)(2,1)}, bf16[32,1,32,128]{2,3,0,1:T(8,128)(2,1)}) fusion(bf16[32,1,32,128]{2,3,0,1:T(8,128)(2,1)S(1)} %bitcast.21, pred[128]{0:T(512)(128)(4,1)S(1)} %iota.70, pred[128]{0:T(512)(128)(4,1)S(1)} %iota.75, ...), kind=kLoop, calls=%fused_computation.5 | loop fusion | flops 524288 | bytes 1573120 | tf_op jit(solution)/shard_map/jit(_where)/select_n | solution.py:128
  44.8 1.6 %copy.12 = bf16[32,1,32,128]{3,2,1,0:T(8,128)(2,1)S(1)} copy(bf16[32,1,32,128]{2,3,0,1:T(8,128)(2,1)} %get-tuple-element.14) | data formatting | bytes 524288 | tf_op jit(solution)/shard_map/jit(_where)/select_n | solution.py:128
  46.4 1.6 %copy.13 = bf16[32,1,32,128]{3,2,1,0:T(8,128)(2,1)S(1)} copy(bf16[32,1,32,128]{2,3,0,1:T(8,128)(2,1)} %get-tuple-element.13) | data formatting | bytes 524288 | tf_op jit(solution)/shard_map/jit(_where)/select_n | solution.py:128
  48.0 0.3 copy.14
  48.3 0.3 copy.15
  48.7 1.1 %pad_maximum_fusion.1 = bf16[32,4,32,128]{3,2,1,0:T(8,128)(2,1)} fusion(bf16[32,1,32,128]{3,2,1,0:T(8,128)(2,1)S(1)} %copy.15, bf16[32,1,32,128]{3,2,1,0:T(8,128)(2,1)S(1)} %copy.14, bf16[32,1,32,128]{3,2,1,0:T(8,128)(2,1)S(1)} %copy.13, bf16[32,1,32,128]{3,2,1,0:T(8,128)(2,1)S(1)} %copy.12), kind=kLoop, calls=%fused_computation.2 | loop fusion | flops 1572864 | bytes 2097152 | tf_op jit(solution)/shard_map/stack | solution.py:129
  49.8 21.6 %all-gather.2.cloned.1.call-done.every_ref = bf16[8,32,32,128]{3,2,1,0:T(8,128)(2,1)} async-done(((bf16[1,32,32,128]{3,2,1,0:T(8,128)(2,1)}), bf16[8,32,32,128]{3,2,1,0:T(8,128)(2,1)}) %all-gather.2.cloned.1.call-update) | async-done | bytes 2097168 | tf_op jit(solution)/shard_map/all_gather | solution.py:115
  71.4 4.9 %shard_map.29 = f32[2,64,32,256]{3,2,1,0:T(8,128)} custom-call(bf16[32,128,128]{2,1,0:T(8,128)(2,1)} %bitcast.20, bf16[8,32,32,128]{3,2,1,0:T(8,128)(2,1)} %all-gather.2.cloned.1.call-done.every_ref), custom_call_target="tpu_custom_call" | custom-call | flops 268435456 | bytes 7340032 | tf_op jit(solution)/shard_map/pallas_call | solution.py:149
  (12 shorter events, 0.4 us)
Async XLA Ops:
  6.5 64.9 %all-gather.2.cloned.1.call-start = ((), (), s32[]{:S(2)}) async-start(), calls=%async_computation.1 | async-start | bytes 2359296 | tf_op jit(solution)/shard_map/all_gather | solution.py:115
  7.3 10.1 %collective-permute-start = (bf16[32,256]{1,0:T(8,128)(2,1)S(1)}, bf16[32,256]{1,0:T(8,128)(2,1)S(1)}, u32[]{:S(2)}, u32[]{:S(2)}) collective-permute-start(bf16[32,256]{1,0:T(8,128)(2,1)S(1)} %slice.12), channel_id=1, source_target_pairs={{0,8},{8,16},{16,24},{1,9},{9,17},{17,25},{2,10},{10,18},{18,26},{... | collective-permute-start | bytes 49160 | tf_op jit(solution)/shard_map/ppermute | solution.py:16
Sparse Core Ops, SparseCore 0:
  42.6 28.8 all-gather.1

commit v7 on v6

--- a/solution.py
+++ b/solution.py
@@ -1,11 +1,13 @@
 import math
 
 import jax
+import ml_dtypes
+import numpy as np
 import jax.numpy as jnp
 from jax import lax
 from jax.experimental import pallas as pl
 from jax.experimental.pallas import tpu as pltpu
-from jax.sharding import PartitionSpec as P
+from jax.sharding import Mesh, PartitionSpec as P
 
 SEG = 512
 
@@ -17,14 +19,15 @@
 
 
 def make_table():
-    sample_idx = jnp.arange(SEG, dtype=jnp.int32)
-    bin_idx = jnp.arange(SEG // 2, dtype=jnp.int32)
+    sample_idx = np.arange(SEG, dtype=np.int32)
+    bin_idx = np.arange(SEG // 2, dtype=np.int32)
     phases = sample_idx[:, None] * bin_idx[None, :] % SEG
-    angles = phases.astype(jnp.float32) * (2.0 * math.pi / SEG)
-    window = 0.5 - 0.5 * jnp.cos(sample_idx.astype(jnp.float32) * (2.0 * math.pi / SEG))
-    cosine = window[:, None] * jnp.cos(angles)
-    sine_part = -window[:, None] * jnp.sin(angles)
-    return jnp.stack([cosine, sine_part], axis=1).astype(jnp.bfloat16)
+    step = np.float32(2.0 * math.pi / SEG)
+    angles = phases.astype(np.float32) * step
+    window = np.float32(0.5) - np.float32(0.5) * np.cos(sample_idx.astype(np.float32) * step)
+    cosine = window[:, None] * np.cos(angles)
+    sine_part = -window[:, None] * np.sin(angles)
+    return np.stack([cosine, sine_part], axis=1).astype(ml_dtypes.bfloat16)
 
 
 def toeplitz(fir_taps):
@@ -103,7 +106,9 @@
     parts = lax.axis_size("tm")
     table = make_table()
     bins = table.shape[2]
-    table = table.reshape(SEG, 2, parts, bins // parts).transpose(0, 2, 1, 3).reshape(SEG, 2 * bins)
+    table = jnp.asarray(
+        table.reshape(SEG, 2, parts, bins // parts).transpose(0, 2, 1, 3).reshape(SEG, 2 * bins)
+    )
     spectra = jnp.einsum(
         "xn,nq->qx", segments, table, preferred_element_type=jnp.float32
     ).astype(jnp.bfloat16)
@@ -112,7 +117,9 @@
     pairs = bins // parts // 2
     shard = own.reshape(parts, 2, pairs, 2, channels, -1).transpose(2, 4, 3, 1, 0, 5)
     shard = shard.reshape(pairs, channels, -1)
-    every = lax.all_gather(shard, "chan", axis=0)
+    every = lax.all_gather(shard, "chip", axis=0)
+    every = lax.all_gather(every, "core", axis=1)
+    every = every.reshape((-1,) + shard.shape)
     return cross_spectra(lhs_rows(shard), every)
 
 
@@ -164,7 +171,10 @@
 
 
 def solution(mesh):
-    placed = (P("chan", "tm"), P("chan", None))
+    tm_size, chan_size = mesh.devices.shape
+    split = Mesh(mesh.devices.reshape(tm_size, chan_size // 2, 2), ("tm", "chip", "core"))
+    chan = ("chip", "core")
+    placed = (P(chan, "tm"), P(chan, None))
     return jax.shard_map(
-        shards, mesh=mesh, in_specs=placed, out_specs=P(None, "tm", "chan", None), check_vma=False
+        shards, mesh=split, in_specs=placed, out_specs=P(None, "tm", chan, None), check_vma=False
     )

time: 83.8 us -> 93.4 us (1.11)
  waiting for transfers between devices: 21.6 us -> 32.1 us
  other arithmetic: 5.75 us -> 3.16 us
  matrix products: 0.33 us -> 1.34 us
    all_gather x1 -> x2, waiting for transfers between devices: 21.6 us -> 32 us  [the longest x1 27.8 us: shards(): every = lax.all_gather(shard, 'chip', axis=0)]
    another operation x2 -> x0, other arithmetic: 2.53 us -> none
    dot_general x1, matrix products: 0.33 us -> 1.34 us  [shards(): jnp.einsum('xn,nq->qx', segments, table, preferred_element_type=jnp.float32)]
  transfers between devices with their start and end apart: 2 -> 3, of which waited for: 1 -> 2; matrix products, arithmetic and copies ran while one was open for 15% -> 11% of each run, Pallas kernels for 0% -> 0%
where the time goes in v7:
time: 93.4 us; the launch traced here: 92.7 us
  waiting for transfers between devices  32.1 us (34%)
  local copies, waits for them, and re-layouts  20 us (21%)
  between operations  13.5 us (14%)
  Pallas kernels  8.89 us (10%)
  blocking collectives  8.81 us (9%)
  starting transfers between devices  4.88 us (5%)
  other arithmetic  3.16 us (3%)
  matrix products  1.34 us (1%)
    all_gather x1, waiting for transfers between devices, shards(): every = lax.all_gather(shard, 'chip', axis=0)  27.8 us
    all_to_all x1, blocking collectives, shards(): own = lax.all_to_all(spectra, 'tm', split_axis=0, concat_axis=0, tiled=True)  8.81 us
    reshape x1, local copies, waits for them, and re-layouts, shards(): own.reshape(parts, 2, pairs, 2, channels, -1).transpose(2, 4, 3, 1, 0, 5)  5.86 us
    pallas_call x1, Pallas kernels, cross_spectra(): pl.pallas_call(cross_kernel, out_shape=jax.ShapeDtypeStruct((2, 2 * pairs...  4.87 us
    ppermute x1, starting transfers between devices, shifted(): return lax.ppermute(value, axis, pairs)  4.83 us
    all_gather x1, waiting for transfers between devices, shards(): every = lax.all_gather(every, 'core', axis=1)  4.29 us
    pallas_call x1, Pallas kernels, whiten(): pl.pallas_call(fir_kernel, out_shape=jax.ShapeDtypeStruct(late.shape, jnp...  4.01 us
    select_n x4, local copies, waits for them, and re-layouts, lhs_rows(): jnp.where(parity == b, part, zero).reshape(pairs, channels, lanes)  3.83 us
  transfers between devices with their start and end apart: 3, of which 2 were waited for; matrix products, arithmetic and copies ran while one was open for 11% of the time, Pallas kernels for 0%

profile of v7, /device:TPU:0, one launch (start us, length us, event | category | flops | bytes accessed | tf_op | source)
XLA Modules:
  0.0 92.7 jit_solution(11094018324468291366)
XLA Ops:
  6.5 0.7 slice.12
  7.3 4.8 %collective-permute-start = (bf16[32,256]{1,0:T(8,128)(2,1)S(1)}, bf16[32,256]{1,0:T(8,128)(2,1)S(1)}, u32[]{:S(2)}, u32[]{:S(2)}) collective-permute-start(bf16[32,256]{1,0:T(8,128)(2,1)S(1)} %slice.12), channel_id=1, source_target_pairs={{0,8},{8,16},{16,24},{1,9},{9,17},{17,25},{2,10},{10,18},{18,26},{... | collective-permute-start | bytes 49160 | tf_op jit(solution)/shard_map/ppermute | solution.py:18
  12.1 1.0 %slice.13 = bf16[32,3840]{1,0:T(8,128)(2,1)S(1)} slice(bf16[32,4096]{1,0:T(8,128)(2,1)} %param.3), slice={[0:32], [0:3840]} | slice | bytes 491520 | tf_op jit(solution)/shard_map/slice | solution.py:101
  13.1 1.7 %copy.22 = bf16[4,8,16,256]{3,2,1,0:T(8,128)(2,1)} copy(bf16[4,8,16,256]{3,1,2,0:T(8,128)(2,1)} %bitcast.25) | data formatting | bytes 524288
  14.8 0.8 copy.21
  15.5 4.0 %shard_map.37 = bf16[32,16,256]{2,1,0:T(8,128)(2,1)} custom-call(bf16[32,256]{1,0:T(8,128)(2,1)} %taps_ref.1, bf16[32,16,256]{2,1,0:T(8,128)(2,1)} %bitcast.24, bf16[32,16,256]{2,1,0:T(8,128)(2,1)} %bitcast.23), custom_call_target="tpu_custom_call" | custom-call | flops 134217728 | bytes 802816 | tf_op jit(solution)/shard_map/pallas_call | solution.py:83
  19.5 1.0 %reshape_reshape.8 = bf16[256,512]{1,0:T(8,128)(2,1)S(1)} reshape(bf16[32,16,256]{2,1,0:T(8,128)(2,1)} %shard_map.37) | data formatting | bytes 524288 | tf_op jit(solution)/shard_map/reshape;reshape | solution.py:105
  20.6 1.3 %fusion = bf16[512,256]{0,1:T(8,128)(2,1)S(1)} fusion(bf16[256,512]{1,0:T(8,128)(2,1)S(1)} %reshape_reshape.8, bf16[512,512]{1,0:T(8,128)(2,1)} %constant.8.clone), kind=kOutput, calls=%fused_computation.1 | convolution fusion | flops 134348800 | bytes 1048576 | tf_op jit(solution)/shard_map/xn,nq->qx/dot_general | solution.py:112
  21.9 0.1 copy.20
  22.1 8.8 %all_to_all.5 = bf16[4,128,256]{2,1,0:T(8,128)(2,1)S(1)} all-to-all(bf16[4,128,256]{2,1,0:T(8,128)(2,1)S(1)} %bitcast.27), channel_id=1, replica_groups=mesh['tm'=4,'chip'=4,'core'=2] {'tm'}, dimensions={0} | all-to-all | bytes 524288 | tf_op jit(solution)/shard_map/all_to_all | solution.py:116
  30.9 5.9 %reshape.65 = bf16[4,2,32,2,32,8]{5,4,3,2,1,0:T(8,128)(2,1)} reshape(bf16[4,128,256]{2,1,0:T(8,128)(2,1)S(1)} %all_to_all.5) | data formatting | bytes 524288 | tf_op jit(solution)/shard_map/reshape | solution.py:118
  36.7 3.7 %copy.12 = bf16[32,32,2,2,4,8]{1,5,4,3,2,0:T(8,128)(2,1)S(1)} copy(bf16[32,32,2,2,4,8]{5,1,2,0,3,4:T(8,128)(2,1)} %bitcast.16) | data formatting | bytes 524288 | tf_op jit(solution)/shard_map/transpose | solution.py:118
  40.4 1.0 %copy.19 = bf16[1,32,32,128]{3,2,1,0:T(8,128)(2,1)} copy(bf16[1,32,32,128]{2,3,1,0:T(8,128)(2,1)S(1)} %bitcast.17) | data formatting | bytes 524288 | tf_op jit(solution)/shard_map/all_gather;reshape | solution.py:120
  41.5 27.8 %all-gather.4.cloned.1.call-done = bf16[4,32,32,128]{3,2,1,0:T(8,128)(2,1)} async-done(((bf16[1,32,32,128]{3,2,1,0:T(8,128)(2,1)}), bf16[4,32,32,128]{3,2,1,0:T(8,128)(2,1)}) %all-gather.4.cloned.1.call-update) | async-done | bytes 1048592 | tf_op jit(solution)/shard_map/all_gather | solution.py:120
  69.7 0.1 fusion.1
  69.8 0.2 pad_maximum_fusion
  70.0 1.7 %broadcast_select_fusion.2 = (bf16[32,1,32,128]{2,3,0,1:T(8,128)(2,1)S(1)}, bf16[32,1,32,128]{2,3,0,1:T(8,128)(2,1)S(1)}, bf16[32,1,32,128]{2,3,0,1:T(8,128)(2,1)}, bf16[32,1,32,128]{2,3,0,1:T(8,128)(2,1)}) fusion(bf16[32,1,32,128]{2,3,0,1:T(8,128)(2,1)S(1)} %bitcast.21, pred[128]{0:T(512)(128)(4,1)S(1)} %iota.36, pred[128]{0:T(512)(128)(4,1)S(1)} %iota.40, ...), kind=kLoop, calls=%fused_computation.6 | loop fusion | flops 524288 | bytes 1573120 | tf_op jit(solution)/shard_map/jit(_where)/select_n | solution.py:135
  71.7 1.6 %copy.14 = bf16[32,1,32,128]{3,2,1,0:T(8,128)(2,1)S(1)} copy(bf16[32,1,32,128]{2,3,0,1:T(8,128)(2,1)} %get-tuple-element.12) | data formatting | bytes 524288 | tf_op jit(solution)/shard_map/jit(_where)/select_n | solution.py:135
  73.3 1.6 %copy.15 = bf16[32,1,32,128]{3,2,1,0:T(8,128)(2,1)S(1)} copy(bf16[32,1,32,128]{2,3,0,1:T(8,128)(2,1)} %get-tuple-element.11) | data formatting | bytes 524288 | tf_op jit(solution)/shard_map/jit(_where)/select_n | solution.py:135
  74.8 0.3 copy.16
  75.2 0.3 copy.17
  75.6 1.1 %pad_maximum_fusion.1 = bf16[32,4,32,128]{3,2,1,0:T(8,128)(2,1)} fusion(bf16[32,1,32,128]{3,2,1,0:T(8,128)(2,1)S(1)} %copy.17, bf16[32,1,32,128]{3,2,1,0:T(8,128)(2,1)S(1)} %copy.16, bf16[32,1,32,128]{3,2,1,0:T(8,128)(2,1)S(1)} %copy.15, bf16[32,1,32,128]{3,2,1,0:T(8,128)(2,1)S(1)} %copy.14), kind=kLoop, calls=%fused_computation.3 | loop fusion | flops 1572864 | bytes 2097152 | tf_op jit(solution)/shard_map/stack | solution.py:136
  76.7 4.3 %all-gather.6.cloned.1.call-done = bf16[4,64,32,128]{3,2,1,0:T(8,128)(2,1)} async-done(((bf16[4,32,32,128]{3,2,1,0:T(8,128)(2,1)}), bf16[4,64,32,128]{3,2,1,0:T(8,128)(2,1)}) %all-gather.6.cloned.1.call-update) | async-done | bytes 2097168 | tf_op jit(solution)/shard_map/all_gather | solution.py:121
  81.0 4.9 %shard_map.38 = f32[2,64,32,256]{3,2,1,0:T(8,128)} custom-call(bf16[32,128,128]{2,1,0:T(8,128)(2,1)} %bitcast.20, bf16[8,32,32,128]{3,2,1,0:T(8,128)(2,1)} %bitcast.22), custom_call_target="tpu_custom_call" | custom-call | flops 268435456 | bytes 7340032 | tf_op jit(solution)/shard_map/pallas_call | solution.py:156
  (12 shorter events, 0.4 us)
Async XLA Ops:
  6.5 62.8 %all-gather.4.cloned.1.call-start = ((), (), s32[]{:S(2)}) async-start(), calls=%async_computation.1 | async-start | bytes 1310720 | tf_op jit(solution)/shard_map/all_gather | solution.py:120
  7.3 7.5 %collective-permute-start = (bf16[32,256]{1,0:T(8,128)(2,1)S(1)}, bf16[32,256]{1,0:T(8,128)(2,1)S(1)}, u32[]{:S(2)}, u32[]{:S(2)}) collective-permute-start(bf16[32,256]{1,0:T(8,128)(2,1)S(1)} %slice.12), channel_id=1, source_target_pairs={{0,8},{8,16},{16,24},{1,9},{9,17},{17,25},{2,10},{10,18},{18,26},{... | collective-permute-start | bytes 49160 | tf_op jit(solution)/shard_map/ppermute | solution.py:18
  41.5 39.5 %all-gather.6.cloned.1.call-start = ((), (), s32[]{:S(2)}) async-start(), calls=%async_computation.2 | async-start | bytes 3145728 | tf_op jit(solution)/shard_map/all_gather | solution.py:121
Sparse Core Ops, SparseCore 0:
  41.6 27.6 all-gather.3
  70.8 10.0 all-gather.5

commit v8 on v7

--- a/solution.py
+++ b/solution.py
@@ -7,7 +7,7 @@
 from jax import lax
 from jax.experimental import pallas as pl
 from jax.experimental.pallas import tpu as pltpu
-from jax.sharding import Mesh, PartitionSpec as P
+from jax.sharding import PartitionSpec as P
 
 SEG = 512
 
@@ -115,12 +115,16 @@
     spectra = spectra.reshape(parts, spectra.shape[0] // parts, spectra.shape[1])
     own = lax.all_to_all(spectra, "tm", split_axis=0, concat_axis=0, tiled=True)
     pairs = bins // parts // 2
-    shard = own.reshape(parts, 2, pairs, 2, channels, -1).transpose(2, 4, 3, 1, 0, 5)
-    shard = shard.reshape(pairs, channels, -1)
-    every = lax.all_gather(shard, "chip", axis=0)
-    every = lax.all_gather(every, "core", axis=1)
-    every = every.reshape((-1,) + shard.shape)
-    return cross_spectra(lhs_rows(shard), every)
+    split = own.reshape(parts, 2, pairs, 2, channels, -1)
+    chunks = 2 if pairs % 16 == 0 else 1
+    size = pairs // chunks
+    result = None
+    for h in range(chunks):
+        shard = split[:, :, h * size:(h + 1) * size].transpose(2, 4, 3, 1, 0, 5)
+        shard = shard.reshape(size, channels, -1)
+        every = lax.all_gather(shard, "chan", axis=0)
+        result = cross_spectra(lhs_rows(shard), every, pairs, h * size, result)
+    return result
 
 
 def lhs_rows(shard):
@@ -149,32 +153,39 @@
             out_ref[q // 2, 2 * t + q % 2] = prod[q * channels:(q + 1) * channels]
 
 
-def cross_spectra(lhs, every):
+def cross_spectra(lhs, every, total, start, result):
     sources, pairs, channels, lanes = every.shape
     step = 8 if pairs % 8 == 0 else pairs
     wide = sources * channels
+    first = start // step
+    operands = (lhs, every) if result is None else (lhs, every, result)
+    specs = [
+        pl.BlockSpec((step, 4 * channels, lanes), lambda g: (g, 0, 0)),
+        pl.BlockSpec((sources, step, channels, lanes), lambda g: (0, g, 0, 0)),
+    ]
+    if result is not None:
+        specs.append(pl.BlockSpec(memory_space=pl.ANY))
     return pl.pallas_call(
-        cross_kernel,
-        out_shape=jax.ShapeDtypeStruct((2, 2 * pairs, channels, wide), jnp.float32),
+        cross_kernel if result is None else cross_kernel_into,
+        out_shape=jax.ShapeDtypeStruct((2, 2 * total, channels, wide), jnp.float32),
         grid=(pairs // step,),
-        in_specs=[
-            pl.BlockSpec((step, 4 * channels, lanes), lambda g: (g, 0, 0)),
-            pl.BlockSpec((sources, step, channels, lanes), lambda g: (0, g, 0, 0)),
-        ],
-        out_specs=pl.BlockSpec((2, 2 * step, channels, wide), lambda g: (0, g, 0, 0)),
+        in_specs=specs,
+        out_specs=pl.BlockSpec((2, 2 * step, channels, wide), lambda g: (0, g + first, 0, 0)),
+        input_output_aliases={} if result is None else {2: 0},
         cost_estimate=pl.CostEstimate(
             flops=2 * pairs * 4 * channels * lanes * wide,
             bytes_accessed=lhs.size * 2 + every.size * 2 + 2 * 2 * pairs * channels * wide * 4,
             transcendentals=0,
         ),
-    )(lhs, every)
+    )(*operands)
+
+
+def cross_kernel_into(lhs_ref, every_ref, result_ref, out_ref):
+    cross_kernel(lhs_ref, every_ref, out_ref)
 
 
 def solution(mesh):
-    tm_size, chan_size = mesh.devices.shape
-    split = Mesh(mesh.devices.reshape(tm_size, chan_size // 2, 2), ("tm", "chip", "core"))
-    chan = ("chip", "core")
-    placed = (P(chan, "tm"), P(chan, None))
+    placed = (P("chan", "tm"), P("chan", None))
     return jax.shard_map(
-        shards, mesh=split, in_specs=placed, out_specs=P(None, "tm", chan, None), check_vma=False
+        shards, mesh=mesh, in_specs=placed, out_specs=P(None, "tm", "chan", None), check_vma=False
     )

time: 93.4 us -> 100 us (1.071)
  local copies, waits for them, and re-layouts: 20 us -> 26.9 us
  waiting for transfers between devices: 32.1 us -> 31 us
    transpose x1 -> x3, local copies, waits for them, and re-layouts: 3.69 us -> 7.93 us  [shards(): shard = split[:, :, h * size:(h + 1) * size].transpose(2, 4, 3, 1, 0, 5)]
    select_n x4 -> x8, local copies, waits for them, and re-layouts: 3.83 us -> 5.76 us  [lhs_rows(): jnp.where(parity == b, part, zero).reshape(pairs, channels, lanes)]
    all_gather x2, waiting for transfers between devices: 32 us -> 31 us  [shards(): every = lax.all_gather(shard, 'chan', axis=0)]
    pallas_call x1 -> x2, Pallas kernels: 4.87 us -> 5.48 us  [cross_spectra(): pl.pallas_call(cross_kernel if result is None else cross_kernel_into, out...]
  transfers between devices with their start and end apart: 3 -> 3, of which waited for: 2 -> 2; matrix products, arithmetic and copies ran while one was open for 11% -> 14% of each run, Pallas kernels for 0% -> 3%
where the time goes in v8:
time: 100 us; the launch traced here: 99.5 us
  waiting for transfers between devices  31 us (31%)
  local copies, waits for them, and re-layouts  26.9 us (27%)
  between operations  13.5 us (14%)
  Pallas kernels  9.5 us (10%)
  blocking collectives  8.79 us (9%)
  starting transfers between devices  4.87 us (5%)
  other arithmetic  3.59 us (4%)
  matrix products  1.34 us (1%)
    all_gather x2, waiting for transfers between devices, shards(): every = lax.all_gather(shard, 'chan', axis=0)  31 us
    all_to_all x1, blocking collectives, shards(): own = lax.all_to_all(spectra, 'tm', split_axis=0, concat_axis=0, tiled=True)  8.79 us
    transpose x3, local copies, waits for them, and re-layouts, shards(): shard = split[:, :, h * size:(h + 1) * size].transpose(2, 4, 3, 1, 0, 5)  7.93 us
    reshape x1, local copies, waits for them, and re-layouts, shards(): split = own.reshape(parts, 2, pairs, 2, channels, -1)  5.86 us
    select_n x8, local copies, waits for them, and re-layouts, lhs_rows(): jnp.where(parity == b, part, zero).reshape(pairs, channels, lanes)  5.76 us
    pallas_call x2, Pallas kernels, cross_spectra(): pl.pallas_call(cross_kernel if result is None else cross_kernel_into, out...  5.48 us
    ppermute x1, starting transfers between devices, shifted(): return lax.ppermute(value, axis, pairs)  4.83 us
    pallas_call x1, Pallas kernels, whiten(): pl.pallas_call(fir_kernel, out_shape=jax.ShapeDtypeStruct(late.shape, jnp...  4.02 us
  transfers between devices with their start and end apart: 3, of which 2 were waited for; matrix products, arithmetic and copies ran while one was open for 14% of the time, Pallas kernels for 3%

profile of v8, /device:TPU:0, one launch (start us, length us, event | category | flops | bytes accessed | tf_op | source)
XLA Modules:
  0.0 99.5 jit_solution(1829573721821727951)
XLA Ops:
  7.3 4.8 %collective-permute-start = (bf16[32,256]{1,0:T(8,128)(2,1)S(1)}, bf16[32,256]{1,0:T(8,128)(2,1)S(1)}, u32[]{:S(2)}, u32[]{:S(2)}) collective-permute-start(bf16[32,256]{1,0:T(8,128)(2,1)S(1)} %slice.24), channel_id=1, source_target_pairs={{0,8},{8,16},{16,24},{1,9},{9,17},{17,25},{2,10},{10,18},{18,26},{... | collective-permute-start | bytes 49160 | tf_op jit(solution)/shard_map/ppermute | solution.py:18
  12.1 1.0 slice.25
  13.1 1.7 %copy.39 = bf16[4,8,16,256]{3,2,1,0:T(8,128)(2,1)} copy(bf16[4,8,16,256]{3,1,2,0:T(8,128)(2,1)} %bitcast.35) | data formatting | bytes 524288
  15.5 4.0 %shard_map.37 = bf16[32,16,256]{2,1,0:T(8,128)(2,1)} custom-call(bf16[32,256]{1,0:T(8,128)(2,1)} %taps_ref.1, bf16[32,16,256]{2,1,0:T(8,128)(2,1)} %bitcast.34, bf16[32,16,256]{2,1,0:T(8,128)(2,1)} %bitcast.33), custom_call_target="tpu_custom_call" | custom-call | flops 134217728 | bytes 802816 | tf_op jit(solution)/shard_map/pallas_call | solution.py:83
  19.6 1.0 %reshape_reshape.13 = bf16[256,512]{1,0:T(8,128)(2,1)S(1)} reshape(bf16[32,16,256]{2,1,0:T(8,128)(2,1)} %shard_map.37) | data formatting | bytes 524288 | tf_op jit(solution)/shard_map/reshape;reshape | solution.py:105
  20.6 1.3 %fusion = bf16[512,256]{0,1:T(8,128)(2,1)S(1)} fusion(bf16[256,512]{1,0:T(8,128)(2,1)S(1)} %reshape_reshape.13, bf16[512,512]{1,0:T(8,128)(2,1)} %constant.8.clone), kind=kOutput, calls=%fused_computation.3 | convolution fusion | flops 134348800 | bytes 1048576 | tf_op jit(solution)/shard_map/xn,nq->qx/dot_general | solution.py:112
  22.1 8.8 %all_to_all.5 = bf16[4,128,256]{2,1,0:T(8,128)(2,1)S(1)} all-to-all(bf16[4,128,256]{2,1,0:T(8,128)(2,1)S(1)} %bitcast.37), channel_id=1, replica_groups=mesh['tm'=4,'chan'=8] {'tm'}, dimensions={0} | all-to-all | bytes 524288 | tf_op jit(solution)/shard_map/all_to_all | solution.py:116
  30.9 5.9 %reshape.109 = bf16[4,2,32,2,32,8]{5,4,3,2,1,0:T(8,128)(2,1)} reshape(bf16[4,128,256]{2,1,0:T(8,128)(2,1)S(1)} %all_to_all.5) | data formatting | bytes 524288 | tf_op jit(solution)/shard_map/reshape | solution.py:118
  36.7 5.0 %slice_bitcast_fusion = (bf16[16,32,2,2,4,8]{5,1,2,0,3,4:T(8,128)(2,1)}, bf16[16,32,2,2,4,8]{5,1,2,0,3,4:T(8,128)(2,1)S(1)}) fusion(bf16[4,2,32,2,32,8]{5,4,3,2,1,0:T(8,128)(2,1)} %reshape.109), kind=kLoop, calls=%fused_computation | loop fusion | bytes 524288 | tf_op jit(solution)/shard_map/transpose | solution.py:123
  41.7 2.0 %copy.29 = bf16[16,32,2,2,4,8]{1,5,4,3,2,0:T(8,128)(2,1)S(1)} copy(bf16[16,32,2,2,4,8]{5,1,2,0,3,4:T(8,128)(2,1)} %get-tuple-element.5) | data formatting | bytes 262144 | tf_op jit(solution)/shard_map/transpose | solution.py:123
  43.7 0.9 copy.36
  44.7 0.9 copy.21
  45.6 0.8 copy.28
  47.2 1.5 %broadcast_select_fusion.6 = (bf16[16,1,32,128]{2,3,0,1:T(8,128)(2,1)}, bf16[16,1,32,128]{2,3,0,1:T(8,128)(2,1)}, bf16[16,1,32,128]{2,3,0,1:T(8,128)(2,1)}, bf16...) fusion(bf16[16,1,32,128]{2,3,0,1:T(8,128)(2,1)S(1)} %bitcast.30, ...), kind=kLoop, calls=%fused_computation.14 | loop fusion | flops 524288 | bytes 1573120 | tf_op jit(solution)/shard_map/jit(_where)/select_n | solution.py:139
  48.7 1.2 %copy.25 = bf16[16,1,32,128]{3,2,1,0:T(8,128)(2,1)S(1)} copy(bf16[16,1,32,128]{2,3,0,1:T(8,128)(2,1)} %get-tuple-element.15) | data formatting | bytes 262144 | tf_op jit(solution)/shard_map/jit(_where)/select_n | solution.py:139
  49.9 1.2 %copy.26 = bf16[16,1,32,128]{3,2,1,0:T(8,128)(2,1)S(1)} copy(bf16[16,1,32,128]{2,3,0,1:T(8,128)(2,1)} %get-tuple-element.16) | data formatting | bytes 262144 | tf_op jit(solution)/shard_map/jit(_where)/select_n | solution.py:139
  51.2 1.2 %copy.32 = bf16[16,1,32,128]{3,2,1,0:T(8,128)(2,1)S(1)} copy(bf16[16,1,32,128]{2,3,0,1:T(8,128)(2,1)} %get-tuple-element.19) | data formatting | bytes 262144 | tf_op jit(solution)/shard_map/jit(_where)/select_n | solution.py:139
  52.4 1.2 %copy.31 = bf16[16,1,32,128]{3,2,1,0:T(8,128)(2,1)S(1)} copy(bf16[16,1,32,128]{2,3,0,1:T(8,128)(2,1)} %get-tuple-element.20) | data formatting | bytes 262144 | tf_op jit(solution)/shard_map/jit(_where)/select_n | solution.py:139
  54.5 0.9 pad_maximum_fusion.3
  55.4 0.9 pad_maximum_fusion.1
  56.2 10.4 %all-gather.5.cloned.1.call-done.every_ref = bf16[8,16,32,128]{3,2,1,0:T(8,128)(2,1)} async-done(((bf16[1,16,32,128]{3,2,1,0:T(8,128)(2,1)}), bf16[8,16,32,128]{3,2,1,0:T(8,128)(2,1)}) %all-gather.5.cloned.1.call-update) | async-done | bytes 1048592 | tf_op jit(solution)/shard_map/all_gather | solution.py:125
  66.6 2.7 %shard_map.38.result_ref = f32[2,64,32,256]{3,2,1,0:T(8,128)} custom-call(bf16[16,128,128]{2,1,0:T(8,128)(2,1)} %bitcast.32, bf16[8,16,32,128]{3,2,1,0:T(8,128)(2,1)} %all-gather.5.cloned.1.call-done.every_ref), custom_call_target="tpu_custom_call" | custom-call | flops 134217728 | bytes 3670016 | tf_op jit(solution)/shard_map/pallas_call | solution.py:168
  69.4 20.6 %all-gather.3.cloned.1.call-done.every_ref = bf16[8,16,32,128]{3,2,1,0:T(8,128)(2,1)} async-done(((bf16[1,16,32,128]{3,2,1,0:T(8,128)(2,1)}), bf16[8,16,32,128]{3,2,1,0:T(8,128)(2,1)}) %all-gather.3.cloned.1.call-update) | async-done | bytes 1048592 | tf_op jit(solution)/shard_map/all_gather | solution.py:125
  90.0 2.7 %shard_map.39 = f32[2,64,32,256]{3,2,1,0:T(8,128)} custom-call(bf16[16,128,128]{2,1,0:T(8,128)(2,1)} %bitcast.29, bf16[8,16,32,128]{3,2,1,0:T(8,128)(2,1)} %all-gather.3.cloned.1.call-done.every_ref, f32[2,64,32,256]{3,2,1,0:T(8,128)} %shard_map.38.result_ref), custom_call_target="tpu_custom_call", output_to_operand_aliasing={{}: (2, {})} | custom-call | flops 134217728 | bytes 3670016 | tf_op jit(solution)/shard_map/pallas_call | solution.py:168
  (23 shorter events, 3.2 us)
Async XLA Ops:
  6.5 60.1 %all-gather.5.cloned.1.call-start = ((), (), s32[]{:S(2)}) async-start(), calls=%async_computation.2 | async-start | bytes 1179648 | tf_op jit(solution)/shard_map/all_gather | solution.py:125
  7.3 7.5 %collective-permute-start = (bf16[32,256]{1,0:T(8,128)(2,1)S(1)}, bf16[32,256]{1,0:T(8,128)(2,1)S(1)}, u32[]{:S(2)}, u32[]{:S(2)}) collective-permute-start(bf16[32,256]{1,0:T(8,128)(2,1)S(1)} %slice.24), channel_id=1, source_target_pairs={{0,8},{8,16},{16,24},{1,9},{9,17},{17,25},{2,10},{10,18},{18,26},{... | collective-permute-start | bytes 49160 | tf_op jit(solution)/shard_map/ppermute | solution.py:18
  44.6 45.3 %all-gather.3.cloned.1.call-start = ((), (), s32[]{:S(2)}) async-start(), calls=%async_computation.1 | async-start | bytes 1179648 | tf_op jit(solution)/shard_map/all_gather | solution.py:125
Sparse Core Ops, SparseCore 0:
  44.7 21.8 all-gather.4
  68.2 21.6 all-gather.2

commit v9 on v7

--- a/solution.py
+++ b/solution.py
@@ -7,7 +7,7 @@
 from jax import lax
 from jax.experimental import pallas as pl
 from jax.experimental.pallas import tpu as pltpu
-from jax.sharding import Mesh, PartitionSpec as P
+from jax.sharding import PartitionSpec as P
 
 SEG = 512
 
@@ -117,9 +117,7 @@
     pairs = bins // parts // 2
     shard = own.reshape(parts, 2, pairs, 2, channels, -1).transpose(2, 4, 3, 1, 0, 5)
     shard = shard.reshape(pairs, channels, -1)
-    every = lax.all_gather(shard, "chip", axis=0)
-    every = lax.all_gather(every, "core", axis=1)
-    every = every.reshape((-1,) + shard.shape)
+    every = lax.all_gather(shard, "chan", axis=0)
     return cross_spectra(lhs_rows(shard), every)
 
 
@@ -171,10 +169,7 @@
 
 
 def solution(mesh):
-    tm_size, chan_size = mesh.devices.shape
-    split = Mesh(mesh.devices.reshape(tm_size, chan_size // 2, 2), ("tm", "chip", "core"))
-    chan = ("chip", "core")
-    placed = (P(chan, "tm"), P(chan, None))
+    placed = (P("chan", "tm"), P("chan", None))
     return jax.shard_map(
-        shards, mesh=split, in_specs=placed, out_specs=P(None, "tm", chan, None), check_vma=False
+        shards, mesh=mesh, in_specs=placed, out_specs=P(None, "tm", "chan", None), check_vma=False
     )

time: 93.4 us -> 82.9 us (0.89)
  waiting for transfers between devices: 32.1 us -> 21.6 us
    all_gather x2 -> x1, waiting for transfers between devices: 32 us -> 21.6 us  [shards(): every = lax.all_gather(shard, 'chan', axis=0)]
  transfers between devices with their start and end apart: 3 -> 2, of which waited for: 2 -> 1; matrix products, arithmetic and copies ran while one was open for 11% -> 12% of each run, Pallas kernels for 0% -> 0%
where the time goes in v9:
time: 82.9 us; the launch traced here: 82.2 us
  waiting for transfers between devices  21.6 us (26%)
  local copies, waits for them, and re-layouts  20 us (24%)
  between operations  13.5 us (16%)
  Pallas kernels  8.88 us (11%)
  blocking collectives  8.8 us (11%)
  starting transfers between devices  4.83 us (6%)
  other arithmetic  3.17 us (4%)
  matrix products  1.34 us (2%)
    all_gather x1, waiting for transfers between devices, shards(): every = lax.all_gather(shard, 'chan', axis=0)  21.6 us
    all_to_all x1, blocking collectives, shards(): own = lax.all_to_all(spectra, 'tm', split_axis=0, concat_axis=0, tiled=True)  8.8 us
    reshape x1, local copies, waits for them, and re-layouts, shards(): own.reshape(parts, 2, pairs, 2, channels, -1).transpose(2, 4, 3, 1, 0, 5)  5.86 us
    pallas_call x1, Pallas kernels, cross_spectra(): pl.pallas_call(cross_kernel, out_shape=jax.ShapeDtypeStruct((2, 2 * pairs...  4.88 us
    ppermute x1, starting transfers between devices, shifted(): return lax.ppermute(value, axis, pairs)  4.83 us
    pallas_call x1, Pallas kernels, whiten(): pl.pallas_call(fir_kernel, out_shape=jax.ShapeDtypeStruct(late.shape, jnp...  4 us
    select_n x4, local copies, waits for them, and re-layouts, lhs_rows(): jnp.where(parity == b, part, zero).reshape(pairs, channels, lanes)  3.83 us
    transpose x1, local copies, waits for them, and re-layouts, shards(): own.reshape(parts, 2, pairs, 2, channels, -1).transpose(2, 4, 3, 1, 0, 5)  3.69 us
  transfers between devices with their start and end apart: 2, of which 1 were waited for; matrix products, arithmetic and copies ran while one was open for 12% of the time, Pallas kernels for 0%

profile of v9, /device:TPU:0, one launch (start us, length us, event | category | flops | bytes accessed | tf_op | source)
XLA Modules:
  0.0 82.2 jit_solution(9634512533371235504)
XLA Ops:
  6.5 0.7 slice.12
  7.3 4.8 %collective-permute-start = (bf16[32,256]{1,0:T(8,128)(2,1)S(1)}, bf16[32,256]{1,0:T(8,128)(2,1)S(1)}, u32[]{:S(2)}, u32[]{:S(2)}) collective-permute-start(bf16[32,256]{1,0:T(8,128)(2,1)S(1)} %slice.12), channel_id=1, source_target_pairs={{0,8},{8,16},{16,24},{1,9},{9,17},{17,25},{2,10},{10,18},{18,26},{... | collective-permute-start | bytes 49160 | tf_op jit(solution)/shard_map/ppermute | solution.py:18
  12.1 1.0 %slice.13 = bf16[32,3840]{1,0:T(8,128)(2,1)S(1)} slice(bf16[32,4096]{1,0:T(8,128)(2,1)} %param.3), slice={[0:32], [0:3840]} | slice | bytes 491520 | tf_op jit(solution)/shard_map/slice | solution.py:101
  13.1 1.7 %copy.23 = bf16[4,8,16,256]{3,2,1,0:T(8,128)(2,1)} copy(bf16[4,8,16,256]{3,1,2,0:T(8,128)(2,1)} %bitcast.23) | data formatting | bytes 524288
  14.8 0.8 copy.22
  15.5 4.0 %shard_map.37 = bf16[32,16,256]{2,1,0:T(8,128)(2,1)} custom-call(bf16[32,256]{1,0:T(8,128)(2,1)} %taps_ref.1, bf16[32,16,256]{2,1,0:T(8,128)(2,1)} %bitcast.22, bf16[32,16,256]{2,1,0:T(8,128)(2,1)} %bitcast.21), custom_call_target="tpu_custom_call" | custom-call | flops 134217728 | bytes 802816 | tf_op jit(solution)/shard_map/pallas_call | solution.py:83
  19.5 1.0 %reshape_reshape.8 = bf16[256,512]{1,0:T(8,128)(2,1)S(1)} reshape(bf16[32,16,256]{2,1,0:T(8,128)(2,1)} %shard_map.37) | data formatting | bytes 524288 | tf_op jit(solution)/shard_map/reshape;reshape | solution.py:105
  20.6 1.3 %fusion = bf16[512,256]{0,1:T(8,128)(2,1)S(1)} fusion(bf16[256,512]{1,0:T(8,128)(2,1)S(1)} %reshape_reshape.8, bf16[512,512]{1,0:T(8,128)(2,1)} %constant.8.clone), kind=kOutput, calls=%fused_computation.1 | convolution fusion | flops 134348800 | bytes 1048576 | tf_op jit(solution)/shard_map/xn,nq->qx/dot_general | solution.py:112
  21.9 0.1 copy.21
  22.1 8.8 %all_to_all.5 = bf16[4,128,256]{2,1,0:T(8,128)(2,1)S(1)} all-to-all(bf16[4,128,256]{2,1,0:T(8,128)(2,1)S(1)} %bitcast.25), channel_id=1, replica_groups=mesh['tm'=4,'chan'=8] {'tm'}, dimensions={0} | all-to-all | bytes 524288 | tf_op jit(solution)/shard_map/all_to_all | solution.py:116
  30.9 5.9 %reshape.62 = bf16[4,2,32,2,32,8]{5,4,3,2,1,0:T(8,128)(2,1)} reshape(bf16[4,128,256]{2,1,0:T(8,128)(2,1)S(1)} %all_to_all.5) | data formatting | bytes 524288 | tf_op jit(solution)/shard_map/reshape | solution.py:118
  36.7 3.7 %copy.13 = bf16[32,32,2,2,4,8]{1,5,4,3,2,0:T(8,128)(2,1)S(1)} copy(bf16[32,32,2,2,4,8]{5,1,2,0,3,4:T(8,128)(2,1)} %bitcast.15) | data formatting | bytes 524288 | tf_op jit(solution)/shard_map/transpose | solution.py:118
  40.4 1.0 %copy.20 = bf16[1,32,32,128]{3,2,1,0:T(8,128)(2,1)} copy(bf16[1,32,32,128]{2,3,1,0:T(8,128)(2,1)S(1)} %bitcast.16) | data formatting | bytes 524288 | tf_op jit(solution)/shard_map/all_gather;reshape | solution.py:120
  41.6 0.1 iota.36
  41.8 0.1 fusion.1
  41.9 0.2 pad_maximum_fusion
  42.2 1.7 %broadcast_select_fusion.2 = (bf16[32,1,32,128]{2,3,0,1:T(8,128)(2,1)S(1)}, bf16[32,1,32,128]{2,3,0,1:T(8,128)(2,1)S(1)}, bf16[32,1,32,128]{2,3,0,1:T(8,128)(2,1)}, bf16[32,1,32,128]{2,3,0,1:T(8,128)(2,1)}) fusion(bf16[32,1,32,128]{2,3,0,1:T(8,128)(2,1)S(1)} %bitcast.20, pred[128]{0:T(512)(128)(4,1)S(1)} %iota.36, pred[128]{0:T(512)(128)(4,1)S(1)} %iota.40, ...), kind=kLoop, calls=%fused_computation.6 | loop fusion | flops 524288 | bytes 1573120 | tf_op jit(solution)/shard_map/jit(_where)/select_n | solution.py:133
  43.9 1.6 %copy.15 = bf16[32,1,32,128]{3,2,1,0:T(8,128)(2,1)S(1)} copy(bf16[32,1,32,128]{2,3,0,1:T(8,128)(2,1)} %get-tuple-element.12) | data formatting | bytes 524288 | tf_op jit(solution)/shard_map/jit(_where)/select_n | solution.py:133
  45.4 1.6 %copy.16 = bf16[32,1,32,128]{3,2,1,0:T(8,128)(2,1)S(1)} copy(bf16[32,1,32,128]{2,3,0,1:T(8,128)(2,1)} %get-tuple-element.11) | data formatting | bytes 524288 | tf_op jit(solution)/shard_map/jit(_where)/select_n | solution.py:133
  47.0 0.3 copy.17
  47.4 0.3 copy.18
  47.7 1.1 %pad_maximum_fusion.1 = bf16[32,4,32,128]{3,2,1,0:T(8,128)(2,1)} fusion(bf16[32,1,32,128]{3,2,1,0:T(8,128)(2,1)S(1)} %copy.18, bf16[32,1,32,128]{3,2,1,0:T(8,128)(2,1)S(1)} %copy.17, bf16[32,1,32,128]{3,2,1,0:T(8,128)(2,1)S(1)} %copy.16, bf16[32,1,32,128]{3,2,1,0:T(8,128)(2,1)S(1)} %copy.15), kind=kLoop, calls=%fused_computation.3 | loop fusion | flops 1572864 | bytes 2097152 | tf_op jit(solution)/shard_map/stack | solution.py:134
  48.8 21.6 %all-gather.2.cloned.1.call-done.every_ref = bf16[8,32,32,128]{3,2,1,0:T(8,128)(2,1)} async-done(((bf16[1,32,32,128]{3,2,1,0:T(8,128)(2,1)}), bf16[8,32,32,128]{3,2,1,0:T(8,128)(2,1)}) %all-gather.2.cloned.1.call-update) | async-done | bytes 2097168 | tf_op jit(solution)/shard_map/all_gather | solution.py:120
  70.5 4.9 %shard_map.38 = f32[2,64,32,256]{3,2,1,0:T(8,128)} custom-call(bf16[32,128,128]{2,1,0:T(8,128)(2,1)} %bitcast.19, bf16[8,32,32,128]{3,2,1,0:T(8,128)(2,1)} %all-gather.2.cloned.1.call-done.every_ref), custom_call_target="tpu_custom_call" | custom-call | flops 268435456 | bytes 7340032 | tf_op jit(solution)/shard_map/pallas_call | solution.py:154
  (9 shorter events, 0.3 us)
Async XLA Ops:
  6.5 63.9 %all-gather.2.cloned.1.call-start = ((), (), s32[]{:S(2)}) async-start(), calls=%async_computation.1 | async-start | bytes 2359296 | tf_op jit(solution)/shard_map/all_gather | solution.py:120
  7.3 7.5 %collective-permute-start = (bf16[32,256]{1,0:T(8,128)(2,1)S(1)}, bf16[32,256]{1,0:T(8,128)(2,1)S(1)}, u32[]{:S(2)}, u32[]{:S(2)}) collective-permute-start(bf16[32,256]{1,0:T(8,128)(2,1)S(1)} %slice.12), channel_id=1, source_target_pairs={{0,8},{8,16},{16,24},{1,9},{9,17},{17,25},{2,10},{10,18},{18,26},{... | collective-permute-start | bytes 49160 | tf_op jit(solution)/shard_map/ppermute | solution.py:18
Sparse Core Ops, SparseCore 0:
  41.6 28.8 all-gather.1

commit v10 on v9

--- a/solution.py
+++ b/solution.py
@@ -49,12 +49,13 @@
     return jnp.stack([real_part, imag_part], axis=0)
 
 
-def fir_kernel(taps_ref, early_ref, late_ref, out_ref):
+def fir_kernel(taps_ref, previous_ref, late_ref, out_ref):
     half = taps_ref.shape[1] // 2
     row = lax.broadcasted_iota(jnp.int32, (half, half), 0)
     col = lax.broadcasted_iota(jnp.int32, (half, half), 1)
     upper = col >= row
     zero = jnp.zeros((half, half), jnp.float32)
+    first = lax.broadcasted_iota(jnp.int32, late_ref.shape[1:], 0) == 0
     for ci in range(taps_ref.shape[0]):
         taps = taps_ref[pl.ds(ci, 1), :].astype(jnp.float32)
         low = jnp.broadcast_to(taps[:, :half], (half, half))
@@ -71,37 +72,39 @@
         bottom = jnp.concatenate(
             [jnp.concatenate([d2, d1], axis=1), jnp.concatenate([none, d2], axis=1)], axis=0
         )
-        acc = jnp.dot(early_ref[ci], top, preferred_element_type=jnp.float32)
-        acc = acc + jnp.dot(late_ref[ci], bottom, preferred_element_type=jnp.float32)
+        late = late_ref[ci]
+        shifted_down = pltpu.roll(jnp.dot(late, top, preferred_element_type=jnp.float32), 1, 0)
+        head = jnp.dot(previous_ref[pl.ds(ci, 1), :], top, preferred_element_type=jnp.float32)
+        acc = jnp.where(first, jnp.broadcast_to(head, shifted_down.shape), shifted_down)
+        acc = acc + jnp.dot(late, bottom, preferred_element_type=jnp.float32)
         out_ref[ci] = acc.astype(out_ref.dtype)
 
 
-def whiten(fir_taps, early, late):
+def whiten(fir_taps, previous, late):
     channels, nblocks, tap_count = late.shape
     group = 8
     block = pl.BlockSpec((group, nblocks, tap_count), lambda g: (g, 0, 0))
+    rows = pl.BlockSpec((group, tap_count), lambda g: (g, 0))
     return pl.pallas_call(
         fir_kernel,
         out_shape=jax.ShapeDtypeStruct(late.shape, jnp.bfloat16),
         grid=(channels // group,),
-        in_specs=[pl.BlockSpec((group, tap_count), lambda g: (g, 0)), block, block],
+        in_specs=[rows, rows, block],
         out_specs=block,
         cost_estimate=pl.CostEstimate(
             flops=4 * channels * nblocks * tap_count * tap_count,
-            bytes_accessed=3 * late.size * 2 + fir_taps.size * 2,
+            bytes_accessed=2 * late.size * 2 + 2 * fir_taps.size * 2,
             transcendentals=0,
         ),
-    )(fir_taps, early, late)
+    )(fir_taps, previous, late)
 
 
 def shards(strain, fir_taps):
     tap_count = fir_taps.shape[1]
     channels = strain.shape[0]
     previous = shifted(strain[:, -tap_count:], "tm", 1)
-    early = jnp.concatenate([previous, strain[:, :-tap_count]], axis=1)
-    early = early.reshape(channels, -1, tap_count)
     late = strain.reshape(channels, -1, tap_count)
-    whitened = whiten(fir_taps, early, late).reshape(channels, -1)
+    whitened = whiten(fir_taps, previous, late).reshape(channels, -1)
     segments = whitened.reshape(channels * (whitened.shape[1] // SEG), SEG)
     parts = lax.axis_size("tm")
     table = make_table()

time: 82.9 us -> 82.9 us (level)
  local copies, waits for them, and re-layouts: 20 us -> 18.9 us
  blocking collectives: 8.8 us -> 9.76 us
    slice x1 -> x0, local copies, waits for them, and re-layouts: 0.96 us -> none  [shards(): early = jnp.concatenate([previous, strain[:, :-tap_count]], axis=1)]
    all_to_all x1, blocking collectives: 8.8 us -> 9.76 us  [shards(): own = lax.all_to_all(spectra, 'tm', split_axis=0, concat_axis=0, tiled=True)]
    unnamed x2 -> x3, local copies, waits for them, and re-layouts: 2.45 us -> 2.3 us
  transfers between devices with their start and end apart: 2 -> 2, of which waited for: 1 -> 1; matrix products, arithmetic and copies ran while one was open for 12% -> 11% of each run, Pallas kernels for 0% -> 0%
where the time goes in v10:
time: 82.9 us; the launch traced here: 82.2 us
  waiting for transfers between devices  21.6 us (26%)
  local copies, waits for them, and re-layouts  18.9 us (23%)
  between operations  13.5 us (16%)
  blocking collectives  9.76 us (12%)
  Pallas kernels  9.09 us (11%)
  starting transfers between devices  4.83 us (6%)
  other arithmetic  3.19 us (4%)
  matrix products  1.34 us (2%)
    all_gather x1, waiting for transfers between devices, shards(): every = lax.all_gather(shard, 'chan', axis=0)  21.6 us
    all_to_all x1, blocking collectives, shards(): own = lax.all_to_all(spectra, 'tm', split_axis=0, concat_axis=0, tiled=True)  9.76 us
    reshape x1, local copies, waits for them, and re-layouts, shards(): own.reshape(parts, 2, pairs, 2, channels, -1).transpose(2, 4, 3, 1, 0, 5)  5.86 us
    pallas_call x1, Pallas kernels, cross_spectra(): pl.pallas_call(cross_kernel, out_shape=jax.ShapeDtypeStruct((2, 2 * pairs...  4.87 us
    ppermute x1, starting transfers between devices, shifted(): return lax.ppermute(value, axis, pairs)  4.83 us
    pallas_call x1, Pallas kernels, whiten(): pl.pallas_call(fir_kernel, out_shape=jax.ShapeDtypeStruct(late.shape, jnp...  4.21 us
    select_n x4, local copies, waits for them, and re-layouts, lhs_rows(): jnp.where(parity == b, part, zero).reshape(pairs, channels, lanes)  3.83 us
    transpose x1, local copies, waits for them, and re-layouts, shards(): own.reshape(parts, 2, pairs, 2, channels, -1).transpose(2, 4, 3, 1, 0, 5)  3.69 us
  transfers between devices with their start and end apart: 2, of which 1 were waited for; matrix products, arithmetic and copies ran while one was open for 11% of the time, Pallas kernels for 0%

profile of v10, /device:TPU:0, one launch (start us, length us, event | category | flops | bytes accessed | tf_op | source)
XLA Modules:
  0.0 82.2 jit_solution(17979546977798797601)
XLA Ops:
  6.5 0.7 slice.9
  7.3 4.8 %collective-permute-start = (bf16[32,256]{1,0:T(8,128)(2,1)S(1)}, bf16[32,256]{1,0:T(8,128)(2,1)S(1)}, u32[]{:S(2)}, u32[]{:S(2)}) collective-permute-start(bf16[32,256]{1,0:T(8,128)(2,1)S(1)} %slice.9), channel_id=1, source_target_pairs={{0,8},{8,16},{16,24},{1,9},{9,17},{17,25},{2,10},{10,18},{18,26},{... | collective-permute-start | bytes 49160 | tf_op jit(solution)/shard_map/ppermute | solution.py:18
  12.1 1.7 %copy.22 = bf16[4,8,16,256]{3,2,1,0:T(8,128)(2,1)} copy(bf16[4,8,16,256]{3,1,2,0:T(8,128)(2,1)} %bitcast.21) | data formatting | bytes 524288
  13.8 0.6 copy-done
  14.4 4.2 %shard_map.37 = bf16[32,16,256]{2,1,0:T(8,128)(2,1)} custom-call(bf16[32,256]{1,0:T(8,128)(2,1)} %taps_ref.1, bf16[32,256]{1,0:T(8,128)(2,1)} %copy-done, bf16[32,16,256]{2,1,0:T(8,128)(2,1)} %bitcast.19), custom_call_target="tpu_custom_call" | custom-call | flops 134217728 | bytes 557056 | tf_op jit(solution)/shard_map/pallas_call | solution.py:88
  18.6 1.0 %reshape_reshape.8 = bf16[256,512]{1,0:T(8,128)(2,1)S(1)} reshape(bf16[32,16,256]{2,1,0:T(8,128)(2,1)} %shard_map.37) | data formatting | bytes 524288 | tf_op jit(solution)/shard_map/reshape;reshape | solution.py:108
  19.7 1.3 %fusion = bf16[512,256]{0,1:T(8,128)(2,1)S(1)} fusion(bf16[256,512]{1,0:T(8,128)(2,1)S(1)} %reshape_reshape.8, bf16[512,512]{1,0:T(8,128)(2,1)} %constant.8.clone), kind=kOutput, calls=%fused_computation.1 | convolution fusion | flops 134348800 | bytes 1048576 | tf_op jit(solution)/shard_map/xn,nq->qx/dot_general | solution.py:115
  21.0 0.1 copy.21
  21.1 9.8 %all_to_all.5 = bf16[4,128,256]{2,1,0:T(8,128)(2,1)S(1)} all-to-all(bf16[4,128,256]{2,1,0:T(8,128)(2,1)S(1)} %bitcast.20), channel_id=1, replica_groups=mesh['tm'=4,'chan'=8] {'tm'}, dimensions={0} | all-to-all | bytes 524288 | tf_op jit(solution)/shard_map/all_to_all | solution.py:119
  30.9 5.9 %reshape.58 = bf16[4,2,32,2,32,8]{5,4,3,2,1,0:T(8,128)(2,1)} reshape(bf16[4,128,256]{2,1,0:T(8,128)(2,1)S(1)} %all_to_all.5) | data formatting | bytes 524288 | tf_op jit(solution)/shard_map/reshape | solution.py:121
  36.8 3.7 %copy.13 = bf16[32,32,2,2,4,8]{1,5,4,3,2,0:T(8,128)(2,1)S(1)} copy(bf16[32,32,2,2,4,8]{5,1,2,0,3,4:T(8,128)(2,1)} %bitcast.13) | data formatting | bytes 524288 | tf_op jit(solution)/shard_map/transpose | solution.py:121
  40.5 1.0 %copy.20 = bf16[1,32,32,128]{3,2,1,0:T(8,128)(2,1)} copy(bf16[1,32,32,128]{2,3,1,0:T(8,128)(2,1)S(1)} %bitcast.14) | data formatting | bytes 524288 | tf_op jit(solution)/shard_map/all_gather;reshape | solution.py:123
  41.6 0.1 iota.36
  41.8 0.1 iota.40
  41.9 0.1 fusion.1
  42.0 0.2 pad_maximum_fusion
  42.2 1.7 %broadcast_select_fusion.2 = (bf16[32,1,32,128]{2,3,0,1:T(8,128)(2,1)S(1)}, bf16[32,1,32,128]{2,3,0,1:T(8,128)(2,1)S(1)}, bf16[32,1,32,128]{2,3,0,1:T(8,128)(2,1)}, bf16[32,1,32,128]{2,3,0,1:T(8,128)(2,1)}) fusion(bf16[32,1,32,128]{2,3,0,1:T(8,128)(2,1)S(1)} %bitcast.18, pred[128]{0:T(512)(128)(4,1)S(1)} %iota.36, pred[128]{0:T(512)(128)(4,1)S(1)} %iota.40, ...), kind=kLoop, calls=%fused_computation.6 | loop fusion | flops 524288 | bytes 1573120 | tf_op jit(solution)/shard_map/jit(_where)/select_n | solution.py:136
  43.9 1.6 %copy.15 = bf16[32,1,32,128]{3,2,1,0:T(8,128)(2,1)S(1)} copy(bf16[32,1,32,128]{2,3,0,1:T(8,128)(2,1)} %get-tuple-element.12) | data formatting | bytes 524288 | tf_op jit(solution)/shard_map/jit(_where)/select_n | solution.py:136
  45.5 1.6 %copy.16 = bf16[32,1,32,128]{3,2,1,0:T(8,128)(2,1)S(1)} copy(bf16[32,1,32,128]{2,3,0,1:T(8,128)(2,1)} %get-tuple-element.11) | data formatting | bytes 524288 | tf_op jit(solution)/shard_map/jit(_where)/select_n | solution.py:136
  47.1 0.3 copy.17
  47.4 0.3 copy.18
  47.8 1.1 %pad_maximum_fusion.1 = bf16[32,4,32,128]{3,2,1,0:T(8,128)(2,1)} fusion(bf16[32,1,32,128]{3,2,1,0:T(8,128)(2,1)S(1)} %copy.18, bf16[32,1,32,128]{3,2,1,0:T(8,128)(2,1)S(1)} %copy.17, bf16[32,1,32,128]{3,2,1,0:T(8,128)(2,1)S(1)} %copy.16, bf16[32,1,32,128]{3,2,1,0:T(8,128)(2,1)S(1)} %copy.15), kind=kLoop, calls=%fused_computation.3 | loop fusion | flops 1572864 | bytes 2097152 | tf_op jit(solution)/shard_map/stack | solution.py:137
  48.9 21.6 %all-gather.2.cloned.1.call-done.every_ref = bf16[8,32,32,128]{3,2,1,0:T(8,128)(2,1)} async-done(((bf16[1,32,32,128]{3,2,1,0:T(8,128)(2,1)}), bf16[8,32,32,128]{3,2,1,0:T(8,128)(2,1)}) %all-gather.2.cloned.1.call-update) | async-done | bytes 2097168 | tf_op jit(solution)/shard_map/all_gather | solution.py:123
  70.5 4.9 %shard_map.38 = f32[2,64,32,256]{3,2,1,0:T(8,128)} custom-call(bf16[32,128,128]{2,1,0:T(8,128)(2,1)} %bitcast.17, bf16[8,32,32,128]{3,2,1,0:T(8,128)(2,1)} %all-gather.2.cloned.1.call-done.every_ref), custom_call_target="tpu_custom_call" | custom-call | flops 268435456 | bytes 7340032 | tf_op jit(solution)/shard_map/pallas_call | solution.py:157
  (8 shorter events, 0.2 us)
Async XLA Ops:
  6.5 64.0 %all-gather.2.cloned.1.call-start = ((), (), s32[]{:S(2)}) async-start(), calls=%async_computation.1 | async-start | bytes 2359296 | tf_op jit(solution)/shard_map/all_gather | solution.py:123
  7.3 6.5 %collective-permute-start = (bf16[32,256]{1,0:T(8,128)(2,1)S(1)}, bf16[32,256]{1,0:T(8,128)(2,1)S(1)}, u32[]{:S(2)}, u32[]{:S(2)}) collective-permute-start(bf16[32,256]{1,0:T(8,128)(2,1)S(1)} %slice.9), channel_id=1, source_target_pairs={{0,8},{8,16},{16,24},{1,9},{9,17},{17,25},{2,10},{10,18},{18,26},{... | collective-permute-start | bytes 49160 | tf_op jit(solution)/shard_map/ppermute | solution.py:18
  13.8 0.6 copy-start
Sparse Core Ops, SparseCore 0:
  41.6 28.8 all-gather.1

commit v11 on v10

--- a/solution.py
+++ b/solution.py
@@ -152,7 +152,7 @@
 
 def cross_spectra(lhs, every):
     sources, pairs, channels, lanes = every.shape
-    step = 8 if pairs % 8 == 0 else pairs
+    step = 4 if pairs % 4 == 0 else pairs
     wide = sources * channels
     return pl.pallas_call(
         cross_kernel,

time: 82.9 us -> 85.3 us (1.029)
  Pallas kernels: 9.09 us -> 11.4 us
    pallas_call x1, Pallas kernels: 4.87 us -> 7.21 us  [cross_spectra(): pl.pallas_call(cross_kernel, out_shape=jax.ShapeDtypeStruct((2, 2 * pairs...]
where the time goes in v11:
time: 85.3 us; the launch traced here: 84.6 us
  waiting for transfers between devices  21.6 us (25%)
  local copies, waits for them, and re-layouts  18.9 us (22%)
  between operations  13.5 us (16%)
  Pallas kernels  11.4 us (13%)
  blocking collectives  9.76 us (11%)
  starting transfers between devices  4.83 us (6%)
  other arithmetic  3.19 us (4%)
  matrix products  1.34 us (2%)
    all_gather x1, waiting for transfers between devices, shards(): every = lax.all_gather(shard, 'chan', axis=0)  21.6 us
    all_to_all x1, blocking collectives, shards(): own = lax.all_to_all(spectra, 'tm', split_axis=0, concat_axis=0, tiled=True)  9.76 us
    pallas_call x1, Pallas kernels, cross_spectra(): pl.pallas_call(cross_kernel, out_shape=jax.ShapeDtypeStruct((2, 2 * pairs...  7.21 us
    reshape x1, local copies, waits for them, and re-layouts, shards(): own.reshape(parts, 2, pairs, 2, channels, -1).transpose(2, 4, 3, 1, 0, 5)  5.86 us
    ppermute x1, starting transfers between devices, shifted(): return lax.ppermute(value, axis, pairs)  4.83 us
    pallas_call x1, Pallas kernels, whiten(): pl.pallas_call(fir_kernel, out_shape=jax.ShapeDtypeStruct(late.shape, jnp...  4.21 us
    select_n x4, local copies, waits for them, and re-layouts, lhs_rows(): jnp.where(parity == b, part, zero).reshape(pairs, channels, lanes)  3.83 us
    transpose x1, local copies, waits for them, and re-layouts, shards(): own.reshape(parts, 2, pairs, 2, channels, -1).transpose(2, 4, 3, 1, 0, 5)  3.69 us
  transfers between devices with their start and end apart: 2, of which 1 were waited for; matrix products, arithmetic and copies ran while one was open for 11% of the time, Pallas kernels for 0%

profile of v11, /device:TPU:0, one launch (start us, length us, event | category | flops | bytes accessed | tf_op | source)
XLA Modules:
  0.0 84.6 jit_solution(12413238895026907951)
XLA Ops:
  6.5 0.7 slice.9
  7.3 4.8 %collective-permute-start = (bf16[32,256]{1,0:T(8,128)(2,1)S(1)}, bf16[32,256]{1,0:T(8,128)(2,1)S(1)}, u32[]{:S(2)}, u32[]{:S(2)}) collective-permute-start(bf16[32,256]{1,0:T(8,128)(2,1)S(1)} %slice.9), channel_id=1, source_target_pairs={{0,8},{8,16},{16,24},{1,9},{9,17},{17,25},{2,10},{10,18},{18,26},{... | collective-permute-start | bytes 49160 | tf_op jit(solution)/shard_map/ppermute | solution.py:18
  12.1 1.7 %copy.22 = bf16[4,8,16,256]{3,2,1,0:T(8,128)(2,1)} copy(bf16[4,8,16,256]{3,1,2,0:T(8,128)(2,1)} %bitcast.21) | data formatting | bytes 524288
  13.8 0.6 copy-done
  14.4 4.2 %shard_map.37 = bf16[32,16,256]{2,1,0:T(8,128)(2,1)} custom-call(bf16[32,256]{1,0:T(8,128)(2,1)} %taps_ref.1, bf16[32,256]{1,0:T(8,128)(2,1)} %copy-done, bf16[32,16,256]{2,1,0:T(8,128)(2,1)} %bitcast.19), custom_call_target="tpu_custom_call" | custom-call | flops 134217728 | bytes 557056 | tf_op jit(solution)/shard_map/pallas_call | solution.py:88
  18.6 1.0 %reshape_reshape.8 = bf16[256,512]{1,0:T(8,128)(2,1)S(1)} reshape(bf16[32,16,256]{2,1,0:T(8,128)(2,1)} %shard_map.37) | data formatting | bytes 524288 | tf_op jit(solution)/shard_map/reshape;reshape | solution.py:108
  19.7 1.3 %fusion = bf16[512,256]{0,1:T(8,128)(2,1)S(1)} fusion(bf16[256,512]{1,0:T(8,128)(2,1)S(1)} %reshape_reshape.8, bf16[512,512]{1,0:T(8,128)(2,1)} %constant.8.clone), kind=kOutput, calls=%fused_computation.1 | convolution fusion | flops 134348800 | bytes 1048576 | tf_op jit(solution)/shard_map/xn,nq->qx/dot_general | solution.py:115
  21.0 0.1 copy.21
  21.1 9.8 %all_to_all.5 = bf16[4,128,256]{2,1,0:T(8,128)(2,1)S(1)} all-to-all(bf16[4,128,256]{2,1,0:T(8,128)(2,1)S(1)} %bitcast.20), channel_id=1, replica_groups=mesh['tm'=4,'chan'=8] {'tm'}, dimensions={0} | all-to-all | bytes 524288 | tf_op jit(solution)/shard_map/all_to_all | solution.py:119
  30.9 5.9 %reshape.58 = bf16[4,2,32,2,32,8]{5,4,3,2,1,0:T(8,128)(2,1)} reshape(bf16[4,128,256]{2,1,0:T(8,128)(2,1)S(1)} %all_to_all.5) | data formatting | bytes 524288 | tf_op jit(solution)/shard_map/reshape | solution.py:121
  36.8 3.7 %copy.13 = bf16[32,32,2,2,4,8]{1,5,4,3,2,0:T(8,128)(2,1)S(1)} copy(bf16[32,32,2,2,4,8]{5,1,2,0,3,4:T(8,128)(2,1)} %bitcast.13) | data formatting | bytes 524288 | tf_op jit(solution)/shard_map/transpose | solution.py:121
  40.5 1.0 %copy.20 = bf16[1,32,32,128]{3,2,1,0:T(8,128)(2,1)} copy(bf16[1,32,32,128]{2,3,1,0:T(8,128)(2,1)S(1)} %bitcast.14) | data formatting | bytes 524288 | tf_op jit(solution)/shard_map/all_gather;reshape | solution.py:123
  41.6 0.1 iota.36
  41.8 0.1 iota.40
  41.9 0.1 fusion.1
  42.0 0.2 pad_maximum_fusion
  42.2 1.7 %broadcast_select_fusion.2 = (bf16[32,1,32,128]{2,3,0,1:T(8,128)(2,1)S(1)}, bf16[32,1,32,128]{2,3,0,1:T(8,128)(2,1)S(1)}, bf16[32,1,32,128]{2,3,0,1:T(8,128)(2,1)}, bf16[32,1,32,128]{2,3,0,1:T(8,128)(2,1)}) fusion(bf16[32,1,32,128]{2,3,0,1:T(8,128)(2,1)S(1)} %bitcast.18, pred[128]{0:T(512)(128)(4,1)S(1)} %iota.36, pred[128]{0:T(512)(128)(4,1)S(1)} %iota.40, ...), kind=kLoop, calls=%fused_computation.6 | loop fusion | flops 524288 | bytes 1573120 | tf_op jit(solution)/shard_map/jit(_where)/select_n | solution.py:136
  43.9 1.6 %copy.15 = bf16[32,1,32,128]{3,2,1,0:T(8,128)(2,1)S(1)} copy(bf16[32,1,32,128]{2,3,0,1:T(8,128)(2,1)} %get-tuple-element.12) | data formatting | bytes 524288 | tf_op jit(solution)/shard_map/jit(_where)/select_n | solution.py:136
  45.5 1.6 %copy.16 = bf16[32,1,32,128]{3,2,1,0:T(8,128)(2,1)S(1)} copy(bf16[32,1,32,128]{2,3,0,1:T(8,128)(2,1)} %get-tuple-element.11) | data formatting | bytes 524288 | tf_op jit(solution)/shard_map/jit(_where)/select_n | solution.py:136
  47.1 0.3 copy.17
  47.4 0.3 copy.18
  47.8 1.1 %pad_maximum_fusion.1 = bf16[32,4,32,128]{3,2,1,0:T(8,128)(2,1)} fusion(bf16[32,1,32,128]{3,2,1,0:T(8,128)(2,1)S(1)} %copy.18, bf16[32,1,32,128]{3,2,1,0:T(8,128)(2,1)S(1)} %copy.17, bf16[32,1,32,128]{3,2,1,0:T(8,128)(2,1)S(1)} %copy.16, bf16[32,1,32,128]{3,2,1,0:T(8,128)(2,1)S(1)} %copy.15), kind=kLoop, calls=%fused_computation.3 | loop fusion | flops 1572864 | bytes 2097152 | tf_op jit(solution)/shard_map/stack | solution.py:137
  48.9 21.6 %all-gather.2.cloned.1.call-done.every_ref = bf16[8,32,32,128]{3,2,1,0:T(8,128)(2,1)} async-done(((bf16[1,32,32,128]{3,2,1,0:T(8,128)(2,1)}), bf16[8,32,32,128]{3,2,1,0:T(8,128)(2,1)}) %all-gather.2.cloned.1.call-update) | async-done | bytes 2097168 | tf_op jit(solution)/shard_map/all_gather | solution.py:123
  70.5 7.2 %shard_map.38 = f32[2,64,32,256]{3,2,1,0:T(8,128)} custom-call(bf16[32,128,128]{2,1,0:T(8,128)(2,1)} %bitcast.17, bf16[8,32,32,128]{3,2,1,0:T(8,128)(2,1)} %all-gather.2.cloned.1.call-done.every_ref), custom_call_target="tpu_custom_call" | custom-call | flops 268435456 | bytes 7340032 | tf_op jit(solution)/shard_map/pallas_call | solution.py:157
  (8 shorter events, 0.2 us)
Async XLA Ops:
  6.5 64.0 %all-gather.2.cloned.1.call-start = ((), (), s32[]{:S(2)}) async-start(), calls=%async_computation.1 | async-start | bytes 2359296 | tf_op jit(solution)/shard_map/all_gather | solution.py:123
  7.3 6.5 %collective-permute-start = (bf16[32,256]{1,0:T(8,128)(2,1)S(1)}, bf16[32,256]{1,0:T(8,128)(2,1)S(1)}, u32[]{:S(2)}, u32[]{:S(2)}) collective-permute-start(bf16[32,256]{1,0:T(8,128)(2,1)S(1)} %slice.9), channel_id=1, source_target_pairs={{0,8},{8,16},{16,24},{1,9},{9,17},{17,25},{2,10},{10,18},{18,26},{... | collective-permute-start | bytes 49160 | tf_op jit(solution)/shard_map/ppermute | solution.py:18
  13.8 0.6 copy-start
Sparse Core Ops, SparseCore 0:
  41.6 28.8 all-gather.1

commit v12 on v11

--- a/solution.py
+++ b/solution.py
@@ -152,7 +152,7 @@
 
 def cross_spectra(lhs, every):
     sources, pairs, channels, lanes = every.shape
-    step = 4 if pairs % 4 == 0 else pairs
+    step = 16 if pairs % 16 == 0 else pairs
     wide = sources * channels
     return pl.pallas_call(
         cross_kernel,

time: 85.3 us -> 81.8 us (0.959)
  Pallas kernels: 11.4 us -> 8.08 us
    pallas_call x1, Pallas kernels: 7.21 us -> 3.87 us  [cross_spectra(): pl.pallas_call(cross_kernel, out_shape=jax.ShapeDtypeStruct((2, 2 * pairs...]
where the time goes in v12:
time: 81.8 us; the launch traced here: 81.2 us
  waiting for transfers between devices  21.6 us (26%)
  local copies, waits for them, and re-layouts  18.9 us (23%)
  between operations  13.5 us (17%)
  blocking collectives  9.76 us (12%)
  Pallas kernels  8.08 us (10%)
  starting transfers between devices  4.83 us (6%)
  other arithmetic  3.19 us (4%)
  matrix products  1.34 us (2%)
    all_gather x1, waiting for transfers between devices, shards(): every = lax.all_gather(shard, 'chan', axis=0)  21.6 us
    all_to_all x1, blocking collectives, shards(): own = lax.all_to_all(spectra, 'tm', split_axis=0, concat_axis=0, tiled=True)  9.76 us
    reshape x1, local copies, waits for them, and re-layouts, shards(): own.reshape(parts, 2, pairs, 2, channels, -1).transpose(2, 4, 3, 1, 0, 5)  5.86 us
    ppermute x1, starting transfers between devices, shifted(): return lax.ppermute(value, axis, pairs)  4.83 us
    pallas_call x1, Pallas kernels, whiten(): pl.pallas_call(fir_kernel, out_shape=jax.ShapeDtypeStruct(late.shape, jnp...  4.21 us
    pallas_call x1, Pallas kernels, cross_spectra(): pl.pallas_call(cross_kernel, out_shape=jax.ShapeDtypeStruct((2, 2 * pairs...  3.87 us
    select_n x4, local copies, waits for them, and re-layouts, lhs_rows(): jnp.where(parity == b, part, zero).reshape(pairs, channels, lanes)  3.83 us
    transpose x1, local copies, waits for them, and re-layouts, shards(): own.reshape(parts, 2, pairs, 2, channels, -1).transpose(2, 4, 3, 1, 0, 5)  3.69 us
  transfers between devices with their start and end apart: 2, of which 1 were waited for; matrix products, arithmetic and copies ran while one was open for 11% of the time, Pallas kernels for 0%

profile of v12, /device:TPU:0, one launch (start us, length us, event | category | flops | bytes accessed | tf_op | source)
XLA Modules:
  0.0 81.2 jit_solution(5392715166081306041)
XLA Ops:
  6.5 0.7 slice.9
  7.3 4.8 %collective-permute-start = (bf16[32,256]{1,0:T(8,128)(2,1)S(1)}, bf16[32,256]{1,0:T(8,128)(2,1)S(1)}, u32[]{:S(2)}, u32[]{:S(2)}) collective-permute-start(bf16[32,256]{1,0:T(8,128)(2,1)S(1)} %slice.9), channel_id=1, source_target_pairs={{0,8},{8,16},{16,24},{1,9},{9,17},{17,25},{2,10},{10,18},{18,26},{... | collective-permute-start | bytes 49160 | tf_op jit(solution)/shard_map/ppermute | solution.py:18
  12.1 1.7 %copy.22 = bf16[4,8,16,256]{3,2,1,0:T(8,128)(2,1)} copy(bf16[4,8,16,256]{3,1,2,0:T(8,128)(2,1)} %bitcast.21) | data formatting | bytes 524288
  13.8 0.6 copy-done
  14.4 4.2 %shard_map.37 = bf16[32,16,256]{2,1,0:T(8,128)(2,1)} custom-call(bf16[32,256]{1,0:T(8,128)(2,1)} %taps_ref.1, bf16[32,256]{1,0:T(8,128)(2,1)} %copy-done, bf16[32,16,256]{2,1,0:T(8,128)(2,1)} %bitcast.19), custom_call_target="tpu_custom_call" | custom-call | flops 134217728 | bytes 557056 | tf_op jit(solution)/shard_map/pallas_call | solution.py:88
  18.6 1.0 %reshape_reshape.8 = bf16[256,512]{1,0:T(8,128)(2,1)S(1)} reshape(bf16[32,16,256]{2,1,0:T(8,128)(2,1)} %shard_map.37) | data formatting | bytes 524288 | tf_op jit(solution)/shard_map/reshape;reshape | solution.py:108
  19.7 1.3 %fusion = bf16[512,256]{0,1:T(8,128)(2,1)S(1)} fusion(bf16[256,512]{1,0:T(8,128)(2,1)S(1)} %reshape_reshape.8, bf16[512,512]{1,0:T(8,128)(2,1)} %constant.8.clone), kind=kOutput, calls=%fused_computation.1 | convolution fusion | flops 134348800 | bytes 1048576 | tf_op jit(solution)/shard_map/xn,nq->qx/dot_general | solution.py:115
  21.0 0.1 copy.21
  21.1 9.8 %all_to_all.5 = bf16[4,128,256]{2,1,0:T(8,128)(2,1)S(1)} all-to-all(bf16[4,128,256]{2,1,0:T(8,128)(2,1)S(1)} %bitcast.20), channel_id=1, replica_groups=mesh['tm'=4,'chan'=8] {'tm'}, dimensions={0} | all-to-all | bytes 524288 | tf_op jit(solution)/shard_map/all_to_all | solution.py:119
  30.9 5.9 %reshape.58 = bf16[4,2,32,2,32,8]{5,4,3,2,1,0:T(8,128)(2,1)} reshape(bf16[4,128,256]{2,1,0:T(8,128)(2,1)S(1)} %all_to_all.5) | data formatting | bytes 524288 | tf_op jit(solution)/shard_map/reshape | solution.py:121
  36.8 3.7 %copy.13 = bf16[32,32,2,2,4,8]{1,5,4,3,2,0:T(8,128)(2,1)S(1)} copy(bf16[32,32,2,2,4,8]{5,1,2,0,3,4:T(8,128)(2,1)} %bitcast.13) | data formatting | bytes 524288 | tf_op jit(solution)/shard_map/transpose | solution.py:121
  40.5 1.0 %copy.20 = bf16[1,32,32,128]{3,2,1,0:T(8,128)(2,1)} copy(bf16[1,32,32,128]{2,3,1,0:T(8,128)(2,1)S(1)} %bitcast.14) | data formatting | bytes 524288 | tf_op jit(solution)/shard_map/all_gather;reshape | solution.py:123
  41.6 0.1 iota.36
  41.8 0.1 iota.40
  41.9 0.1 fusion.1
  42.0 0.2 pad_maximum_fusion
  42.2 1.7 %broadcast_select_fusion.2 = (bf16[32,1,32,128]{2,3,0,1:T(8,128)(2,1)S(1)}, bf16[32,1,32,128]{2,3,0,1:T(8,128)(2,1)S(1)}, bf16[32,1,32,128]{2,3,0,1:T(8,128)(2,1)}, bf16[32,1,32,128]{2,3,0,1:T(8,128)(2,1)}) fusion(bf16[32,1,32,128]{2,3,0,1:T(8,128)(2,1)S(1)} %bitcast.18, pred[128]{0:T(512)(128)(4,1)S(1)} %iota.36, pred[128]{0:T(512)(128)(4,1)S(1)} %iota.40, ...), kind=kLoop, calls=%fused_computation.6 | loop fusion | flops 524288 | bytes 1573120 | tf_op jit(solution)/shard_map/jit(_where)/select_n | solution.py:136
  43.9 1.6 %copy.15 = bf16[32,1,32,128]{3,2,1,0:T(8,128)(2,1)S(1)} copy(bf16[32,1,32,128]{2,3,0,1:T(8,128)(2,1)} %get-tuple-element.12) | data formatting | bytes 524288 | tf_op jit(solution)/shard_map/jit(_where)/select_n | solution.py:136
  45.5 1.6 %copy.16 = bf16[32,1,32,128]{3,2,1,0:T(8,128)(2,1)S(1)} copy(bf16[32,1,32,128]{2,3,0,1:T(8,128)(2,1)} %get-tuple-element.11) | data formatting | bytes 524288 | tf_op jit(solution)/shard_map/jit(_where)/select_n | solution.py:136
  47.1 0.3 copy.17
  47.4 0.3 copy.18
  47.8 1.1 %pad_maximum_fusion.1 = bf16[32,4,32,128]{3,2,1,0:T(8,128)(2,1)} fusion(bf16[32,1,32,128]{3,2,1,0:T(8,128)(2,1)S(1)} %copy.18, bf16[32,1,32,128]{3,2,1,0:T(8,128)(2,1)S(1)} %copy.17, bf16[32,1,32,128]{3,2,1,0:T(8,128)(2,1)S(1)} %copy.16, bf16[32,1,32,128]{3,2,1,0:T(8,128)(2,1)S(1)} %copy.15), kind=kLoop, calls=%fused_computation.3 | loop fusion | flops 1572864 | bytes 2097152 | tf_op jit(solution)/shard_map/stack | solution.py:137
  48.9 21.6 %all-gather.2.cloned.1.call-done.every_ref = bf16[8,32,32,128]{3,2,1,0:T(8,128)(2,1)} async-done(((bf16[1,32,32,128]{3,2,1,0:T(8,128)(2,1)}), bf16[8,32,32,128]{3,2,1,0:T(8,128)(2,1)}) %all-gather.2.cloned.1.call-update) | async-done | bytes 2097168 | tf_op jit(solution)/shard_map/all_gather | solution.py:123
  70.5 3.9 %shard_map.38 = f32[2,64,32,256]{3,2,1,0:T(8,128)} custom-call(bf16[32,128,128]{2,1,0:T(8,128)(2,1)} %bitcast.17, bf16[8,32,32,128]{3,2,1,0:T(8,128)(2,1)} %all-gather.2.cloned.1.call-done.every_ref), custom_call_target="tpu_custom_call" | custom-call | flops 268435456 | bytes 7340032 | tf_op jit(solution)/shard_map/pallas_call | solution.py:157
  (8 shorter events, 0.2 us)
Async XLA Ops:
  6.5 64.0 %all-gather.2.cloned.1.call-start = ((), (), s32[]{:S(2)}) async-start(), calls=%async_computation.1 | async-start | bytes 2359296 | tf_op jit(solution)/shard_map/all_gather | solution.py:123
  7.3 6.5 %collective-permute-start = (bf16[32,256]{1,0:T(8,128)(2,1)S(1)}, bf16[32,256]{1,0:T(8,128)(2,1)S(1)}, u32[]{:S(2)}, u32[]{:S(2)}) collective-permute-start(bf16[32,256]{1,0:T(8,128)(2,1)S(1)} %slice.9), channel_id=1, source_target_pairs={{0,8},{8,16},{16,24},{1,9},{9,17},{17,25},{2,10},{10,18},{18,26},{... | collective-permute-start | bytes 49160 | tf_op jit(solution)/shard_map/ppermute | solution.py:18
  13.8 0.6 copy-start
Sparse Core Ops, SparseCore 0:
  41.6 28.8 all-gather.1

commit v13 on v12

--- a/solution.py
+++ b/solution.py
@@ -82,7 +82,7 @@
 
 def whiten(fir_taps, previous, late):
     channels, nblocks, tap_count = late.shape
-    group = 8
+    group = 16 if channels % 16 == 0 else channels
     block = pl.BlockSpec((group, nblocks, tap_count), lambda g: (g, 0, 0))
     rows = pl.BlockSpec((group, tap_count), lambda g: (g, 0))
     return pl.pallas_call(

time: 81.8 us -> 81.1 us (level)
  no operation moved by 1% of the time
where the time goes in v13:
time: 81.1 us; the launch traced here: 80.6 us
  waiting for transfers between devices  21.6 us (27%)
  local copies, waits for them, and re-layouts  18.9 us (23%)
  between operations  13.5 us (17%)
  blocking collectives  9.76 us (12%)
  Pallas kernels  7.46 us (9%)
  starting transfers between devices  4.83 us (6%)
  other arithmetic  3.19 us (4%)
  matrix products  1.34 us (2%)
    all_gather x1, waiting for transfers between devices, shards(): every = lax.all_gather(shard, 'chan', axis=0)  21.6 us
    all_to_all x1, blocking collectives, shards(): own = lax.all_to_all(spectra, 'tm', split_axis=0, concat_axis=0, tiled=True)  9.76 us
    reshape x1, local copies, waits for them, and re-layouts, shards(): own.reshape(parts, 2, pairs, 2, channels, -1).transpose(2, 4, 3, 1, 0, 5)  5.86 us
    ppermute x1, starting transfers between devices, shifted(): return lax.ppermute(value, axis, pairs)  4.83 us
    pallas_call x1, Pallas kernels, cross_spectra(): pl.pallas_call(cross_kernel, out_shape=jax.ShapeDtypeStruct((2, 2 * pairs...  3.84 us
    select_n x4, local copies, waits for them, and re-layouts, lhs_rows(): jnp.where(parity == b, part, zero).reshape(pairs, channels, lanes)  3.83 us
    transpose x1, local copies, waits for them, and re-layouts, shards(): own.reshape(parts, 2, pairs, 2, channels, -1).transpose(2, 4, 3, 1, 0, 5)  3.69 us
    pallas_call x1, Pallas kernels, whiten(): pl.pallas_call(fir_kernel, out_shape=jax.ShapeDtypeStruct(late.shape, jnp...  3.62 us
  transfers between devices with their start and end apart: 2, of which 1 were waited for; matrix products, arithmetic and copies ran while one was open for 11% of the time, Pallas kernels for 0%

profile of v13, /device:TPU:0, one launch (start us, length us, event | category | flops | bytes accessed | tf_op | source)
XLA Modules:
  0.0 80.6 jit_solution(657469095108738964)
XLA Ops:
  6.5 0.7 slice.9
  7.3 4.8 %collective-permute-start = (bf16[32,256]{1,0:T(8,128)(2,1)S(1)}, bf16[32,256]{1,0:T(8,128)(2,1)S(1)}, u32[]{:S(2)}, u32[]{:S(2)}) collective-permute-start(bf16[32,256]{1,0:T(8,128)(2,1)S(1)} %slice.9), channel_id=1, source_target_pairs={{0,8},{8,16},{16,24},{1,9},{9,17},{17,25},{2,10},{10,18},{18,26},{... | collective-permute-start | bytes 49160 | tf_op jit(solution)/shard_map/ppermute | solution.py:18
  12.1 1.7 %copy.22 = bf16[4,8,16,256]{3,2,1,0:T(8,128)(2,1)} copy(bf16[4,8,16,256]{3,1,2,0:T(8,128)(2,1)} %bitcast.21) | data formatting | bytes 524288
  13.8 0.6 copy-done
  14.4 3.6 %shard_map.37 = bf16[32,16,256]{2,1,0:T(8,128)(2,1)} custom-call(bf16[32,256]{1,0:T(8,128)(2,1)} %taps_ref.1, bf16[32,256]{1,0:T(8,128)(2,1)} %copy-done, bf16[32,16,256]{2,1,0:T(8,128)(2,1)} %bitcast.19), custom_call_target="tpu_custom_call" | custom-call | flops 134217728 | bytes 557056 | tf_op jit(solution)/shard_map/pallas_call | solution.py:88
  18.0 1.0 %reshape_reshape.8 = bf16[256,512]{1,0:T(8,128)(2,1)S(1)} reshape(bf16[32,16,256]{2,1,0:T(8,128)(2,1)} %shard_map.37) | data formatting | bytes 524288 | tf_op jit(solution)/shard_map/reshape;reshape | solution.py:108
  19.1 1.3 %fusion = bf16[512,256]{0,1:T(8,128)(2,1)S(1)} fusion(bf16[256,512]{1,0:T(8,128)(2,1)S(1)} %reshape_reshape.8, bf16[512,512]{1,0:T(8,128)(2,1)} %constant.8.clone), kind=kOutput, calls=%fused_computation.1 | convolution fusion | flops 134348800 | bytes 1048576 | tf_op jit(solution)/shard_map/xn,nq->qx/dot_general | solution.py:115
  20.4 0.1 copy.21
  20.5 9.8 %all_to_all.5 = bf16[4,128,256]{2,1,0:T(8,128)(2,1)S(1)} all-to-all(bf16[4,128,256]{2,1,0:T(8,128)(2,1)S(1)} %bitcast.20), channel_id=1, replica_groups=mesh['tm'=4,'chan'=8] {'tm'}, dimensions={0} | all-to-all | bytes 524288 | tf_op jit(solution)/shard_map/all_to_all | solution.py:119
  30.3 5.9 %reshape.58 = bf16[4,2,32,2,32,8]{5,4,3,2,1,0:T(8,128)(2,1)} reshape(bf16[4,128,256]{2,1,0:T(8,128)(2,1)S(1)} %all_to_all.5) | data formatting | bytes 524288 | tf_op jit(solution)/shard_map/reshape | solution.py:121
  36.2 3.7 %copy.13 = bf16[32,32,2,2,4,8]{1,5,4,3,2,0:T(8,128)(2,1)S(1)} copy(bf16[32,32,2,2,4,8]{5,1,2,0,3,4:T(8,128)(2,1)} %bitcast.13) | data formatting | bytes 524288 | tf_op jit(solution)/shard_map/transpose | solution.py:121
  39.9 1.0 %copy.20 = bf16[1,32,32,128]{3,2,1,0:T(8,128)(2,1)} copy(bf16[1,32,32,128]{2,3,1,0:T(8,128)(2,1)S(1)} %bitcast.14) | data formatting | bytes 524288 | tf_op jit(solution)/shard_map/all_gather;reshape | solution.py:123
  41.0 0.1 iota.36
  41.2 0.1 iota.40
  41.3 0.1 fusion.1
  41.4 0.2 pad_maximum_fusion
  41.6 1.7 %broadcast_select_fusion.2 = (bf16[32,1,32,128]{2,3,0,1:T(8,128)(2,1)S(1)}, bf16[32,1,32,128]{2,3,0,1:T(8,128)(2,1)S(1)}, bf16[32,1,32,128]{2,3,0,1:T(8,128)(2,1)}, bf16[32,1,32,128]{2,3,0,1:T(8,128)(2,1)}) fusion(bf16[32,1,32,128]{2,3,0,1:T(8,128)(2,1)S(1)} %bitcast.18, pred[128]{0:T(512)(128)(4,1)S(1)} %iota.36, pred[128]{0:T(512)(128)(4,1)S(1)} %iota.40, ...), kind=kLoop, calls=%fused_computation.6 | loop fusion | flops 524288 | bytes 1573120 | tf_op jit(solution)/shard_map/jit(_where)/select_n | solution.py:136
  43.3 1.6 %copy.15 = bf16[32,1,32,128]{3,2,1,0:T(8,128)(2,1)S(1)} copy(bf16[32,1,32,128]{2,3,0,1:T(8,128)(2,1)} %get-tuple-element.12) | data formatting | bytes 524288 | tf_op jit(solution)/shard_map/jit(_where)/select_n | solution.py:136
  44.9 1.6 %copy.16 = bf16[32,1,32,128]{3,2,1,0:T(8,128)(2,1)S(1)} copy(bf16[32,1,32,128]{2,3,0,1:T(8,128)(2,1)} %get-tuple-element.11) | data formatting | bytes 524288 | tf_op jit(solution)/shard_map/jit(_where)/select_n | solution.py:136
  46.5 0.3 copy.17
  46.8 0.3 copy.18
  47.2 1.1 %pad_maximum_fusion.1 = bf16[32,4,32,128]{3,2,1,0:T(8,128)(2,1)} fusion(bf16[32,1,32,128]{3,2,1,0:T(8,128)(2,1)S(1)} %copy.18, bf16[32,1,32,128]{3,2,1,0:T(8,128)(2,1)S(1)} %copy.17, bf16[32,1,32,128]{3,2,1,0:T(8,128)(2,1)S(1)} %copy.16, bf16[32,1,32,128]{3,2,1,0:T(8,128)(2,1)S(1)} %copy.15), kind=kLoop, calls=%fused_computation.3 | loop fusion | flops 1572864 | bytes 2097152 | tf_op jit(solution)/shard_map/stack | solution.py:137
  48.3 21.6 %all-gather.2.cloned.1.call-done.every_ref = bf16[8,32,32,128]{3,2,1,0:T(8,128)(2,1)} async-done(((bf16[1,32,32,128]{3,2,1,0:T(8,128)(2,1)}), bf16[8,32,32,128]{3,2,1,0:T(8,128)(2,1)}) %all-gather.2.cloned.1.call-update) | async-done | bytes 2097168 | tf_op jit(solution)/shard_map/all_gather | solution.py:123
  69.9 3.8 %shard_map.38 = f32[2,64,32,256]{3,2,1,0:T(8,128)} custom-call(bf16[32,128,128]{2,1,0:T(8,128)(2,1)} %bitcast.17, bf16[8,32,32,128]{3,2,1,0:T(8,128)(2,1)} %all-gather.2.cloned.1.call-done.every_ref), custom_call_target="tpu_custom_call" | custom-call | flops 268435456 | bytes 7340032 | tf_op jit(solution)/shard_map/pallas_call | solution.py:157
  (8 shorter events, 0.2 us)
Async XLA Ops:
  6.5 63.4 %all-gather.2.cloned.1.call-start = ((), (), s32[]{:S(2)}) async-start(), calls=%async_computation.1 | async-start | bytes 2359296 | tf_op jit(solution)/shard_map/all_gather | solution.py:123
  7.3 6.5 %collective-permute-start = (bf16[32,256]{1,0:T(8,128)(2,1)S(1)}, bf16[32,256]{1,0:T(8,128)(2,1)S(1)}, u32[]{:S(2)}, u32[]{:S(2)}) collective-permute-start(bf16[32,256]{1,0:T(8,128)(2,1)S(1)} %slice.9), channel_id=1, source_target_pairs={{0,8},{8,16},{16,24},{1,9},{9,17},{17,25},{2,10},{10,18},{18,26},{... | collective-permute-start | bytes 49160 | tf_op jit(solution)/shard_map/ppermute | solution.py:18
  13.8 0.6 copy-start
Sparse Core Ops, SparseCore 0:
  41.0 28.8 all-gather.1

commit v14 on v13

--- a/solution.py
+++ b/solution.py
@@ -118,7 +118,9 @@
     spectra = spectra.reshape(parts, spectra.shape[0] // parts, spectra.shape[1])
     own = lax.all_to_all(spectra, "tm", split_axis=0, concat_axis=0, tiled=True)
     pairs = bins // parts // 2
-    shard = own.reshape(parts, 2, pairs, 2, channels, -1).transpose(2, 4, 3, 1, 0, 5)
+    rows = own.reshape(parts, 2, pairs, 2, own.shape[-1]).transpose(2, 3, 1, 0, 4)
+    segs = own.shape[-1] // channels
+    shard = rows.reshape(pairs, 4 * parts, channels, segs).transpose(0, 2, 1, 3)
     shard = shard.reshape(pairs, channels, -1)
     every = lax.all_gather(shard, "chan", axis=0)
     return cross_spectra(lhs_rows(shard), every)

time: 81.1 us -> 74.2 us (0.915)
  local copies, waits for them, and re-layouts: 18.9 us -> 12.1 us
    reshape x1 -> x0, local copies, waits for them, and re-layouts: 5.86 us -> none  [shards(): own.reshape(parts, 2, pairs, 2, channels, -1).transpose(2, 4, 3, 1, 0, 5)]
    transpose x1 -> x2, local copies, waits for them, and re-layouts: 3.69 us -> 2.54 us  [the longest x1 2.05 us: shards(): shard = rows.reshape(pairs, 4 * parts, channels, segs).transpose(0, 2, 1, 3)]
  transfers between devices with their start and end apart: 2 -> 2, of which waited for: 1 -> 1; matrix products, arithmetic and copies ran while one was open for 11% -> 12% of each run, Pallas kernels for 0% -> 0%
where the time goes in v14:
time: 74.2 us; the launch traced here: 73.8 us
  waiting for transfers between devices  21.6 us (29%)
  between operations  13.5 us (18%)
  local copies, waits for them, and re-layouts  12.1 us (16%)
  blocking collectives  9.76 us (13%)
  Pallas kernels  7.49 us (10%)
  starting transfers between devices  4.83 us (7%)
  other arithmetic  3.19 us (4%)
  matrix products  1.34 us (2%)
    all_gather x1, waiting for transfers between devices, shards(): every = lax.all_gather(shard, 'chan', axis=0)  21.6 us
    all_to_all x1, blocking collectives, shards(): own = lax.all_to_all(spectra, 'tm', split_axis=0, concat_axis=0, tiled=True)  9.76 us
    ppermute x1, starting transfers between devices, shifted(): return lax.ppermute(value, axis, pairs)  4.83 us
    pallas_call x1, Pallas kernels, cross_spectra(): pl.pallas_call(cross_kernel, out_shape=jax.ShapeDtypeStruct((2, 2 * pairs...  3.87 us
    select_n x4, local copies, waits for them, and re-layouts, lhs_rows(): jnp.where(parity == b, part, zero).reshape(pairs, channels, lanes)  3.83 us
    pallas_call x1, Pallas kernels, whiten(): pl.pallas_call(fir_kernel, out_shape=jax.ShapeDtypeStruct(late.shape, jnp...  3.62 us
    unnamed x3, local copies, waits for them, and re-layouts  2.3 us
    transpose x1, local copies, waits for them, and re-layouts, shards(): shard = rows.reshape(pairs, 4 * parts, channels, segs).transpose(0, 2, 1, 3)  2.05 us
  transfers between devices with their start and end apart: 2, of which 1 were waited for; matrix products, arithmetic and copies ran while one was open for 12% of the time, Pallas kernels for 0%

profile of v14, /device:TPU:0, one launch (start us, length us, event | category | flops | bytes accessed | tf_op | source)
XLA Modules:
  0.0 73.8 jit_solution(1583371738450621728)
XLA Ops:
  6.5 0.7 slice.9
  7.3 4.8 %collective-permute-start = (bf16[32,256]{1,0:T(8,128)(2,1)S(1)}, bf16[32,256]{1,0:T(8,128)(2,1)S(1)}, u32[]{:S(2)}, u32[]{:S(2)}) collective-permute-start(bf16[32,256]{1,0:T(8,128)(2,1)S(1)} %slice.9), channel_id=1, source_target_pairs={{0,8},{8,16},{16,24},{1,9},{9,17},{17,25},{2,10},{10,18},{18,26},{... | collective-permute-start | bytes 49160 | tf_op jit(solution)/shard_map/ppermute | solution.py:18
  12.1 1.7 %copy.25 = bf16[4,8,16,256]{3,2,1,0:T(8,128)(2,1)} copy(bf16[4,8,16,256]{3,1,2,0:T(8,128)(2,1)} %bitcast.28) | data formatting | bytes 524288
  13.8 0.6 copy-done
  14.4 3.6 %shard_map.37 = bf16[32,16,256]{2,1,0:T(8,128)(2,1)} custom-call(bf16[32,256]{1,0:T(8,128)(2,1)} %taps_ref.1, bf16[32,256]{1,0:T(8,128)(2,1)} %copy-done, bf16[32,16,256]{2,1,0:T(8,128)(2,1)} %bitcast.26), custom_call_target="tpu_custom_call" | custom-call | flops 134217728 | bytes 557056 | tf_op jit(solution)/shard_map/pallas_call | solution.py:88
  18.0 1.0 %reshape_reshape.8 = bf16[256,512]{1,0:T(8,128)(2,1)S(1)} reshape(bf16[32,16,256]{2,1,0:T(8,128)(2,1)} %shard_map.37) | data formatting | bytes 524288 | tf_op jit(solution)/shard_map/reshape;reshape | solution.py:108
  19.1 1.3 %fusion = bf16[512,256]{0,1:T(8,128)(2,1)S(1)} fusion(bf16[256,512]{1,0:T(8,128)(2,1)S(1)} %reshape_reshape.8, bf16[512,512]{1,0:T(8,128)(2,1)} %constant.8.clone), kind=kOutput, calls=%fused_computation.1 | convolution fusion | flops 134348800 | bytes 1048576 | tf_op jit(solution)/shard_map/xn,nq->qx/dot_general | solution.py:115
  20.4 0.1 copy.24
  20.5 9.8 %all_to_all.5 = bf16[4,128,256]{2,1,0:T(8,128)(2,1)S(1)} all-to-all(bf16[4,128,256]{2,1,0:T(8,128)(2,1)S(1)} %bitcast.27), channel_id=1, replica_groups=mesh['tm'=4,'chan'=8] {'tm'}, dimensions={0} | all-to-all | bytes 524288 | tf_op jit(solution)/shard_map/all_to_all | solution.py:119
  30.3 0.2 copy.14
  30.5 0.5 copy.15
  31.0 2.0 %copy.16 = bf16[32,32,16,8]{1,3,2,0:T(8,128)(2,1)S(1)} copy(bf16[32,32,16,8]{0,3,1,2:T(8,128)(2,1)S(1)} %bitcast.23) | data formatting | bytes 524288 | tf_op jit(solution)/shard_map/transpose | solution.py:123
  33.1 1.0 %copy.23 = bf16[1,32,32,128]{3,2,1,0:T(8,128)(2,1)} copy(bf16[1,32,32,128]{2,3,1,0:T(8,128)(2,1)S(1)} %bitcast.20) | data formatting | bytes 524288 | tf_op jit(solution)/shard_map/all_gather;reshape | solution.py:125
  34.2 0.1 iota.36
  34.5 0.1 fusion.1
  34.6 0.2 pad_maximum_fusion
  34.8 1.7 %broadcast_select_fusion.1 = (bf16[32,1,32,128]{2,3,0,1:T(8,128)(2,1)S(1)}, bf16[32,1,32,128]{2,3,0,1:T(8,128)(2,1)S(1)}, bf16[32,1,32,128]{2,3,0,1:T(8,128)(2,1)}, bf16[32,1,32,128]{2,3,0,1:T(8,128)(2,1)}) fusion(bf16[32,1,32,128]{2,3,0,1:T(8,128)(2,1)S(1)} %bitcast.24, pred[128]{0:T(512)(128)(4,1)S(1)} %iota.36, pred[128]{0:T(512)(128)(4,1)S(1)} %iota.40, ...), kind=kLoop, calls=%fused_computation.7 | loop fusion | flops 524288 | bytes 1573120 | tf_op jit(solution)/shard_map/jit(_where)/select_n | solution.py:138
  36.5 1.6 %copy.18 = bf16[32,1,32,128]{3,2,1,0:T(8,128)(2,1)S(1)} copy(bf16[32,1,32,128]{2,3,0,1:T(8,128)(2,1)} %get-tuple-element.12) | data formatting | bytes 524288 | tf_op jit(solution)/shard_map/jit(_where)/select_n | solution.py:138
  38.1 1.6 %copy.19 = bf16[32,1,32,128]{3,2,1,0:T(8,128)(2,1)S(1)} copy(bf16[32,1,32,128]{2,3,0,1:T(8,128)(2,1)} %get-tuple-element.11) | data formatting | bytes 524288 | tf_op jit(solution)/shard_map/jit(_where)/select_n | solution.py:138
  39.7 0.3 copy.20
  40.0 0.3 copy.21
  40.4 1.1 %pad_maximum_fusion.1 = bf16[32,4,32,128]{3,2,1,0:T(8,128)(2,1)} fusion(bf16[32,1,32,128]{3,2,1,0:T(8,128)(2,1)S(1)} %copy.21, bf16[32,1,32,128]{3,2,1,0:T(8,128)(2,1)S(1)} %copy.20, bf16[32,1,32,128]{3,2,1,0:T(8,128)(2,1)S(1)} %copy.19, bf16[32,1,32,128]{3,2,1,0:T(8,128)(2,1)S(1)} %copy.18), kind=kLoop, calls=%fused_computation.3 | loop fusion | flops 1572864 | bytes 2097152 | tf_op jit(solution)/shard_map/stack | solution.py:139
  41.5 21.6 %all-gather.2.cloned.1.call-done.every_ref = bf16[8,32,32,128]{3,2,1,0:T(8,128)(2,1)} async-done(((bf16[1,32,32,128]{3,2,1,0:T(8,128)(2,1)}), bf16[8,32,32,128]{3,2,1,0:T(8,128)(2,1)}) %all-gather.2.cloned.1.call-update) | async-done | bytes 2097168 | tf_op jit(solution)/shard_map/all_gather | solution.py:125
  63.1 3.9 %shard_map.38 = f32[2,64,32,256]{3,2,1,0:T(8,128)} custom-call(bf16[32,128,128]{2,1,0:T(8,128)(2,1)} %bitcast.22, bf16[8,32,32,128]{3,2,1,0:T(8,128)(2,1)} %all-gather.2.cloned.1.call-done.every_ref), custom_call_target="tpu_custom_call" | custom-call | flops 268435456 | bytes 7340032 | tf_op jit(solution)/shard_map/pallas_call | solution.py:159
  (9 shorter events, 0.3 us)
Async XLA Ops:
  6.5 56.6 %all-gather.2.cloned.1.call-start = ((), (), s32[]{:S(2)}) async-start(), calls=%async_computation.1 | async-start | bytes 2359296 | tf_op jit(solution)/shard_map/all_gather | solution.py:125
  7.3 6.5 %collective-permute-start = (bf16[32,256]{1,0:T(8,128)(2,1)S(1)}, bf16[32,256]{1,0:T(8,128)(2,1)S(1)}, u32[]{:S(2)}, u32[]{:S(2)}) collective-permute-start(bf16[32,256]{1,0:T(8,128)(2,1)S(1)} %slice.9), channel_id=1, source_target_pairs={{0,8},{8,16},{16,24},{1,9},{9,17},{17,25},{2,10},{10,18},{18,26},{... | collective-permute-start | bytes 49160 | tf_op jit(solution)/shard_map/ppermute | solution.py:18
  13.8 0.6 copy-start
Sparse Core Ops, SparseCore 0:
  34.2 28.8 all-gather.1

commit v15 on v14

--- a/solution.py
+++ b/solution.py
@@ -110,28 +110,29 @@
     table = make_table()
     bins = table.shape[2]
     table = jnp.asarray(
-        table.reshape(SEG, 2, parts, bins // parts).transpose(0, 2, 1, 3).reshape(SEG, 2 * bins)
+        table.reshape(SEG, 2, parts, bins // parts // 2, 2)
+        .transpose(0, 2, 3, 4, 1)
+        .reshape(SEG, 2 * bins)
     )
     spectra = jnp.einsum(
         "xn,nq->qx", segments, table, preferred_element_type=jnp.float32
     ).astype(jnp.bfloat16)
-    spectra = spectra.reshape(parts, spectra.shape[0] // parts, spectra.shape[1])
-    own = lax.all_to_all(spectra, "tm", split_axis=0, concat_axis=0, tiled=True)
     pairs = bins // parts // 2
-    rows = own.reshape(parts, 2, pairs, 2, own.shape[-1]).transpose(2, 3, 1, 0, 4)
+    spectra = spectra.reshape(parts, pairs, 4, spectra.shape[1])
+    own = lax.all_to_all(spectra, "tm", split_axis=0, concat_axis=1, tiled=False)
     segs = own.shape[-1] // channels
-    shard = rows.reshape(pairs, 4 * parts, channels, segs).transpose(0, 2, 1, 3)
+    shard = own.reshape(pairs, 4 * parts, channels, segs).transpose(0, 2, 1, 3)
     shard = shard.reshape(pairs, channels, -1)
     every = lax.all_gather(shard, "chan", axis=0)
-    return cross_spectra(lhs_rows(shard), every)
+    return cross_spectra(lhs_rows(shard, parts), every)
 
 
-def lhs_rows(shard):
+def lhs_rows(shard, parts):
     pairs, channels, lanes = shard.shape
-    split = shard.reshape(pairs, channels, 2, 2, lanes // 4)
-    parity = lax.broadcasted_iota(jnp.int32, split.shape, 2)
+    split = shard.reshape(pairs, channels, parts, 2, 2, lanes // 4 // parts)
+    parity = lax.broadcasted_iota(jnp.int32, split.shape, 3)
     zero = jnp.zeros_like(split)
-    swapped = jnp.concatenate([split[:, :, :, 1:], -split[:, :, :, :1]], axis=3)
+    swapped = jnp.concatenate([split[:, :, :, :, 1:], -split[:, :, :, :, :1]], axis=4)
     rows = []
     for part in (split, swapped):
         for b in range(2):

time: 74.2 us -> 74.1 us (level)
  waiting for transfers between devices: 21.6 us -> 19.3 us
  local copies, waits for them, and re-layouts: 12.1 us -> 14.2 us
    all_gather x1, waiting for transfers between devices: 21.6 us -> 19.3 us  [shards(): every = lax.all_gather(shard, 'chan', axis=0)]
    unnamed x3 -> x5, local copies, waits for them, and re-layouts: 2.3 us -> 4.37 us
    transpose x2 -> x1, local copies, waits for them, and re-layouts: 2.54 us -> 2.05 us  [shards(): shard = own.reshape(pairs, 4 * parts, channels, segs).transpose(0, 2, 1, 3)]
  transfers between devices with their start and end apart: 2 -> 2, of which waited for: 1 -> 1; matrix products, arithmetic and copies ran while one was open for 12% -> 15% of each run, Pallas kernels for 0% -> 0%
where the time goes in v15:
time: 74.1 us; the launch traced here: 73.7 us
  waiting for transfers between devices  19.3 us (26%)
  local copies, waits for them, and re-layouts  14.2 us (19%)
  between operations  13.5 us (18%)
  blocking collectives  9.76 us (13%)
  Pallas kernels  7.46 us (10%)
  starting transfers between devices  4.83 us (7%)
  other arithmetic  3.24 us (4%)
  matrix products  1.34 us (2%)
    all_gather x1, waiting for transfers between devices, shards(): every = lax.all_gather(shard, 'chan', axis=0)  19.3 us
    all_to_all x1, blocking collectives, shards(): lax.all_to_all(spectra, 'tm', split_axis=0, concat_axis=1, tiled=False)  9.76 us
    ppermute x1, starting transfers between devices, shifted(): return lax.ppermute(value, axis, pairs)  4.83 us
    unnamed x5, local copies, waits for them, and re-layouts  4.37 us
    select_n x4, local copies, waits for them, and re-layouts, lhs_rows(): jnp.where(parity == b, part, zero).reshape(pairs, channels, lanes)  3.87 us
    pallas_call x1, Pallas kernels, cross_spectra(): pl.pallas_call(cross_kernel, out_shape=jax.ShapeDtypeStruct((2, 2 * pairs...  3.84 us
    pallas_call x1, Pallas kernels, whiten(): pl.pallas_call(fir_kernel, out_shape=jax.ShapeDtypeStruct(late.shape, jnp...  3.62 us
    transpose x1, local copies, waits for them, and re-layouts, shards(): shard = own.reshape(pairs, 4 * parts, channels, segs).transpose(0, 2, 1, 3)  2.05 us
  transfers between devices with their start and end apart: 2, of which 1 were waited for; matrix products, arithmetic and copies ran while one was open for 15% of the time, Pallas kernels for 0%

profile of v15, /device:TPU:0, one launch (start us, length us, event | category | flops | bytes accessed | tf_op | source)
XLA Modules:
  0.0 73.7 jit_solution(14062152545176282724)
XLA Ops:
  6.5 0.7 slice.9
  7.3 4.8 %collective-permute-start = (bf16[32,256]{1,0:T(8,128)(2,1)S(1)}, bf16[32,256]{1,0:T(8,128)(2,1)S(1)}, u32[]{:S(2)}, u32[]{:S(2)}) collective-permute-start(bf16[32,256]{1,0:T(8,128)(2,1)S(1)} %slice.9), channel_id=1, source_target_pairs={{0,8},{8,16},{16,24},{1,9},{9,17},{17,25},{2,10},{10,18},{18,26},{... | collective-permute-start | bytes 49160 | tf_op jit(solution)/shard_map/ppermute | solution.py:18
  12.1 1.7 %copy.28 = bf16[4,8,16,256]{3,2,1,0:T(8,128)(2,1)} copy(bf16[4,8,16,256]{3,1,2,0:T(8,128)(2,1)} %bitcast.29) | data formatting | bytes 524288
  13.8 0.6 copy-done
  14.4 3.6 %shard_map.37 = bf16[32,16,256]{2,1,0:T(8,128)(2,1)} custom-call(bf16[32,256]{1,0:T(8,128)(2,1)} %taps_ref.1, bf16[32,256]{1,0:T(8,128)(2,1)} %copy-done, bf16[32,16,256]{2,1,0:T(8,128)(2,1)} %bitcast.27), custom_call_target="tpu_custom_call" | custom-call | flops 134217728 | bytes 557056 | tf_op jit(solution)/shard_map/pallas_call | solution.py:88
  18.0 1.0 %reshape_reshape.8 = bf16[256,512]{1,0:T(8,128)(2,1)S(1)} reshape(bf16[32,16,256]{2,1,0:T(8,128)(2,1)} %shard_map.37) | data formatting | bytes 524288 | tf_op jit(solution)/shard_map/reshape;reshape | solution.py:108
  19.1 1.3 %fusion = bf16[512,256]{0,1:T(8,128)(2,1)S(1)} fusion(bf16[256,512]{1,0:T(8,128)(2,1)S(1)} %reshape_reshape.8, bf16[512,512]{1,0:T(8,128)(2,1)} %constant.8.clone), kind=kOutput, calls=%fused_computation.1 | convolution fusion | flops 134348800 | bytes 1048576 | tf_op jit(solution)/shard_map/xn,nq->qx/dot_general | solution.py:117
  20.4 0.1 copy.14
  20.6 9.8 %all_to_all.15 = bf16[4,32,1,4,256]{4,3,1,2,0:T(4,128)(2,1)S(1)} all-to-all(bf16[4,32,1,4,256]{4,3,1,2,0:T(4,128)(2,1)S(1)} %bitcast.28), channel_id=1, replica_groups=mesh['tm'=4,'chan'=8] {'tm'}, dimensions={0} | all-to-all | bytes 524288 | tf_op jit(solution)/shard_map/all_to_all | solution.py:122
  30.4 0.5 copy.16
  30.9 2.0 %copy.17 = bf16[32,32,16,8]{1,3,2,0:T(8,128)(2,1)S(1)} copy(bf16[32,32,16,8]{0,3,1,2:T(8,128)(2,1)S(1)} %bitcast.22) | data formatting | bytes 524288 | tf_op jit(solution)/shard_map/transpose | solution.py:124
  32.9 1.0 %copy.25 = bf16[1,32,32,128]{3,2,1,0:T(8,128)(2,1)} copy(bf16[1,32,32,128]{2,3,1,0:T(8,128)(2,1)S(1)} %bitcast.24) | data formatting | bytes 524288 | tf_op jit(solution)/shard_map/all_gather;reshape | solution.py:126
  34.5 1.0 %copy.27 = bf16[32,32,4,2,1,8]{1,5,4,3,2,0:T(8,128)(2,1)S(1)} copy(bf16[32,32,4,2,1,8]{0,5,1,4,3,2:T(8,128)(2,1)S(1)} %get-tuple-element.10) | data formatting | bytes 262144
  35.5 0.1 neg.3
  35.7 1.0 %copy.26 = bf16[32,32,4,2,1,8]{1,5,4,3,2,0:T(8,128)(2,1)S(1)} copy(bf16[32,32,4,2,1,8]{0,5,1,4,3,2:T(8,128)(2,1)S(1)} %get-tuple-element.9) | data formatting | bytes 262144
  36.7 0.2 pad_maximum_fusion
  36.9 1.7 %broadcast_select_fusion.1 = (bf16[32,1,32,128]{2,3,0,1:T(8,128)(2,1)S(1)}, bf16[32,1,32,128]{2,3,0,1:T(8,128)(2,1)S(1)}, bf16[32,1,32,128]{2,3,0,1:T(8,128)(2,1)}, bf16[32,1,32,128]{2,3,0,1:T(8,128)(2,1)}) fusion(bf16[32,1,32,128]{2,3,0,1:T(8,128)(2,1)S(1)} %bitcast.26, pred[128]{0:T(512)(128)(4,1)S(1)} %iota.36, pred[128]{0:T(512)(128)(4,1)S(1)} %iota.40, ...), kind=kLoop, calls=%fused_computation.7 | loop fusion | flops 524288 | bytes 1573120 | tf_op jit(solution)/shard_map/jit(_where)/select_n | solution.py:139
  38.7 1.6 %copy.20 = bf16[32,1,32,128]{3,2,1,0:T(8,128)(2,1)S(1)} copy(bf16[32,1,32,128]{2,3,0,1:T(8,128)(2,1)} %get-tuple-element.12) | data formatting | bytes 524288 | tf_op jit(solution)/shard_map/jit(_where)/select_n | solution.py:139
  40.2 1.6 %copy.21 = bf16[32,1,32,128]{3,2,1,0:T(8,128)(2,1)S(1)} copy(bf16[32,1,32,128]{2,3,0,1:T(8,128)(2,1)} %get-tuple-element.11) | data formatting | bytes 524288 | tf_op jit(solution)/shard_map/jit(_where)/select_n | solution.py:139
  41.9 0.3 copy.22
  42.2 0.3 copy.23
  42.6 1.1 %pad_maximum_fusion.1 = bf16[32,4,32,128]{3,2,1,0:T(8,128)(2,1)} fusion(bf16[32,1,32,128]{3,2,1,0:T(8,128)(2,1)S(1)} %copy.23, bf16[32,1,32,128]{3,2,1,0:T(8,128)(2,1)S(1)} %copy.22, bf16[32,1,32,128]{3,2,1,0:T(8,128)(2,1)S(1)} %copy.21, bf16[32,1,32,128]{3,2,1,0:T(8,128)(2,1)S(1)} %copy.20), kind=kLoop, calls=%fused_computation.3 | loop fusion | flops 1572864 | bytes 2097152 | tf_op jit(solution)/shard_map/stack | solution.py:140
  43.7 19.3 %all-gather.2.cloned.1.call-done.every_ref = bf16[8,32,32,128]{3,2,1,0:T(8,128)(2,1)} async-done(((bf16[1,32,32,128]{3,2,1,0:T(8,128)(2,1)}), bf16[8,32,32,128]{3,2,1,0:T(8,128)(2,1)}) %all-gather.2.cloned.1.call-update) | async-done | bytes 2097168 | tf_op jit(solution)/shard_map/all_gather | solution.py:126
  63.0 3.8 %shard_map.38 = f32[2,64,32,256]{3,2,1,0:T(8,128)} custom-call(bf16[32,128,128]{2,1,0:T(8,128)(2,1)} %bitcast.25, bf16[8,32,32,128]{3,2,1,0:T(8,128)(2,1)} %all-gather.2.cloned.1.call-done.every_ref), custom_call_target="tpu_custom_call" | custom-call | flops 268435456 | bytes 7340032 | tf_op jit(solution)/shard_map/pallas_call | solution.py:160
  (12 shorter events, 0.5 us)
Async XLA Ops:
  6.5 56.4 %all-gather.2.cloned.1.call-start = ((), (), s32[]{:S(2)}) async-start(), calls=%async_computation.1 | async-start | bytes 2359296 | tf_op jit(solution)/shard_map/all_gather | solution.py:126
  7.3 6.5 %collective-permute-start = (bf16[32,256]{1,0:T(8,128)(2,1)S(1)}, bf16[32,256]{1,0:T(8,128)(2,1)S(1)}, u32[]{:S(2)}, u32[]{:S(2)}) collective-permute-start(bf16[32,256]{1,0:T(8,128)(2,1)S(1)} %slice.9), channel_id=1, source_target_pairs={{0,8},{8,16},{16,24},{1,9},{9,17},{17,25},{2,10},{10,18},{18,26},{... | collective-permute-start | bytes 49160 | tf_op jit(solution)/shard_map/ppermute | solution.py:18
  13.8 0.6 copy-start
Sparse Core Ops, SparseCore 0:
  34.1 28.8 all-gather.1

commit v16 on v15

--- a/solution.py
+++ b/solution.py
@@ -1,3 +1,4 @@
+import functools
 import math
 
 import jax
@@ -124,54 +125,54 @@
     shard = own.reshape(pairs, 4 * parts, channels, segs).transpose(0, 2, 1, 3)
     shard = shard.reshape(pairs, channels, -1)
     every = lax.all_gather(shard, "chan", axis=0)
-    return cross_spectra(lhs_rows(shard, parts), every)
+    return cross_spectra(shard, every, parts)
 
 
-def lhs_rows(shard, parts):
-    pairs, channels, lanes = shard.shape
-    split = shard.reshape(pairs, channels, parts, 2, 2, lanes // 4 // parts)
-    parity = lax.broadcasted_iota(jnp.int32, split.shape, 3)
-    zero = jnp.zeros_like(split)
-    swapped = jnp.concatenate([split[:, :, :, :, 1:], -split[:, :, :, :, :1]], axis=4)
-    rows = []
-    for part in (split, swapped):
-        for b in range(2):
-            rows.append(jnp.where(parity == b, part, zero).reshape(pairs, channels, lanes))
-    return jnp.stack(rows, axis=1).reshape(pairs, 4 * channels, lanes)
-
-
-def cross_kernel(lhs_ref, every_ref, out_ref):
+def cross_kernel(parts, own_ref, every_ref, out_ref):
     sources, count, channels, lanes = every_ref.shape
+    segs = lanes // 4 // parts
     factor = 1.0 / (lanes // 4 * SEG)
+    lane = lax.broadcasted_iota(jnp.int32, (channels, lanes), 1)
+    parity = (lane // (2 * segs)) % 2
+    second = (lane // segs) % 2 == 1
     for t in range(count):
+        own = own_ref[t].astype(jnp.float32)
+        later = pltpu.roll(own, lanes - segs, 1)
+        earlier = pltpu.roll(own, segs, 1)
+        swapped = jnp.where(second, -earlier, later)
+        rows = []
+        for part in (own, swapped):
+            for b in range(2):
+                rows.append(jnp.where(parity == b, part, 0.0))
+        lhs = jnp.concatenate(rows, axis=0).astype(jnp.bfloat16)
         rhs = every_ref[:, t].reshape(sources * channels, lanes)
         prod = lax.dot_general(
-            lhs_ref[t], rhs, (((1,), (1,)), ((), ())), preferred_element_type=jnp.float32
+            lhs, rhs, (((1,), (1,)), ((), ())), preferred_element_type=jnp.float32
         )
         prod = prod * factor
         for q in range(4):
             out_ref[q // 2, 2 * t + q % 2] = prod[q * channels:(q + 1) * channels]
 
 
-def cross_spectra(lhs, every):
+def cross_spectra(own, every, parts):
     sources, pairs, channels, lanes = every.shape
     step = 16 if pairs % 16 == 0 else pairs
     wide = sources * channels
     return pl.pallas_call(
-        cross_kernel,
+        functools.partial(cross_kernel, parts),
         out_shape=jax.ShapeDtypeStruct((2, 2 * pairs, channels, wide), jnp.float32),
         grid=(pairs // step,),
         in_specs=[
-            pl.BlockSpec((step, 4 * channels, lanes), lambda g: (g, 0, 0)),
+            pl.BlockSpec((step, channels, lanes), lambda g: (g, 0, 0)),
             pl.BlockSpec((sources, step, channels, lanes), lambda g: (0, g, 0, 0)),
         ],
         out_specs=pl.BlockSpec((2, 2 * step, channels, wide), lambda g: (0, g, 0, 0)),
         cost_estimate=pl.CostEstimate(
             flops=2 * pairs * 4 * channels * lanes * wide,
-            bytes_accessed=lhs.size * 2 + every.size * 2 + 2 * 2 * pairs * channels * wide * 4,
+            bytes_accessed=own.size * 2 + every.size * 2 + 2 * 2 * pairs * channels * wide * 4,
             transcendentals=0,
         ),
-    )(lhs, every)
+    )(own, every)
 
 
 def solution(mesh):

time: 74.1 us -> 74 us (level)
  waiting for transfers between devices: 19.3 us -> 28 us
  local copies, waits for them, and re-layouts: 14.2 us -> 8.87 us
  other arithmetic: 3.24 us -> 0 us
    all_gather x1, waiting for transfers between devices: 19.3 us -> 27.9 us  [shards(): every = lax.all_gather(shard, 'chan', axis=0)]
    select_n x4 -> x0, local copies, waits for them, and re-layouts: 3.87 us -> none  [lhs_rows(): jnp.where(parity == b, part, zero).reshape(pairs, channels, lanes)]
    unnamed x5 -> x3, local copies, waits for them, and re-layouts: 4.37 us -> 2.3 us
    select_n x1 -> x0, other arithmetic: 1.73 us -> none  [lhs_rows(): jnp.where(parity == b, part, zero).reshape(pairs, channels, lanes)]
    another operation x1 -> x0, other arithmetic: 1.13 us -> none  [lhs_rows(): return jnp.stack(rows, axis=1).reshape(pairs, 4 * channels, lanes)]
    reshape x0 -> x1, local copies, waits for them, and re-layouts: none -> 1.03 us  [shards(): shard = shard.reshape(pairs, channels, -1)]
  transfers between devices with their start and end apart: 2 -> 2, of which waited for: 1 -> 1; matrix products, arithmetic and copies ran while one was open for 15% -> 4% of each run, Pallas kernels for 0% -> 0%
where the time goes in v16:
time: 74 us; the launch traced here: 73.6 us
  waiting for transfers between devices  28 us (38%)
  between operations  13.4 us (18%)
  blocking collectives  9.76 us (13%)
  local copies, waits for them, and re-layouts  8.87 us (12%)
  Pallas kernels  7.41 us (10%)
  starting transfers between devices  4.83 us (7%)
  matrix products  1.34 us (2%)
    all_gather x1, waiting for transfers between devices, shards(): every = lax.all_gather(shard, 'chan', axis=0)  27.9 us
    all_to_all x1, blocking collectives, shards(): lax.all_to_all(spectra, 'tm', split_axis=0, concat_axis=1, tiled=False)  9.76 us
    ppermute x1, starting transfers between devices, shifted(): return lax.ppermute(value, axis, pairs)  4.83 us
    pallas_call x1, Pallas kernels, cross_spectra(): pl.pallas_call(functools.partial(cross_kernel, parts), out_shape=jax.Shap...  3.79 us
    pallas_call x1, Pallas kernels, whiten(): pl.pallas_call(fir_kernel, out_shape=jax.ShapeDtypeStruct(late.shape, jnp...  3.62 us
    unnamed x3, local copies, waits for them, and re-layouts  2.3 us
    transpose x1, local copies, waits for them, and re-layouts, shards(): shard = own.reshape(pairs, 4 * parts, channels, segs).transpose(0, 2, 1, 3)  2.05 us
  transfers between devices with their start and end apart: 2, of which 1 were waited for; matrix products, arithmetic and copies ran while one was open for 4% of the time, Pallas kernels for 0%

profile of v16, /device:TPU:0, one launch (start us, length us, event | category | flops | bytes accessed | tf_op | source)
XLA Modules:
  0.0 73.6 jit_solution(4807640481665105259)
XLA Ops:
  6.5 0.0 all-gather.2.cloned.1.call-start
  6.5 0.7 slice.3
  7.3 4.8 %collective-permute-start = (bf16[32,256]{1,0:T(8,128)(2,1)S(1)}, bf16[32,256]{1,0:T(8,128)(2,1)S(1)}, u32[]{:S(2)}, u32[]{:S(2)}) collective-permute-start(bf16[32,256]{1,0:T(8,128)(2,1)S(1)} %slice.3), channel_id=1, source_target_pairs={{0,8},{8,16},{16,24},{1,9},{9,17},{17,25},{2,10},{10,18},{18,26},{... | collective-permute-start | bytes 49160 | tf_op jit(solution)/shard_map/ppermute | solution.py:19
  12.1 1.7 %copy.17 = bf16[4,8,16,256]{3,2,1,0:T(8,128)(2,1)} copy(bf16[4,8,16,256]{3,1,2,0:T(8,128)(2,1)} %bitcast.21) | data formatting | bytes 524288
  13.8 0.0 collective-permute-done.previous_ref
  13.8 0.0 copy-start
  13.8 0.6 copy-done
  14.4 3.6 %shard_map.37 = bf16[32,16,256]{2,1,0:T(8,128)(2,1)} custom-call(bf16[32,256]{1,0:T(8,128)(2,1)} %taps_ref.1, bf16[32,256]{1,0:T(8,128)(2,1)} %copy-done, bf16[32,16,256]{2,1,0:T(8,128)(2,1)} %bitcast.19), custom_call_target="tpu_custom_call" | custom-call | flops 134217728 | bytes 557056 | tf_op jit(solution)/shard_map/pallas_call | solution.py:89
  18.0 1.0 %reshape_reshape.3 = bf16[256,512]{1,0:T(8,128)(2,1)S(1)} reshape(bf16[32,16,256]{2,1,0:T(8,128)(2,1)} %shard_map.37) | data formatting | bytes 524288 | tf_op jit(solution)/shard_map/reshape;reshape | solution.py:109
  19.1 1.3 %fusion = bf16[512,256]{0,1:T(8,128)(2,1)S(1)} fusion(bf16[256,512]{1,0:T(8,128)(2,1)S(1)} %reshape_reshape.3, bf16[512,512]{1,0:T(8,128)(2,1)} %constant.2.clone), kind=kOutput, calls=%fused_computation.1 | convolution fusion | flops 134348800 | bytes 1048576 | tf_op jit(solution)/shard_map/xn,nq->qx/dot_general | solution.py:118
  20.4 0.1 copy.10
  20.5 0.1 broadcast_in_dim_reshape.3
  20.6 9.8 %all_to_all.15 = bf16[4,32,1,4,256]{4,3,1,2,0:T(4,128)(2,1)S(1)} all-to-all(bf16[4,32,1,4,256]{4,3,1,2,0:T(4,128)(2,1)S(1)} %bitcast.20), channel_id=1, replica_groups=mesh['tm'=4,'chan'=8] {'tm'}, dimensions={0} | all-to-all | bytes 524288 | tf_op jit(solution)/shard_map/all_to_all | solution.py:123
  30.4 0.5 copy.12
  30.9 2.0 %copy.13 = bf16[32,32,16,8]{1,3,2,0:T(8,128)(2,1)S(1)} copy(bf16[32,32,16,8]{0,3,1,2:T(8,128)(2,1)S(1)} %bitcast.18) | data formatting | bytes 524288 | tf_op jit(solution)/shard_map/transpose | solution.py:125
  33.0 1.0 %copy.15 = bf16[1,32,32,128]{3,2,1,0:T(8,128)(2,1)} copy(bf16[1,32,32,128]{2,3,1,0:T(8,128)(2,1)S(1)} %bitcast.16) | data formatting | bytes 524288 | tf_op jit(solution)/shard_map/all_gather;reshape | solution.py:127
  34.0 0.0 all-gather.2.cloned.1.call-update
  34.0 1.0 %copy.16.own_ref = bf16[32,32,128]{2,1,0:T(8,128)(2,1)} copy(bf16[32,32,128]{1,2,0:T(8,128)(2,1)S(1)} %bitcast.17) | data formatting | bytes 524288 | tf_op jit(solution)/shard_map/reshape | solution.py:126
  35.0 27.9 %all-gather.2.cloned.1.call-done.every_ref = bf16[8,32,32,128]{3,2,1,0:T(8,128)(2,1)} async-done(((bf16[1,32,32,128]{3,2,1,0:T(8,128)(2,1)}), bf16[8,32,32,128]{3,2,1,0:T(8,128)(2,1)}) %all-gather.2.cloned.1.call-update) | async-done | bytes 2097168 | tf_op jit(solution)/shard_map/all_gather | solution.py:127
  63.0 3.8 %shard_map.38 = f32[2,64,32,256]{3,2,1,0:T(8,128)} custom-call(bf16[32,32,128]{2,1,0:T(8,128)(2,1)} %copy.16.own_ref, bf16[8,32,32,128]{3,2,1,0:T(8,128)(2,1)} %all-gather.2.cloned.1.call-done.every_ref), custom_call_target="tpu_custom_call" | custom-call | flops 268435456 | bytes 6553600 | tf_op jit(solution)/shard_map/pallas_call | solution.py:161
Async XLA Ops:
  6.5 56.4 %all-gather.2.cloned.1.call-start = ((), (), s32[]{:S(2)}) async-start(), calls=%async_computation.1 | async-start | bytes 2359296 | tf_op jit(solution)/shard_map/all_gather | solution.py:127
  7.3 6.5 %collective-permute-start = (bf16[32,256]{1,0:T(8,128)(2,1)S(1)}, bf16[32,256]{1,0:T(8,128)(2,1)S(1)}, u32[]{:S(2)}, u32[]{:S(2)}) collective-permute-start(bf16[32,256]{1,0:T(8,128)(2,1)S(1)} %slice.3), channel_id=1, source_target_pairs={{0,8},{8,16},{16,24},{1,9},{9,17},{17,25},{2,10},{10,18},{18,26},{... | collective-permute-start | bytes 49160 | tf_op jit(solution)/shard_map/ppermute | solution.py:19
  13.8 0.6 copy-start
Sparse Core Ops, SparseCore 0:
  34.1 28.8 all-gather.1

commit v17 on v16

--- a/solution.py
+++ b/solution.py
@@ -83,7 +83,7 @@
 
 def whiten(fir_taps, previous, late):
     channels, nblocks, tap_count = late.shape
-    group = 16 if channels % 16 == 0 else channels
+    group = channels
     block = pl.BlockSpec((group, nblocks, tap_count), lambda g: (g, 0, 0))
     rows = pl.BlockSpec((group, tap_count), lambda g: (g, 0))
     return pl.pallas_call(

time: 74 us -> 73.9 us (level)
  no operation moved by 1% of the time
where the time goes in v17:
time: 73.9 us; the launch traced here: 73.5 us
  waiting for transfers between devices  28 us (38%)
  between operations  13.4 us (18%)
  blocking collectives  9.76 us (13%)
  local copies, waits for them, and re-layouts  8.87 us (12%)
  Pallas kernels  7.3 us (10%)
  starting transfers between devices  4.83 us (7%)
  matrix products  1.34 us (2%)
    all_gather x1, waiting for transfers between devices, shards(): every = lax.all_gather(shard, 'chan', axis=0)  27.9 us
    all_to_all x1, blocking collectives, shards(): lax.all_to_all(spectra, 'tm', split_axis=0, concat_axis=1, tiled=False)  9.76 us
    ppermute x1, starting transfers between devices, shifted(): return lax.ppermute(value, axis, pairs)  4.83 us
    pallas_call x1, Pallas kernels, cross_spectra(): pl.pallas_call(functools.partial(cross_kernel, parts), out_shape=jax.Shap...  3.79 us
    pallas_call x1, Pallas kernels, whiten(): pl.pallas_call(fir_kernel, out_shape=jax.ShapeDtypeStruct(late.shape, jnp...  3.51 us
    unnamed x3, local copies, waits for them, and re-layouts  2.3 us
    transpose x1, local copies, waits for them, and re-layouts, shards(): shard = own.reshape(pairs, 4 * parts, channels, segs).transpose(0, 2, 1, 3)  2.05 us
  transfers between devices with their start and end apart: 2, of which 1 were waited for; matrix products, arithmetic and copies ran while one was open for 4% of the time, Pallas kernels for 0%

profile of v17, /device:TPU:0, one launch (start us, length us, event | category | flops | bytes accessed | tf_op | source)
XLA Modules:
  0.0 73.5 jit_solution(16656091398949031939)
XLA Ops:
  6.5 0.0 all-gather.2.cloned.1.call-start
  6.5 0.7 slice.3
  7.3 4.8 %collective-permute-start = (bf16[32,256]{1,0:T(8,128)(2,1)S(1)}, bf16[32,256]{1,0:T(8,128)(2,1)S(1)}, u32[]{:S(2)}, u32[]{:S(2)}) collective-permute-start(bf16[32,256]{1,0:T(8,128)(2,1)S(1)} %slice.3), channel_id=1, source_target_pairs={{0,8},{8,16},{16,24},{1,9},{9,17},{17,25},{2,10},{10,18},{18,26},{... | collective-permute-start | bytes 49160 | tf_op jit(solution)/shard_map/ppermute | solution.py:19
  12.1 1.7 %copy.17 = bf16[4,8,16,256]{3,2,1,0:T(8,128)(2,1)} copy(bf16[4,8,16,256]{3,1,2,0:T(8,128)(2,1)} %bitcast.21) | data formatting | bytes 524288
  13.8 0.0 collective-permute-done.previous_ref
  13.8 0.0 copy-start
  13.8 0.6 copy-done
  14.4 3.5 %shard_map.37 = bf16[32,16,256]{2,1,0:T(8,128)(2,1)} custom-call(bf16[32,256]{1,0:T(8,128)(2,1)} %taps_ref.1, bf16[32,256]{1,0:T(8,128)(2,1)} %copy-done, bf16[32,16,256]{2,1,0:T(8,128)(2,1)} %bitcast.19), custom_call_target="tpu_custom_call" | custom-call | flops 134217728 | bytes 557056 | tf_op jit(solution)/shard_map/pallas_call | solution.py:89
  17.9 1.0 %reshape_reshape.3 = bf16[256,512]{1,0:T(8,128)(2,1)S(1)} reshape(bf16[32,16,256]{2,1,0:T(8,128)(2,1)} %shard_map.37) | data formatting | bytes 524288 | tf_op jit(solution)/shard_map/reshape;reshape | solution.py:109
  18.9 1.3 %fusion = bf16[512,256]{0,1:T(8,128)(2,1)S(1)} fusion(bf16[256,512]{1,0:T(8,128)(2,1)S(1)} %reshape_reshape.3, bf16[512,512]{1,0:T(8,128)(2,1)} %constant.2.clone), kind=kOutput, calls=%fused_computation.1 | convolution fusion | flops 134348800 | bytes 1048576 | tf_op jit(solution)/shard_map/xn,nq->qx/dot_general | solution.py:118
  20.3 0.1 copy.10
  20.4 0.1 broadcast_in_dim_reshape.3
  20.5 9.8 %all_to_all.15 = bf16[4,32,1,4,256]{4,3,1,2,0:T(4,128)(2,1)S(1)} all-to-all(bf16[4,32,1,4,256]{4,3,1,2,0:T(4,128)(2,1)S(1)} %bitcast.20), channel_id=1, replica_groups=mesh['tm'=4,'chan'=8] {'tm'}, dimensions={0} | all-to-all | bytes 524288 | tf_op jit(solution)/shard_map/all_to_all | solution.py:123
  30.3 0.5 copy.12
  30.8 2.0 %copy.13 = bf16[32,32,16,8]{1,3,2,0:T(8,128)(2,1)S(1)} copy(bf16[32,32,16,8]{0,3,1,2:T(8,128)(2,1)S(1)} %bitcast.18) | data formatting | bytes 524288 | tf_op jit(solution)/shard_map/transpose | solution.py:125
  32.8 1.0 %copy.15 = bf16[1,32,32,128]{3,2,1,0:T(8,128)(2,1)} copy(bf16[1,32,32,128]{2,3,1,0:T(8,128)(2,1)S(1)} %bitcast.16) | data formatting | bytes 524288 | tf_op jit(solution)/shard_map/all_gather;reshape | solution.py:127
  33.9 0.0 all-gather.2.cloned.1.call-update
  33.9 1.0 %copy.16.own_ref = bf16[32,32,128]{2,1,0:T(8,128)(2,1)} copy(bf16[32,32,128]{1,2,0:T(8,128)(2,1)S(1)} %bitcast.17) | data formatting | bytes 524288 | tf_op jit(solution)/shard_map/reshape | solution.py:126
  34.9 27.9 %all-gather.2.cloned.1.call-done.every_ref = bf16[8,32,32,128]{3,2,1,0:T(8,128)(2,1)} async-done(((bf16[1,32,32,128]{3,2,1,0:T(8,128)(2,1)}), bf16[8,32,32,128]{3,2,1,0:T(8,128)(2,1)}) %all-gather.2.cloned.1.call-update) | async-done | bytes 2097168 | tf_op jit(solution)/shard_map/all_gather | solution.py:127
  62.9 3.8 %shard_map.38 = f32[2,64,32,256]{3,2,1,0:T(8,128)} custom-call(bf16[32,32,128]{2,1,0:T(8,128)(2,1)} %copy.16.own_ref, bf16[8,32,32,128]{3,2,1,0:T(8,128)(2,1)} %all-gather.2.cloned.1.call-done.every_ref), custom_call_target="tpu_custom_call" | custom-call | flops 268435456 | bytes 6553600 | tf_op jit(solution)/shard_map/pallas_call | solution.py:161
Async XLA Ops:
  6.5 56.3 %all-gather.2.cloned.1.call-start = ((), (), s32[]{:S(2)}) async-start(), calls=%async_computation.1 | async-start | bytes 2359296 | tf_op jit(solution)/shard_map/all_gather | solution.py:127
  7.3 6.5 %collective-permute-start = (bf16[32,256]{1,0:T(8,128)(2,1)S(1)}, bf16[32,256]{1,0:T(8,128)(2,1)S(1)}, u32[]{:S(2)}, u32[]{:S(2)}) collective-permute-start(bf16[32,256]{1,0:T(8,128)(2,1)S(1)} %slice.3), channel_id=1, source_target_pairs={{0,8},{8,16},{16,24},{1,9},{9,17},{17,25},{2,10},{10,18},{18,26},{... | collective-permute-start | bytes 49160 | tf_op jit(solution)/shard_map/ppermute | solution.py:19
  13.8 0.6 copy-start
Sparse Core Ops, SparseCore 0:
  34.0 28.8 all-gather.1

commit v18 on v16

--- a/solution.py
+++ b/solution.py
@@ -156,7 +156,7 @@
 
 def cross_spectra(own, every, parts):
     sources, pairs, channels, lanes = every.shape
-    step = 16 if pairs % 16 == 0 else pairs
+    step = pairs
     wide = sources * channels
     return pl.pallas_call(
         functools.partial(cross_kernel, parts),

time: 74 us -> 74.6 us (level)
  no operation moved by 1% of the time
where the time goes in v18:
time: 74.6 us; the launch traced here: 74.3 us
  waiting for transfers between devices  28 us (38%)
  between operations  13.4 us (18%)
  blocking collectives  9.76 us (13%)
  local copies, waits for them, and re-layouts  8.87 us (12%)
  Pallas kernels  8.06 us (11%)
  starting transfers between devices  4.83 us (6%)
  matrix products  1.34 us (2%)
    all_gather x1, waiting for transfers between devices, shards(): every = lax.all_gather(shard, 'chan', axis=0)  27.9 us
    all_to_all x1, blocking collectives, shards(): lax.all_to_all(spectra, 'tm', split_axis=0, concat_axis=1, tiled=False)  9.76 us
    ppermute x1, starting transfers between devices, shifted(): return lax.ppermute(value, axis, pairs)  4.83 us
    pallas_call x1, Pallas kernels, cross_spectra(): pl.pallas_call(functools.partial(cross_kernel, parts), out_shape=jax.Shap...  4.44 us
    pallas_call x1, Pallas kernels, whiten(): pl.pallas_call(fir_kernel, out_shape=jax.ShapeDtypeStruct(late.shape, jnp...  3.62 us
    unnamed x3, local copies, waits for them, and re-layouts  2.3 us
    transpose x1, local copies, waits for them, and re-layouts, shards(): shard = own.reshape(pairs, 4 * parts, channels, segs).transpose(0, 2, 1, 3)  2.05 us
  transfers between devices with their start and end apart: 2, of which 1 were waited for; matrix products, arithmetic and copies ran while one was open for 4% of the time, Pallas kernels for 0%

profile of v18, /device:TPU:0, one launch (start us, length us, event | category | flops | bytes accessed | tf_op | source)
XLA Modules:
  0.0 74.3 jit_solution(7198593171655551524)
XLA Ops:
  6.5 0.0 all-gather.2.cloned.1.call-start
  6.5 0.7 slice.3
  7.3 4.8 %collective-permute-start = (bf16[32,256]{1,0:T(8,128)(2,1)S(1)}, bf16[32,256]{1,0:T(8,128)(2,1)S(1)}, u32[]{:S(2)}, u32[]{:S(2)}) collective-permute-start(bf16[32,256]{1,0:T(8,128)(2,1)S(1)} %slice.3), channel_id=1, source_target_pairs={{0,8},{8,16},{16,24},{1,9},{9,17},{17,25},{2,10},{10,18},{18,26},{... | collective-permute-start | bytes 49160 | tf_op jit(solution)/shard_map/ppermute | solution.py:19
  12.1 1.7 %copy.17 = bf16[4,8,16,256]{3,2,1,0:T(8,128)(2,1)} copy(bf16[4,8,16,256]{3,1,2,0:T(8,128)(2,1)} %bitcast.21) | data formatting | bytes 524288
  13.8 0.0 collective-permute-done.previous_ref
  13.8 0.0 copy-start
  13.8 0.6 copy-done
  14.4 3.6 %shard_map.37 = bf16[32,16,256]{2,1,0:T(8,128)(2,1)} custom-call(bf16[32,256]{1,0:T(8,128)(2,1)} %taps_ref.1, bf16[32,256]{1,0:T(8,128)(2,1)} %copy-done, bf16[32,16,256]{2,1,0:T(8,128)(2,1)} %bitcast.19), custom_call_target="tpu_custom_call" | custom-call | flops 134217728 | bytes 557056 | tf_op jit(solution)/shard_map/pallas_call | solution.py:89
  18.0 1.0 %reshape_reshape.3 = bf16[256,512]{1,0:T(8,128)(2,1)S(1)} reshape(bf16[32,16,256]{2,1,0:T(8,128)(2,1)} %shard_map.37) | data formatting | bytes 524288 | tf_op jit(solution)/shard_map/reshape;reshape | solution.py:109
  19.1 1.3 %fusion = bf16[512,256]{0,1:T(8,128)(2,1)S(1)} fusion(bf16[256,512]{1,0:T(8,128)(2,1)S(1)} %reshape_reshape.3, bf16[512,512]{1,0:T(8,128)(2,1)} %constant.2.clone), kind=kOutput, calls=%fused_computation.1 | convolution fusion | flops 134348800 | bytes 1048576 | tf_op jit(solution)/shard_map/xn,nq->qx/dot_general | solution.py:118
  20.4 0.1 copy.10
  20.5 0.1 broadcast_in_dim_reshape.3
  20.6 9.8 %all_to_all.15 = bf16[4,32,1,4,256]{4,3,1,2,0:T(4,128)(2,1)S(1)} all-to-all(bf16[4,32,1,4,256]{4,3,1,2,0:T(4,128)(2,1)S(1)} %bitcast.20), channel_id=1, replica_groups=mesh['tm'=4,'chan'=8] {'tm'}, dimensions={0} | all-to-all | bytes 524288 | tf_op jit(solution)/shard_map/all_to_all | solution.py:123
  30.4 0.5 copy.12
  30.9 2.0 %copy.13 = bf16[32,32,16,8]{1,3,2,0:T(8,128)(2,1)S(1)} copy(bf16[32,32,16,8]{0,3,1,2:T(8,128)(2,1)S(1)} %bitcast.18) | data formatting | bytes 524288 | tf_op jit(solution)/shard_map/transpose | solution.py:125
  33.0 1.0 %copy.15 = bf16[1,32,32,128]{3,2,1,0:T(8,128)(2,1)} copy(bf16[1,32,32,128]{2,3,1,0:T(8,128)(2,1)S(1)} %bitcast.16) | data formatting | bytes 524288 | tf_op jit(solution)/shard_map/all_gather;reshape | solution.py:127
  34.0 0.0 all-gather.2.cloned.1.call-update
  34.0 1.0 %copy.16.own_ref = bf16[32,32,128]{2,1,0:T(8,128)(2,1)} copy(bf16[32,32,128]{1,2,0:T(8,128)(2,1)S(1)} %bitcast.17) | data formatting | bytes 524288 | tf_op jit(solution)/shard_map/reshape | solution.py:126
  35.0 27.9 %all-gather.2.cloned.1.call-done.every_ref = bf16[8,32,32,128]{3,2,1,0:T(8,128)(2,1)} async-done(((bf16[1,32,32,128]{3,2,1,0:T(8,128)(2,1)}), bf16[8,32,32,128]{3,2,1,0:T(8,128)(2,1)}) %all-gather.2.cloned.1.call-update) | async-done | bytes 2097168 | tf_op jit(solution)/shard_map/all_gather | solution.py:127
  63.0 4.4 %shard_map.38 = f32[2,64,32,256]{3,2,1,0:T(8,128)} custom-call(bf16[32,32,128]{2,1,0:T(8,128)(2,1)} %copy.16.own_ref, bf16[8,32,32,128]{3,2,1,0:T(8,128)(2,1)} %all-gather.2.cloned.1.call-done.every_ref), custom_call_target="tpu_custom_call" | custom-call | flops 268435456 | bytes 6553600 | tf_op jit(solution)/shard_map/pallas_call | solution.py:161
Async XLA Ops:
  6.5 56.4 %all-gather.2.cloned.1.call-start = ((), (), s32[]{:S(2)}) async-start(), calls=%async_computation.1 | async-start | bytes 2359296 | tf_op jit(solution)/shard_map/all_gather | solution.py:127
  7.3 6.5 %collective-permute-start = (bf16[32,256]{1,0:T(8,128)(2,1)S(1)}, bf16[32,256]{1,0:T(8,128)(2,1)S(1)}, u32[]{:S(2)}, u32[]{:S(2)}) collective-permute-start(bf16[32,256]{1,0:T(8,128)(2,1)S(1)} %slice.3), channel_id=1, source_target_pairs={{0,8},{8,16},{16,24},{1,9},{9,17},{17,25},{2,10},{10,18},{18,26},{... | collective-permute-start | bytes 49160 | tf_op jit(solution)/shard_map/ppermute | solution.py:19
  13.8 0.6 copy-start
Sparse Core Ops, SparseCore 0:
  34.1 28.8 all-gather.1

commit v19 on v17

--- a/solution.py
+++ b/solution.py
@@ -50,13 +50,12 @@
     return jnp.stack([real_part, imag_part], axis=0)
 
 
-def fir_kernel(taps_ref, previous_ref, late_ref, out_ref):
+def fir_kernel(taps_ref, previous_ref, seg_ref, out_ref):
     half = taps_ref.shape[1] // 2
     row = lax.broadcasted_iota(jnp.int32, (half, half), 0)
     col = lax.broadcasted_iota(jnp.int32, (half, half), 1)
     upper = col >= row
     zero = jnp.zeros((half, half), jnp.float32)
-    first = lax.broadcasted_iota(jnp.int32, late_ref.shape[1:], 0) == 0
     for ci in range(taps_ref.shape[0]):
         taps = taps_ref[pl.ds(ci, 1), :].astype(jnp.float32)
         low = jnp.broadcast_to(taps[:, :half], (half, half))
@@ -73,40 +72,47 @@
         bottom = jnp.concatenate(
             [jnp.concatenate([d2, d1], axis=1), jnp.concatenate([none, d2], axis=1)], axis=0
         )
-        late = late_ref[ci]
-        shifted_down = pltpu.roll(jnp.dot(late, top, preferred_element_type=jnp.float32), 1, 0)
+        pair = seg_ref[ci].astype(jnp.float32)
+        half_seg = pair.shape[1] // 2
+        stacked = jnp.concatenate([pair[:, :half_seg], pair[:, half_seg:]], axis=0)
+        stacked = stacked.astype(jnp.bfloat16)
+        count = pair.shape[0]
+        upper_part = jnp.dot(stacked, top, preferred_element_type=jnp.float32)
+        lower_part = jnp.dot(stacked, bottom, preferred_element_type=jnp.float32)
         head = jnp.dot(previous_ref[pl.ds(ci, 1), :], top, preferred_element_type=jnp.float32)
-        acc = jnp.where(first, jnp.broadcast_to(head, shifted_down.shape), shifted_down)
-        acc = acc + jnp.dot(late, bottom, preferred_element_type=jnp.float32)
-        out_ref[ci] = acc.astype(out_ref.dtype)
+        carried = pltpu.roll(upper_part[count:], 1, 0)
+        first = lax.broadcasted_iota(jnp.int32, carried.shape, 0) == 0
+        even = jnp.where(first, jnp.broadcast_to(head, carried.shape), carried) + lower_part[:count]
+        odd = upper_part[:count] + lower_part[count:]
+        out_ref[pl.ds(ci * count, count), :] = jnp.concatenate([even, odd], axis=1).astype(
+            out_ref.dtype
+        )
 
 
-def whiten(fir_taps, previous, late):
-    channels, nblocks, tap_count = late.shape
+def whiten(fir_taps, previous, segs):
+    channels, count, width = segs.shape
+    tap_count = fir_taps.shape[1]
     group = channels
-    block = pl.BlockSpec((group, nblocks, tap_count), lambda g: (g, 0, 0))
     rows = pl.BlockSpec((group, tap_count), lambda g: (g, 0))
     return pl.pallas_call(
         fir_kernel,
-        out_shape=jax.ShapeDtypeStruct(late.shape, jnp.bfloat16),
+        out_shape=jax.ShapeDtypeStruct((channels * count, width), jnp.bfloat16),
         grid=(channels // group,),
-        in_specs=[rows, rows, block],
-        out_specs=block,
+        in_specs=[rows, rows, pl.BlockSpec((group, count, width), lambda g: (g, 0, 0))],
+        out_specs=pl.BlockSpec((group * count, width), lambda g: (g, 0)),
         cost_estimate=pl.CostEstimate(
-            flops=4 * channels * nblocks * tap_count * tap_count,
-            bytes_accessed=2 * late.size * 2 + 2 * fir_taps.size * 2,
+            flops=2 * channels * count * width * tap_count * 2,
+            bytes_accessed=2 * segs.size * 2 + 2 * fir_taps.size * 2,
             transcendentals=0,
         ),
-    )(fir_taps, previous, late)
+    )(fir_taps, previous, segs)
 
 
 def shards(strain, fir_taps):
     tap_count = fir_taps.shape[1]
     channels = strain.shape[0]
     previous = shifted(strain[:, -tap_count:], "tm", 1)
-    late = strain.reshape(channels, -1, tap_count)
-    whitened = whiten(fir_taps, previous, late).reshape(channels, -1)
-    segments = whitened.reshape(channels * (whitened.shape[1] // SEG), SEG)
+    segments = whiten(fir_taps, previous, strain.reshape(channels, -1, SEG))
     parts = lax.axis_size("tm")
     table = make_table()
     bins = table.shape[2]

time: 73.9 us -> 72.9 us (0.986)
  local copies, waits for them, and re-layouts: 8.87 us -> 7.86 us
    another operation x1 -> x0, local copies, waits for them, and re-layouts: 1.04 us -> none  [shards(): segments = whitened.reshape(channels * (whitened.shape[1] // SEG), SEG)]
where the time goes in v19:
time: 72.9 us; the launch traced here: 72.5 us
  waiting for transfers between devices  28 us (38%)
  between operations  13.4 us (18%)
  blocking collectives  9.73 us (13%)
  local copies, waits for them, and re-layouts  7.86 us (11%)
  Pallas kernels  7.3 us (10%)
  starting transfers between devices  4.83 us (7%)
  matrix products  1.42 us (2%)
    all_gather x1, waiting for transfers between devices, shards(): every = lax.all_gather(shard, 'chan', axis=0)  27.9 us
    all_to_all x1, blocking collectives, shards(): lax.all_to_all(spectra, 'tm', split_axis=0, concat_axis=1, tiled=False)  9.73 us
    ppermute x1, starting transfers between devices, shifted(): return lax.ppermute(value, axis, pairs)  4.83 us
    pallas_call x1, Pallas kernels, cross_spectra(): pl.pallas_call(functools.partial(cross_kernel, parts), out_shape=jax.Shap...  3.79 us
    pallas_call x1, Pallas kernels, whiten(): pl.pallas_call(fir_kernel, out_shape=jax.ShapeDtypeStruct((channels * cou...  3.5 us
    unnamed x3, local copies, waits for them, and re-layouts  2.33 us
    transpose x1, local copies, waits for them, and re-layouts, shards(): shard = own.reshape(pairs, 4 * parts, channels, segs).transpose(0, 2, 1, 3)  2.05 us
  transfers between devices with their start and end apart: 2, of which 1 were waited for; matrix products, arithmetic and copies ran while one was open for 4% of the time, Pallas kernels for 0%

profile of v19, /device:TPU:0, one launch (start us, length us, event | category | flops | bytes accessed | tf_op | source)
XLA Modules:
  0.0 72.5 jit_solution(10262077378334851917)
XLA Ops:
  6.5 0.0 all-gather.2.cloned.1.call-start
  6.5 0.7 slice.3
  7.3 4.8 %collective-permute-start = (bf16[32,256]{1,0:T(8,128)(2,1)S(1)}, bf16[32,256]{1,0:T(8,128)(2,1)S(1)}, u32[]{:S(2)}, u32[]{:S(2)}) collective-permute-start(bf16[32,256]{1,0:T(8,128)(2,1)S(1)} %slice.3), channel_id=1, source_target_pairs={{0,8},{8,16},{16,24},{1,9},{9,17},{17,25},{2,10},{10,18},{18,26},{... | collective-permute-start | bytes 49160 | tf_op jit(solution)/shard_map/ppermute | solution.py:19
  12.1 1.7 %copy.17 = bf16[4,8,8,512]{3,2,1,0:T(8,128)(2,1)} copy(bf16[4,8,8,512]{3,1,2,0:T(8,128)(2,1)} %bitcast.21) | data formatting | bytes 524288
  13.8 0.0 collective-permute-done.previous_ref
  13.8 0.0 copy-start
  13.8 0.6 copy-done
  14.4 3.5 %shard_map.37 = bf16[256,512]{1,0:T(8,128)(2,1)} custom-call(bf16[32,256]{1,0:T(8,128)(2,1)} %taps_ref.1, bf16[32,256]{1,0:T(8,128)(2,1)} %copy-done, bf16[32,8,512]{2,1,0:T(8,128)(2,1)} %bitcast.19), custom_call_target="tpu_custom_call" | custom-call | flops 134217728 | bytes 557056 | tf_op jit(solution)/shard_map/pallas_call | solution.py:97
  17.9 1.4 %fusion = bf16[512,256]{0,1:T(8,128)(2,1)S(1)} fusion(bf16[256,512]{1,0:T(8,128)(2,1)} %shard_map.37, bf16[512,512]{1,0:T(8,128)(2,1)} %constant.2.clone), kind=kOutput, calls=%fused_computation.1 | convolution fusion | flops 134348800 | bytes 1048576 | tf_op jit(solution)/shard_map/xn,nq->qx/dot_general | solution.py:124
  19.4 0.1 copy.10
  19.5 0.1 broadcast_in_dim_reshape.3
  19.6 9.7 %all_to_all.15 = bf16[4,32,1,4,256]{4,3,1,2,0:T(4,128)(2,1)S(1)} all-to-all(bf16[4,32,1,4,256]{4,3,1,2,0:T(4,128)(2,1)S(1)} %bitcast.20), channel_id=1, replica_groups=mesh['tm'=4,'chan'=8] {'tm'}, dimensions={0} | all-to-all | bytes 524288 | tf_op jit(solution)/shard_map/all_to_all | solution.py:129
  29.3 0.5 copy.12
  29.8 2.0 %copy.13 = bf16[32,32,16,8]{1,3,2,0:T(8,128)(2,1)S(1)} copy(bf16[32,32,16,8]{0,3,1,2:T(8,128)(2,1)S(1)} %bitcast.18) | data formatting | bytes 524288 | tf_op jit(solution)/shard_map/transpose | solution.py:131
  31.9 1.0 %copy.15 = bf16[1,32,32,128]{3,2,1,0:T(8,128)(2,1)} copy(bf16[1,32,32,128]{2,3,1,0:T(8,128)(2,1)S(1)} %bitcast.16) | data formatting | bytes 524288 | tf_op jit(solution)/shard_map/all_gather;reshape | solution.py:133
  32.9 0.0 all-gather.2.cloned.1.call-update
  32.9 1.0 %copy.16.own_ref = bf16[32,32,128]{2,1,0:T(8,128)(2,1)} copy(bf16[32,32,128]{1,2,0:T(8,128)(2,1)S(1)} %bitcast.17) | data formatting | bytes 524288 | tf_op jit(solution)/shard_map/reshape | solution.py:132
  34.0 27.9 %all-gather.2.cloned.1.call-done.every_ref = bf16[8,32,32,128]{3,2,1,0:T(8,128)(2,1)} async-done(((bf16[1,32,32,128]{3,2,1,0:T(8,128)(2,1)}), bf16[8,32,32,128]{3,2,1,0:T(8,128)(2,1)}) %all-gather.2.cloned.1.call-update) | async-done | bytes 2097168 | tf_op jit(solution)/shard_map/all_gather | solution.py:133
  61.9 3.8 %shard_map.38 = f32[2,64,32,256]{3,2,1,0:T(8,128)} custom-call(bf16[32,32,128]{2,1,0:T(8,128)(2,1)} %copy.16.own_ref, bf16[8,32,32,128]{3,2,1,0:T(8,128)(2,1)} %all-gather.2.cloned.1.call-done.every_ref), custom_call_target="tpu_custom_call" | custom-call | flops 268435456 | bytes 6553600 | tf_op jit(solution)/shard_map/pallas_call | solution.py:167
Async XLA Ops:
  6.5 55.4 %all-gather.2.cloned.1.call-start = ((), (), s32[]{:S(2)}) async-start(), calls=%async_computation.1 | async-start | bytes 2359296 | tf_op jit(solution)/shard_map/all_gather | solution.py:133
  7.3 6.6 %collective-permute-start = (bf16[32,256]{1,0:T(8,128)(2,1)S(1)}, bf16[32,256]{1,0:T(8,128)(2,1)S(1)}, u32[]{:S(2)}, u32[]{:S(2)}) collective-permute-start(bf16[32,256]{1,0:T(8,128)(2,1)S(1)} %slice.3), channel_id=1, source_target_pairs={{0,8},{8,16},{16,24},{1,9},{9,17},{17,25},{2,10},{10,18},{18,26},{... | collective-permute-start | bytes 49160 | tf_op jit(solution)/shard_map/ppermute | solution.py:19
  13.8 0.6 copy-start
Sparse Core Ops, SparseCore 0:
  33.0 28.8 all-gather.1

commit v20 on v19

--- a/solution.py
+++ b/solution.py
@@ -50,7 +50,7 @@
     return jnp.stack([real_part, imag_part], axis=0)
 
 
-def fir_kernel(taps_ref, previous_ref, seg_ref, out_ref):
+def fir_kernel(taps_ref, previous_ref, seg_ref, table_ref, out_ref, whitened_ref):
     half = taps_ref.shape[1] // 2
     row = lax.broadcasted_iota(jnp.int32, (half, half), 0)
     col = lax.broadcasted_iota(jnp.int32, (half, half), 1)
@@ -84,35 +84,42 @@
         first = lax.broadcasted_iota(jnp.int32, carried.shape, 0) == 0
         even = jnp.where(first, jnp.broadcast_to(head, carried.shape), carried) + lower_part[:count]
         odd = upper_part[:count] + lower_part[count:]
-        out_ref[pl.ds(ci * count, count), :] = jnp.concatenate([even, odd], axis=1).astype(
-            out_ref.dtype
+        whitened_ref[pl.ds(ci * count, count), :] = jnp.concatenate([even, odd], axis=1).astype(
+            whitened_ref.dtype
         )
+    out_ref[...] = lax.dot_general(
+        table_ref[...], whitened_ref[...], (((1,), (1,)), ((), ())), preferred_element_type=jnp.float32
+    ).astype(out_ref.dtype)
 
 
-def whiten(fir_taps, previous, segs):
+def whiten(fir_taps, previous, segs, table):
     channels, count, width = segs.shape
     tap_count = fir_taps.shape[1]
-    group = channels
-    rows = pl.BlockSpec((group, tap_count), lambda g: (g, 0))
+    rows = pl.BlockSpec((channels, tap_count), lambda g: (0, 0))
     return pl.pallas_call(
         fir_kernel,
-        out_shape=jax.ShapeDtypeStruct((channels * count, width), jnp.bfloat16),
-        grid=(channels // group,),
-        in_specs=[rows, rows, pl.BlockSpec((group, count, width), lambda g: (g, 0, 0))],
-        out_specs=pl.BlockSpec((group * count, width), lambda g: (g, 0)),
+        out_shape=jax.ShapeDtypeStruct((table.shape[0], channels * count), jnp.bfloat16),
+        grid=(1,),
+        in_specs=[
+            rows,
+            rows,
+            pl.BlockSpec((channels, count, width), lambda g: (0, 0, 0)),
+            pl.BlockSpec(table.shape, lambda g: (0, 0)),
+        ],
+        out_specs=pl.BlockSpec((table.shape[0], channels * count), lambda g: (0, 0)),
+        scratch_shapes=[pltpu.VMEM((channels * count, width), jnp.bfloat16)],
         cost_estimate=pl.CostEstimate(
-            flops=2 * channels * count * width * tap_count * 2,
-            bytes_accessed=2 * segs.size * 2 + 2 * fir_taps.size * 2,
+            flops=2 * channels * count * width * (2 * tap_count + table.shape[0]),
+            bytes_accessed=segs.size * 2 + 2 * fir_taps.size * 2 + table.size * 2 + segs.size * 2,
             transcendentals=0,
         ),
-    )(fir_taps, previous, segs)
+    )(fir_taps, previous, segs, table)
 
 
 def shards(strain, fir_taps):
     tap_count = fir_taps.shape[1]
     channels = strain.shape[0]
     previous = shifted(strain[:, -tap_count:], "tm", 1)
-    segments = whiten(fir_taps, previous, strain.reshape(channels, -1, SEG))
     parts = lax.axis_size("tm")
     table = make_table()
     bins = table.shape[2]
@@ -120,10 +127,9 @@
         table.reshape(SEG, 2, parts, bins // parts // 2, 2)
         .transpose(0, 2, 3, 4, 1)
         .reshape(SEG, 2 * bins)
+        .T
     )
-    spectra = jnp.einsum(
-        "xn,nq->qx", segments, table, preferred_element_type=jnp.float32
-    ).astype(jnp.bfloat16)
+    spectra = whiten(fir_taps, previous, strain.reshape(channels, -1, SEG), table)
     pairs = bins // parts // 2
     spectra = spectra.reshape(parts, pairs, 4, spectra.shape[1])
     own = lax.all_to_all(spectra, "tm", split_axis=0, concat_axis=1, tiled=False)

time: 72.9 us -> 72.7 us (level)
  matrix products: 1.42 us -> 0 us
  local copies, waits for them, and re-layouts: 7.86 us -> 8.68 us
    dot_general x1 -> x0, matrix products: 1.42 us -> none  [shards(): jnp.einsum('xn,nq->qx', segments, table, preferred_element_type=jnp.float32)]
    another operation x1 -> x2, local copies, waits for them, and re-layouts: 0.07 us -> 1.05 us  [shards(): lax.all_to_all(spectra, 'tm', split_axis=0, concat_axis=1, tiled=False)]
where the time goes in v20:
time: 72.7 us; the launch traced here: 72.4 us
  waiting for transfers between devices  28 us (39%)
  between operations  13.4 us (18%)
  blocking collectives  9.73 us (13%)
  local copies, waits for them, and re-layouts  8.68 us (12%)
  Pallas kernels  7.74 us (11%)
  starting transfers between devices  4.83 us (7%)
    all_gather x1, waiting for transfers between devices, shards(): every = lax.all_gather(shard, 'chan', axis=0)  27.9 us
    all_to_all x1, blocking collectives, shards(): lax.all_to_all(spectra, 'tm', split_axis=0, concat_axis=1, tiled=False)  9.73 us
    ppermute x1, starting transfers between devices, shifted(): return lax.ppermute(value, axis, pairs)  4.83 us
    pallas_call x1, Pallas kernels, whiten(): pl.pallas_call(fir_kernel, out_shape=jax.ShapeDtypeStruct((table.shape[0]...  3.95 us
    pallas_call x1, Pallas kernels, cross_spectra(): pl.pallas_call(functools.partial(cross_kernel, parts), out_shape=jax.Shap...  3.79 us
    unnamed x3, local copies, waits for them, and re-layouts  2.33 us
    transpose x1, local copies, waits for them, and re-layouts, shards(): shard = own.reshape(pairs, 4 * parts, channels, segs).transpose(0, 2, 1, 3)  2.05 us
  transfers between devices with their start and end apart: 2, of which 1 were waited for; matrix products, arithmetic and copies ran while one was open for 4% of the time, Pallas kernels for 0%

profile of v20, /device:TPU:0, one launch (start us, length us, event | category | flops | bytes accessed | tf_op | source)
XLA Modules:
  0.0 72.4 jit_solution(10561438490404695001)
XLA Ops:
  6.5 0.0 all-gather.2.cloned.1.call-start
  6.5 0.7 slice.3
  7.3 4.8 %collective-permute-start = (bf16[32,256]{1,0:T(8,128)(2,1)S(1)}, bf16[32,256]{1,0:T(8,128)(2,1)S(1)}, u32[]{:S(2)}, u32[]{:S(2)}) collective-permute-start(bf16[32,256]{1,0:T(8,128)(2,1)S(1)} %slice.3), channel_id=1, source_target_pairs={{0,8},{8,16},{16,24},{1,9},{9,17},{17,25},{2,10},{10,18},{18,26},{... | collective-permute-start | bytes 49160 | tf_op jit(solution)/shard_map/ppermute | solution.py:19
  12.1 1.7 %copy.15 = bf16[4,8,8,512]{3,2,1,0:T(8,128)(2,1)} copy(bf16[4,8,8,512]{3,1,2,0:T(8,128)(2,1)} %bitcast.15) | data formatting | bytes 524288
  13.8 0.0 collective-permute-done.previous_ref
  13.8 0.0 copy-start
  13.8 0.6 copy-done
  14.4 4.0 %shard_map.37 = bf16[512,256]{1,0:T(8,128)(2,1)} custom-call(bf16[32,256]{1,0:T(8,128)(2,1)} %taps_ref.1, bf16[32,256]{1,0:T(8,128)(2,1)} %copy-done, bf16[32,8,512]{2,1,0:T(8,128)(2,1)} %bitcast.14, bf16[512,512]{1,0:T(8,128)(2,1)} %constant.2.clone.table_ref), custom_call_target="tpu_custom_call" | custom-call | flops 268435456 | bytes 1081344 | tf_op jit(solution)/shard_map/pallas_call | solution.py:99
  18.4 1.0 %broadcast_in_dim_reshape.3 = bf16[4,32,1,4,256]{4,3,1,0,2:T(4,128)(2,1)S(1)} reshape(bf16[512,256]{1,0:T(8,128)(2,1)} %shard_map.37) | data formatting | bytes 524288 | tf_op jit(solution)/shard_map/broadcast_in_dim;reshape | solution.py:135
  19.4 9.7 %all_to_all.15 = bf16[4,32,1,4,256]{4,1,3,2,0:T(8,128)(2,1)S(1)} all-to-all(bf16[4,32,1,4,256]{4,1,3,2,0:T(8,128)(2,1)S(1)} %copy.9), channel_id=1, replica_groups=mesh['tm'=4,'chan'=8] {'tm'}, dimensions={0} | all-to-all | bytes 524288 | tf_op jit(solution)/shard_map/all_to_all | solution.py:135
  29.2 0.5 copy.10
  29.7 2.0 %copy.11 = bf16[32,32,16,8]{1,3,2,0:T(8,128)(2,1)S(1)} copy(bf16[32,32,16,8]{0,3,1,2:T(8,128)(2,1)S(1)} %bitcast.13) | data formatting | bytes 524288 | tf_op jit(solution)/shard_map/transpose | solution.py:137
  31.7 1.0 %copy.13 = bf16[1,32,32,128]{3,2,1,0:T(8,128)(2,1)} copy(bf16[1,32,32,128]{2,3,1,0:T(8,128)(2,1)S(1)} %bitcast.11) | data formatting | bytes 524288 | tf_op jit(solution)/shard_map/all_gather;reshape | solution.py:139
  32.7 0.0 all-gather.2.cloned.1.call-update
  32.8 1.0 %copy.14.own_ref = bf16[32,32,128]{2,1,0:T(8,128)(2,1)} copy(bf16[32,32,128]{1,2,0:T(8,128)(2,1)S(1)} %bitcast.12) | data formatting | bytes 524288 | tf_op jit(solution)/shard_map/reshape | solution.py:138
  33.8 27.9 %all-gather.2.cloned.1.call-done.every_ref = bf16[8,32,32,128]{3,2,1,0:T(8,128)(2,1)} async-done(((bf16[1,32,32,128]{3,2,1,0:T(8,128)(2,1)}), bf16[8,32,32,128]{3,2,1,0:T(8,128)(2,1)}) %all-gather.2.cloned.1.call-update) | async-done | bytes 2097168 | tf_op jit(solution)/shard_map/all_gather | solution.py:139
  61.7 3.8 %shard_map.38 = f32[2,64,32,256]{3,2,1,0:T(8,128)} custom-call(bf16[32,32,128]{2,1,0:T(8,128)(2,1)} %copy.14.own_ref, bf16[8,32,32,128]{3,2,1,0:T(8,128)(2,1)} %all-gather.2.cloned.1.call-done.every_ref), custom_call_target="tpu_custom_call" | custom-call | flops 268435456 | bytes 6553600 | tf_op jit(solution)/shard_map/pallas_call | solution.py:173
  (1 shorter events, 0.0 us)
Async XLA Ops:
  6.5 55.2 %all-gather.2.cloned.1.call-start = ((), (), s32[]{:S(2)}) async-start(), calls=%async_computation.1 | async-start | bytes 2359296 | tf_op jit(solution)/shard_map/all_gather | solution.py:139
  7.3 6.6 %collective-permute-start = (bf16[32,256]{1,0:T(8,128)(2,1)S(1)}, bf16[32,256]{1,0:T(8,128)(2,1)S(1)}, u32[]{:S(2)}, u32[]{:S(2)}) collective-permute-start(bf16[32,256]{1,0:T(8,128)(2,1)S(1)} %slice.3), channel_id=1, source_target_pairs={{0,8},{8,16},{16,24},{1,9},{9,17},{17,25},{2,10},{10,18},{18,26},{... | collective-permute-start | bytes 49160 | tf_op jit(solution)/shard_map/ppermute | solution.py:19
  13.8 0.6 copy-start
Sparse Core Ops, SparseCore 0:
  32.9 28.8 all-gather.1

commit v21 on v19

--- a/solution.py
+++ b/solution.py
@@ -72,7 +72,11 @@
         bottom = jnp.concatenate(
             [jnp.concatenate([d2, d1], axis=1), jnp.concatenate([none, d2], axis=1)], axis=0
         )
-        pair = seg_ref[ci].astype(jnp.float32)
+        samples = seg_ref[pl.ds(ci, 1), :].astype(jnp.float32)
+        width = out_ref.shape[1]
+        pair = jnp.concatenate(
+            [samples[:, s * width:(s + 1) * width] for s in range(samples.shape[1] // width)], axis=0
+        )
         half_seg = pair.shape[1] // 2
         stacked = jnp.concatenate([pair[:, :half_seg], pair[:, half_seg:]], axis=0)
         stacked = stacked.astype(jnp.bfloat16)
@@ -89,30 +93,30 @@
         )
 
 
-def whiten(fir_taps, previous, segs):
-    channels, count, width = segs.shape
+def whiten(fir_taps, previous, strain):
+    channels, times = strain.shape
     tap_count = fir_taps.shape[1]
-    group = channels
-    rows = pl.BlockSpec((group, tap_count), lambda g: (g, 0))
+    count = times // SEG
+    rows = pl.BlockSpec((channels, tap_count), lambda g: (0, 0))
     return pl.pallas_call(
         fir_kernel,
-        out_shape=jax.ShapeDtypeStruct((channels * count, width), jnp.bfloat16),
-        grid=(channels // group,),
-        in_specs=[rows, rows, pl.BlockSpec((group, count, width), lambda g: (g, 0, 0))],
-        out_specs=pl.BlockSpec((group * count, width), lambda g: (g, 0)),
+        out_shape=jax.ShapeDtypeStruct((channels * count, SEG), jnp.bfloat16),
+        grid=(1,),
+        in_specs=[rows, rows, pl.BlockSpec((channels, times), lambda g: (0, 0))],
+        out_specs=pl.BlockSpec((channels * count, SEG), lambda g: (0, 0)),
         cost_estimate=pl.CostEstimate(
-            flops=2 * channels * count * width * tap_count * 2,
-            bytes_accessed=2 * segs.size * 2 + 2 * fir_taps.size * 2,
+            flops=2 * channels * times * tap_count * 2,
+            bytes_accessed=2 * strain.size * 2 + 2 * fir_taps.size * 2,
             transcendentals=0,
         ),
-    )(fir_taps, previous, segs)
+    )(fir_taps, previous, strain)
 
 
 def shards(strain, fir_taps):
     tap_count = fir_taps.shape[1]
     channels = strain.shape[0]
     previous = shifted(strain[:, -tap_count:], "tm", 1)
-    segments = whiten(fir_taps, previous, strain.reshape(channels, -1, SEG))
+    segments = whiten(fir_taps, previous, strain)
     parts = lax.axis_size("tm")
     table = make_table()
     bins = table.shape[2]

time: 72.9 us -> 72.9 us (level)
  local copies, waits for them, and re-layouts: 7.86 us -> 6.13 us
  waiting for transfers between devices: 28 us -> 29.4 us
    unnamed x3 -> x2, local copies, waits for them, and re-layouts: 2.33 us -> 0.6 us
    ppermute x1, waiting for transfers between devices: 0.01 us -> 1.43 us  [shifted(): return lax.ppermute(value, axis, pairs)]
  transfers between devices with their start and end apart: 2 -> 2, of which waited for: 1 -> 2; matrix products, arithmetic and copies ran while one was open for 4% -> 1% of each run, Pallas kernels for 0% -> 0%
where the time goes in v21:
time: 72.9 us; the launch traced here: 72.6 us
  waiting for transfers between devices  29.4 us (40%)
  between operations  13.4 us (18%)
  blocking collectives  10 us (14%)
  Pallas kernels  7.39 us (10%)
  local copies, waits for them, and re-layouts  6.13 us (8%)
  starting transfers between devices  4.83 us (7%)
  matrix products  1.42 us (2%)
    all_gather x1, waiting for transfers between devices, shards(): every = lax.all_gather(shard, 'chan', axis=0)  27.9 us
    all_to_all x1, blocking collectives, shards(): lax.all_to_all(spectra, 'tm', split_axis=0, concat_axis=1, tiled=False)  10 us
    ppermute x1, starting transfers between devices, shifted(): return lax.ppermute(value, axis, pairs)  4.83 us
    pallas_call x1, Pallas kernels, cross_spectra(): pl.pallas_call(functools.partial(cross_kernel, parts), out_shape=jax.Shap...  3.79 us
    pallas_call x1, Pallas kernels, whiten(): pl.pallas_call(fir_kernel, out_shape=jax.ShapeDtypeStruct((channels * cou...  3.6 us
    transpose x1, local copies, waits for them, and re-layouts, shards(): shard = own.reshape(pairs, 4 * parts, channels, segs).transpose(0, 2, 1, 3)  2.05 us
  transfers between devices with their start and end apart: 2, of which 2 were waited for; matrix products, arithmetic and copies ran while one was open for 1% of the time, Pallas kernels for 0%

profile of v21, /device:TPU:0, one launch (start us, length us, event | category | flops | bytes accessed | tf_op | source)
XLA Modules:
  0.0 72.6 jit_solution(1743722755224372015)
XLA Ops:
  6.5 0.0 all-gather.2.cloned.1.call-start
  6.5 0.7 slice.3
  7.3 4.8 %collective-permute-start = (bf16[32,256]{1,0:T(8,128)(2,1)S(1)}, bf16[32,256]{1,0:T(8,128)(2,1)S(1)}, u32[]{:S(2)}, u32[]{:S(2)}) collective-permute-start(bf16[32,256]{1,0:T(8,128)(2,1)S(1)} %slice.3), channel_id=1, source_target_pairs={{0,8},{8,16},{16,24},{1,9},{9,17},{17,25},{2,10},{10,18},{18,26},{... | collective-permute-start | bytes 49160 | tf_op jit(solution)/shard_map/ppermute | solution.py:19
  12.1 1.4 %collective-permute-done.previous_ref = bf16[32,256]{1,0:T(8,128)(2,1)S(1)} collective-permute-done((bf16[32,256]{1,0:T(8,128)(2,1)S(1)}, bf16[32,256]{1,0:T(8,128)(2,1)S(1)}, u32[]{:S(2)}, u32[]{:S(2)}) %collective-permute-start) | collective-permute-done | bytes 16416 | tf_op jit(solution)/shard_map/ppermute | solution.py:19
  13.5 0.0 copy-start
  13.5 0.6 copy-done
  14.1 3.6 %shard_map.37 = bf16[256,512]{1,0:T(8,128)(2,1)} custom-call(bf16[32,256]{1,0:T(8,128)(2,1)} %taps_ref.1, bf16[32,256]{1,0:T(8,128)(2,1)} %copy-done, bf16[32,4096]{1,0:T(8,128)(2,1)} %seg_ref.1), custom_call_target="tpu_custom_call" | custom-call | flops 134217728 | bytes 557056 | tf_op jit(solution)/shard_map/pallas_call | solution.py:101
  17.7 1.4 %fusion = bf16[512,256]{0,1:T(8,128)(2,1)S(1)} fusion(bf16[256,512]{1,0:T(8,128)(2,1)} %shard_map.37, bf16[512,512]{1,0:T(8,128)(2,1)} %constant.2.clone), kind=kOutput, calls=%fused_computation.1 | convolution fusion | flops 134348800 | bytes 1048576 | tf_op jit(solution)/shard_map/xn,nq->qx/dot_general | solution.py:128
  19.1 0.1 copy.10
  19.3 0.1 broadcast_in_dim_reshape.3
  19.4 10.0 %all_to_all.15 = bf16[4,32,1,4,256]{4,3,1,2,0:T(4,128)(2,1)S(1)} all-to-all(bf16[4,32,1,4,256]{4,3,1,2,0:T(4,128)(2,1)S(1)} %bitcast.17), channel_id=1, replica_groups=mesh['tm'=4,'chan'=8] {'tm'}, dimensions={0} | all-to-all | bytes 524288 | tf_op jit(solution)/shard_map/all_to_all | solution.py:133
  29.4 0.5 copy.12
  29.9 2.0 %copy.13 = bf16[32,32,16,8]{1,3,2,0:T(8,128)(2,1)S(1)} copy(bf16[32,32,16,8]{0,3,1,2:T(8,128)(2,1)S(1)} %bitcast.16) | data formatting | bytes 524288 | tf_op jit(solution)/shard_map/transpose | solution.py:135
  32.0 1.0 %copy.15 = bf16[1,32,32,128]{3,2,1,0:T(8,128)(2,1)} copy(bf16[1,32,32,128]{2,3,1,0:T(8,128)(2,1)S(1)} %bitcast.14) | data formatting | bytes 524288 | tf_op jit(solution)/shard_map/all_gather;reshape | solution.py:137
  33.0 0.0 all-gather.2.cloned.1.call-update
  33.0 1.0 %copy.16.own_ref = bf16[32,32,128]{2,1,0:T(8,128)(2,1)} copy(bf16[32,32,128]{1,2,0:T(8,128)(2,1)S(1)} %bitcast.15) | data formatting | bytes 524288 | tf_op jit(solution)/shard_map/reshape | solution.py:136
  34.1 27.9 %all-gather.2.cloned.1.call-done.every_ref = bf16[8,32,32,128]{3,2,1,0:T(8,128)(2,1)} async-done(((bf16[1,32,32,128]{3,2,1,0:T(8,128)(2,1)}), bf16[8,32,32,128]{3,2,1,0:T(8,128)(2,1)}) %all-gather.2.cloned.1.call-update) | async-done | bytes 2097168 | tf_op jit(solution)/shard_map/all_gather | solution.py:137
  62.0 3.8 %shard_map.38 = f32[2,64,32,256]{3,2,1,0:T(8,128)} custom-call(bf16[32,32,128]{2,1,0:T(8,128)(2,1)} %copy.16.own_ref, bf16[8,32,32,128]{3,2,1,0:T(8,128)(2,1)} %all-gather.2.cloned.1.call-done.every_ref), custom_call_target="tpu_custom_call" | custom-call | flops 268435456 | bytes 6553600 | tf_op jit(solution)/shard_map/pallas_call | solution.py:171
Async XLA Ops:
  6.5 55.5 %all-gather.2.cloned.1.call-start = ((), (), s32[]{:S(2)}) async-start(), calls=%async_computation.1 | async-start | bytes 2359296 | tf_op jit(solution)/shard_map/all_gather | solution.py:137
  7.3 6.3 %collective-permute-start = (bf16[32,256]{1,0:T(8,128)(2,1)S(1)}, bf16[32,256]{1,0:T(8,128)(2,1)S(1)}, u32[]{:S(2)}, u32[]{:S(2)}) collective-permute-start(bf16[32,256]{1,0:T(8,128)(2,1)S(1)} %slice.3), channel_id=1, source_target_pairs={{0,8},{8,16},{16,24},{1,9},{9,17},{17,25},{2,10},{10,18},{18,26},{... | collective-permute-start | bytes 49160 | tf_op jit(solution)/shard_map/ppermute | solution.py:19
  13.5 0.6 copy-start
Sparse Core Ops, SparseCore 0:
  33.1 28.8 all-gather.1
